TPU v7x, 512 devices: a whole 4x4x16 slice. The times are simulated.
512 devices in a mesh: gx: 32 (over z_hi, x, core), gy: 16 (over y, z_lo).
Axes of the slice: x: 4, y: 4, z: 16 (z_hi: 4, z_lo: 4; z = z_hi * 4 + z_lo), core: 2. Of those that a mesh axis runs over, the one named last changes fastest.
Arguments:
- orbitals: float32 [32, 64, 128, 512], P(None, 'gx', 'gy'), may hold values from -60 to 60
- potential: float32 [64, 128, 512], P('gx', 'gy'), may hold values from 0.2 to 2
- sign_bits: int32 [64, 128, 512], P('gx', 'gy'), may hold values from 0 to 1
- sampled_rows: int32 [32, 16, 8192], P('gx', 'gy'), may hold values from 0 to 8191, each once within a row
Outputs:
- rotated: float32 [32, 64, 128, 512], P(None, 'gx', 'gy')
- sketches: float32 [2, 32, 4096], P(None, None, ('gx', 'gy'))
- projected: float32 [32, 32], replicated
Inputs may be any that keep to these rules, and one draw needn't show every extreme that they name: Each block's row of sampled_rows holds every one of its 8192 cell numbers once.
All inputs are finite; a program needn't handle non-finite values.
Results may differ from a plain program's by a relative error of at most 0.00026.
Values sent between devices are 32-bit elements; how exact they have to be, the bound alone decides.
No kernel may reach another device: no remote copies, remote signals or barrier semaphores. Data moves between devices by JAX's collectives and lax.ppermute only.
A program may use at most 64 MiB of HBM per device.

v0:
```python
import jax
import jax.numpy as jnp
from jax import lax
from jax.sharding import PartitionSpec as P

M = 4096


HIGHEST = lax.Precision.HIGHEST
filter_center = 6.25
filter_half = 4.25


def padded_2(array, sides, width):
    for axis, dim in sides:
        size, length = (lax.axis_size(axis), array.shape[dim])
        up = [(i, (i + 1) % size) for i in range(size - 1)]
        down = [(j, i) for i, j in up]
        last = lax.slice_in_dim(array, length - width, length, axis=dim)
        initial = lax.slice_in_dim(array, 0, width, axis=dim)
        before = lax.ppermute(last, axis, up)
        after = lax.ppermute(initial, axis, down)
        array = jnp.concatenate([before, array, after], axis=dim)
    return array


def hadamard_table(order):
    index = jnp.arange(order, dtype=jnp.int32)
    parity = jnp.zeros((order, order), jnp.int32)
    for bit in range(order.bit_length() - 1):
        weight = 2**bit
        parity = parity + index[:, None] // weight % 2 * (index[None, :] // weight % 2)
    return (1 - 2 * (parity % 2)).astype(jnp.float32)


def second_diff(padded, axis, count):
    parts = [lax.slice_in_dim(padded, k, k + count, axis=axis) for k in range(5)]
    return (16.0 * (parts[1] + parts[3]) - (parts[0] + parts[4]) - 30.0 * parts[2]) / 12.0


def apply_ham(field, potential):
    padded = padded_2(field, (("gx", 1), ("gy", 2)), 2)
    x_padded = padded[:, :, 2:-2, :]
    y_padded = padded[:, 2:-2, :, :]
    z_padded = jnp.pad(field, ((0, 0), (0, 0), (0, 0), (2, 2)))
    total = second_diff(x_padded, 1, field.shape[1])
    total = total + second_diff(y_padded, 2, field.shape[2])
    total = total + second_diff(z_padded, 3, field.shape[3])
    return -0.5 * total + potential[None] * field


def shards(orbitals, potential, sign_bits, sampled_rows):
    first = (apply_ham(orbitals, potential) - filter_center * orbitals) / filter_half
    second = 2.0 * (apply_ham(first, potential) - filter_center * first) / filter_half - orbitals
    filtered = 2.0 * (apply_ham(second, potential) - filter_center * second) / filter_half - first
    applied = apply_ham(filtered, potential)
    count = orbitals.shape[0]
    cells = orbitals.shape[1] * orbitals.shape[2] * orbitals.shape[3]
    stacked = jnp.concatenate([filtered, applied], axis=0)
    sign_block = (2 * sign_bits - 1).astype(jnp.float32)
    flat = (stacked * sign_block[None]).reshape(2 * count, -1, 128)
    mixed = jnp.einsum("nac,cd->nad", flat, hadamard_table(128), precision=HIGHEST)
    mixed = jnp.einsum("ba,nac->nbc", hadamard_table(cells // 128), mixed, precision=HIGHEST)
    mixed = mixed.reshape(2 * count, cells)
    picked = jnp.take(mixed, sampled_rows[0, 0, :M], axis=1)
    devices = lax.axis_size("gx") * lax.axis_size("gy")
    term = (picked / jnp.sqrt(jnp.float32(M * devices))).reshape(2, count, M)
    width = M // devices
    total = lax.psum(term, ("gx", "gy"))
    position = lax.axis_index("gx") * lax.axis_size("gy") + lax.axis_index("gy")
    share = lax.dynamic_slice_in_dim(total, position * width, width, 2)
    gram = jnp.dot(total[0], total[0].T, precision=HIGHEST) / cells
    cross = jnp.dot(total[0], total[1].T, precision=HIGHEST) / cells
    lower = jnp.linalg.cholesky(gram)
    inverse = lax.linalg.triangular_solve(
        lower, jnp.eye(count, dtype=jnp.float32), left_side=True, lower=True
    )
    rotated = jnp.dot(inverse, filtered.reshape(count, -1), precision=HIGHEST).reshape(
        filtered.shape
    )
    inner = jnp.dot(jnp.dot(inverse, cross, precision=HIGHEST), inverse.T, precision=HIGHEST)
    projected = 0.5 * (inner + inner.T)
    return (rotated, share, projected)


def solution(mesh):
    in_specs = (
        P(None, "gx", "gy", None),
        P("gx", "gy", None),
        P("gx", "gy", None),
        P("gx", "gy", None),
    )
    out_specs = (P(None, "gx", "gy", None), P(None, None, ("gx", "gy")), P())
    return jax.shard_map(shards, mesh=mesh, in_specs=in_specs, out_specs=out_specs, check_vma=False)
```

profile of v0, /device:TPU:6, one launch (start us, length us, event | category | flops | bytes accessed | tf_op | source)
XLA Modules:
  0.0 936.9 jit_solution(11268816920238034277)
XLA Ops:
  11.1 3.6 collective-permute-start.1
  14.7 10.5 %collective-permute-done = f32[32,2,8,512]{3,0,2,1:T(8,128)S(1)} collective-permute-done((f32[32,2,8,512]{3,0,2,1:T(8,128)S(1)}, f32[32,2,8,512]{3,0,2,1:T(8,128)S(1)}, u32[]{:S(2)}, u32[]{:S(2)}) %collective-permute-start) | collective-permute-done | bytes 1048608 | tf_op jit(solution)/shard_map/ppermute | solution.py:21
  27.3 3.9 collective-permute-start.2
  32.4 8.1 collective-permute-done.2
  40.6 11.8 %collective-permute-done.3 = f32[32,6,2,512]{3,0,2,1:T(8,128)S(1)} collective-permute-done((f32[32,6,2,512]{3,0,2,1:T(8,128)S(1)}, f32[32,6,2,512]{3,0,2,1:T(8,128)S(1)}, u32[]{:S(2)}, u32[]{:S(2)}) %collective-permute-start.3) | collective-permute-done | bytes 786464 | tf_op jit(solution)/shard_map/ppermute | solution.py:22
  54.0 65.8 %collective-permute-start.4 = (f32[32,2,8,512]{3,0,2,1:T(8,128)S(1)}, f32[32,2,8,512]{3,0,2,1:T(8,128)S(1)}, u32[]{:S(2)}, u32[]{:S(2)}) collective-permute-start(f32[32,2,8,512]{3,0,2,1:T(8,128)S(1)} %get-tuple-element.15), channel_id=1, source_target_pairs={{0,16},{16,32},{32,48},{48,64},{64,80},{80,96},{96,112},{112,128},... | collective-permute-start | bytes 3145736 | tf_op jit(solution)/shard_map/ppermute | solution.py:21
  122.1 12.0 %collective-permute-done.5 = f32[32,2,8,512]{3,0,2,1:T(8,128)S(1)} collective-permute-done((f32[32,2,8,512]{3,0,2,1:T(8,128)S(1)}, f32[32,2,8,512]{3,0,2,1:T(8,128)S(1)}, u32[]{:S(2)}, u32[]{:S(2)}) %collective-permute-start.5) | collective-permute-done | bytes 1048608 | tf_op jit(solution)/shard_map/ppermute | solution.py:22
  134.2 3.7 collective-permute-start.6
  139.2 8.1 collective-permute-done.6
  147.3 12.9 %collective-permute-done.7 = f32[32,6,2,512]{3,0,2,1:T(8,128)S(1)} collective-permute-done((f32[32,6,2,512]{3,0,2,1:T(8,128)S(1)}, f32[32,6,2,512]{3,0,2,1:T(8,128)S(1)}, u32[]{:S(2)}, u32[]{:S(2)}) %collective-permute-start.7) | collective-permute-done | bytes 786464 | tf_op jit(solution)/shard_map/ppermute | solution.py:22
  162.6 57.5 %collective-permute-start.8 = (f32[32,2,8,512]{3,0,2,1:T(8,128)S(1)}, f32[32,2,8,512]{3,0,2,1:T(8,128)S(1)}, u32[]{:S(2)}, u32[]{:S(2)}) collective-permute-start(f32[32,2,8,512]{3,0,2,1:T(8,128)S(1)} %fusion.21), channel_id=1, source_target_pairs={{0,16},{16,32},{32,48},{48,64},{64,80},{80,96},{96,112},{112,128},... | collective-permute-start | bytes 3145736 | tf_op jit(solution)/shard_map/ppermute | solution.py:21
  222.3 12.0 %collective-permute-done.9 = f32[32,2,8,512]{3,0,2,1:T(8,128)S(1)} collective-permute-done((f32[32,2,8,512]{3,0,2,1:T(8,128)S(1)}, f32[32,2,8,512]{3,0,2,1:T(8,128)S(1)}, u32[]{:S(2)}, u32[]{:S(2)}) %collective-permute-start.9) | collective-permute-done | bytes 1048608 | tf_op jit(solution)/shard_map/ppermute | solution.py:22
  238.0 8.1 collective-permute-done.10
  246.1 12.9 %collective-permute-done.11 = f32[32,6,2,512]{3,0,2,1:T(8,128)S(1)} collective-permute-done((f32[32,6,2,512]{3,0,2,1:T(8,128)S(1)}, f32[32,6,2,512]{3,0,2,1:T(8,128)S(1)}, u32[]{:S(2)}, u32[]{:S(2)}) %collective-permute-start.11) | collective-permute-done | bytes 786464 | tf_op jit(solution)/shard_map/ppermute | solution.py:22
  260.7 58.9 %collective-permute-start.12 = (f32[32,2,8,512]{3,0,2,1:T(8,128)S(1)}, f32[32,2,8,512]{3,0,2,1:T(8,128)S(1)}, u32[]{:S(2)}, u32[]{:S(2)}) collective-permute-start(f32[32,2,8,512]{3,0,2,1:T(8,128)S(1)} %fusion.32), channel_id=1, source_target_pairs={{0,16},{16,32},{32,48},{48,64},{64,80},{80,96},{96,112},{112,128},... | collective-permute-start | bytes 3145736 | tf_op jit(solution)/shard_map/ppermute | solution.py:21
  321.9 12.0 %collective-permute-done.13 = f32[32,2,8,512]{3,0,2,1:T(8,128)S(1)} collective-permute-done((f32[32,2,8,512]{3,0,2,1:T(8,128)S(1)}, f32[32,2,8,512]{3,0,2,1:T(8,128)S(1)}, u32[]{:S(2)}, u32[]{:S(2)}) %collective-permute-start.13) | collective-permute-done | bytes 1048608 | tf_op jit(solution)/shard_map/ppermute | solution.py:22
  335.3 3.0 collective-permute-start.14
  340.4 6.9 collective-permute-done.14
  347.3 5.3 collective-permute-done.15
  352.6 3.4 fusion.40
  362.9 2.7 copy.57
  365.6 13.0 %gather_fusion = f32[4096,64]{1,0:T(8,128)S(1)} fusion(f32[64,8192]{0,1:T(8,128)} %bitcast.60, s32[4096]{0:T(1024)S(1)} %broadcast_clamp_fusion), kind=kCustom, calls=%fused_computation | custom fusion | bytes 2113536 | tf_op jit(solution)/shard_map/jit(_take)/gather | solution.py:65
  383.1 530.7 %all-reduce.6.cloned.1.call-done = f32[2,32,4096]{2,1,0:T(8,128)} async-done(((f32[2,32,4096]{2,1,0:T(8,128)}), f32[2,32,4096]{2,1,0:T(8,128)}) %all-reduce.6.cloned.1.call-update) | async-done | bytes 1048592 | tf_op jit(solution)/shard_map/psum | solution.py:69
  915.7 2.9 cholesky.17
  (79 shorter events, 52.7 us)
Async XLA Ops:
  7.2 18.2 %copy-start = (f32[32,2,8,512]{3,2,1,0:T(8,128)S(1)}, f32[32,2,8,512]{3,2,1,0:T(8,128)}, u32[]{:S(2)}) copy-start(f32[32,2,8,512]{3,2,1,0:T(8,128)} %param.4) | copy-start | bytes 3145732
  7.2 906.7 %all-reduce.6.cloned.1.call-start = ((), (), s32[]{:S(2)}) async-start(), calls=%async_computation | async-start | bytes 2097152 | tf_op jit(solution)/shard_map/psum | solution.py:69
  9.1 16.1 %collective-permute-start = (f32[32,2,8,512]{3,0,2,1:T(8,128)S(1)}, f32[32,2,8,512]{3,0,2,1:T(8,128)S(1)}, u32[]{:S(2)}, u32[]{:S(2)}) collective-permute-start(f32[32,2,8,512]{3,0,2,1:T(8,128)S(1)} %copy.36), channel_id=1, source_target_pairs={{0,16},{16,32},{32,48},{48,64},{64,80},{80,96},{96,112},{112,128},... | collective-permute-start | bytes 3145736 | tf_op jit(solution)/shard_map/ppermute | solution.py:21
  11.1 15.9 %collective-permute-start.1 = (f32[32,2,8,512]{3,0,2,1:T(8,128)S(1)}, f32[32,2,8,512]{3,0,2,1:T(8,128)S(1)}, u32[]{:S(2)}, u32[]{:S(2)}) collective-permute-start(f32[32,2,8,512]{3,0,2,1:T(8,128)S(1)} %copy.36), channel_id=1, source_target_pairs={{16,0},{32,16},{48,32},{64,48},{80,64},{96,80},{112,96},{128,112},... | collective-permute-start | bytes 3145736 | tf_op jit(solution)/shard_map/ppermute | solution.py:22
  27.1 25.3 %copy-start.3 = (f32[2,8,512]{2,1,0:T(8,128)S(1)}, f32[2,8,512]{2,1,0:T(8,128)}, u32[]{:S(2)}) copy-start(f32[2,8,512]{2,1,0:T(8,128)} %param.5) | copy-start | bytes 98308
  27.3 13.3 %collective-permute-start.2 = (f32[32,6,2,512]{3,0,2,1:T(8,128)S(1)}, f32[32,6,2,512]{3,0,2,1:T(8,128)S(1)}, u32[]{:S(2)}, u32[]{:S(2)}) collective-permute-start(f32[32,6,2,512]{3,0,2,1:T(8,128)S(1)} %get-tuple-element.23), channel_id=1, source_target_pairs={{0,1},{1,2},{2,3},{3,4},{4,5},{5,6},{6,7},{7,8},{8,9},{9,10},{10,1... | collective-permute-start | bytes 2359304 | tf_op jit(solution)/shard_map/ppermute | solution.py:21
  31.1 21.2 %collective-permute-start.3 = (f32[32,6,2,512]{3,0,2,1:T(8,128)S(1)}, f32[32,6,2,512]{3,0,2,1:T(8,128)S(1)}, u32[]{:S(2)}, u32[]{:S(2)}) collective-permute-start(f32[32,6,2,512]{3,0,2,1:T(8,128)S(1)} %get-tuple-element.24), channel_id=1, source_target_pairs={{1,0},{2,1},{3,2},{4,3},{5,4},{6,5},{7,6},{8,7},{9,8},{10,9},{11,1... | collective-permute-start | bytes 2359304 | tf_op jit(solution)/shard_map/ppermute | solution.py:22
  54.0 68.1 %collective-permute-start.4 = (f32[32,2,8,512]{3,0,2,1:T(8,128)S(1)}, f32[32,2,8,512]{3,0,2,1:T(8,128)S(1)}, u32[]{:S(2)}, u32[]{:S(2)}) collective-permute-start(f32[32,2,8,512]{3,0,2,1:T(8,128)S(1)} %get-tuple-element.15), channel_id=1, source_target_pairs={{0,16},{16,32},{32,48},{48,64},{64,80},{80,96},{96,112},{112,128},... | collective-permute-start | bytes 3145736 | tf_op jit(solution)/shard_map/ppermute | solution.py:21
  119.8 14.2 %collective-permute-start.5 = (f32[32,2,8,512]{3,0,2,1:T(8,128)S(1)}, f32[32,2,8,512]{3,0,2,1:T(8,128)S(1)}, u32[]{:S(2)}, u32[]{:S(2)}) collective-permute-start(f32[32,2,8,512]{3,0,2,1:T(8,128)S(1)} %get-tuple-element.15), channel_id=1, source_target_pairs={{16,0},{32,16},{48,32},{64,48},{80,64},{96,80},{112,96},{128,112},... | collective-permute-start | bytes 3145736 | tf_op jit(solution)/shard_map/ppermute | solution.py:22
  134.2 13.1 %collective-permute-start.6 = (f32[32,6,2,512]{3,0,2,1:T(8,128)S(1)}, f32[32,6,2,512]{3,0,2,1:T(8,128)S(1)}, u32[]{:S(2)}, u32[]{:S(2)}) collective-permute-start(f32[32,6,2,512]{3,0,2,1:T(8,128)S(1)} %get-tuple-element.21), channel_id=1, source_target_pairs={{0,1},{1,2},{2,3},{3,4},{4,5},{5,6},{6,7},{7,8},{8,9},{9,10},{10,1... | collective-permute-start | bytes 2359304 | tf_op jit(solution)/shard_map/ppermute | solution.py:21
  137.9 22.3 %collective-permute-start.7 = (f32[32,6,2,512]{3,0,2,1:T(8,128)S(1)}, f32[32,6,2,512]{3,0,2,1:T(8,128)S(1)}, u32[]{:S(2)}, u32[]{:S(2)}) collective-permute-start(f32[32,6,2,512]{3,0,2,1:T(8,128)S(1)} %get-tuple-element.22), channel_id=1, source_target_pairs={{1,0},{2,1},{3,2},{4,3},{5,4},{6,5},{7,6},{8,7},{9,8},{10,9},{11,1... | collective-permute-start | bytes 2359304 | tf_op jit(solution)/shard_map/ppermute | solution.py:22
  162.6 59.8 %collective-permute-start.8 = (f32[32,2,8,512]{3,0,2,1:T(8,128)S(1)}, f32[32,2,8,512]{3,0,2,1:T(8,128)S(1)}, u32[]{:S(2)}, u32[]{:S(2)}) collective-permute-start(f32[32,2,8,512]{3,0,2,1:T(8,128)S(1)} %fusion.21), channel_id=1, source_target_pairs={{0,16},{16,32},{32,48},{48,64},{64,80},{80,96},{96,112},{112,128},... | collective-permute-start | bytes 3145736 | tf_op jit(solution)/shard_map/ppermute | solution.py:21
  220.1 14.2 %collective-permute-start.9 = (f32[32,2,8,512]{3,0,2,1:T(8,128)S(1)}, f32[32,2,8,512]{3,0,2,1:T(8,128)S(1)}, u32[]{:S(2)}, u32[]{:S(2)}) collective-permute-start(f32[32,2,8,512]{3,0,2,1:T(8,128)S(1)} %fusion.21), channel_id=1, source_target_pairs={{16,0},{32,16},{48,32},{64,48},{80,64},{96,80},{112,96},{128,112},... | collective-permute-start | bytes 3145736 | tf_op jit(solution)/shard_map/ppermute | solution.py:22
  234.4 11.6 %collective-permute-start.10 = (f32[32,6,2,512]{3,0,2,1:T(8,128)S(1)}, f32[32,6,2,512]{3,0,2,1:T(8,128)S(1)}, u32[]{:S(2)}, u32[]{:S(2)}) collective-permute-start(f32[32,6,2,512]{3,0,2,1:T(8,128)S(1)} %get-tuple-element.19), channel_id=1, source_target_pairs={{0,1},{1,2},{2,3},{3,4},{4,5},{5,6},{6,7},{7,8},{8,9},{9,10},{10,1... | collective-permute-start | bytes 2359304 | tf_op jit(solution)/shard_map/ppermute | solution.py:21
  236.6 84.9 %copy-start.5 = (s32[2,8,512]{2,1,0:T(8,128)S(1)}, s32[2,8,512]{2,1,0:T(8,128)}, u32[]{:S(2)}) copy-start(s32[2,8,512]{2,1,0:T(8,128)} %param.6) | copy-start | bytes 98308
  236.6 85.0 %slice-start = ((s32[1,1,8192]{2,1,0:T(1,128)}), s32[1,1,4096]{2,1,0:T(1,128)S(1)}, s32[]{:S(2)}) async-start(s32[1,1,8192]{2,1,0:T(1,128)} %param.7), calls=%async_computation.1 | async-start | bytes 32768 | tf_op jit(solution)/shard_map/slice | solution.py:65
  236.7 22.3 %collective-permute-start.11 = (f32[32,6,2,512]{3,0,2,1:T(8,128)S(1)}, f32[32,6,2,512]{3,0,2,1:T(8,128)S(1)}, u32[]{:S(2)}, u32[]{:S(2)}) collective-permute-start(f32[32,6,2,512]{3,0,2,1:T(8,128)S(1)} %get-tuple-element.20), channel_id=1, source_target_pairs={{1,0},{2,1},{3,2},{4,3},{5,4},{6,5},{7,6},{8,7},{9,8},{10,9},{11,1... | collective-permute-start | bytes 2359304 | tf_op jit(solution)/shard_map/ppermute | solution.py:22
  260.7 61.2 %collective-permute-start.12 = (f32[32,2,8,512]{3,0,2,1:T(8,128)S(1)}, f32[32,2,8,512]{3,0,2,1:T(8,128)S(1)}, u32[]{:S(2)}, u32[]{:S(2)}) collective-permute-start(f32[32,2,8,512]{3,0,2,1:T(8,128)S(1)} %fusion.32), channel_id=1, source_target_pairs={{0,16},{16,32},{32,48},{48,64},{64,80},{80,96},{96,112},{112,128},... | collective-permute-start | bytes 3145736 | tf_op jit(solution)/shard_map/ppermute | solution.py:21
  319.6 14.2 %collective-permute-start.13 = (f32[32,2,8,512]{3,0,2,1:T(8,128)S(1)}, f32[32,2,8,512]{3,0,2,1:T(8,128)S(1)}, u32[]{:S(2)}, u32[]{:S(2)}) collective-permute-start(f32[32,2,8,512]{3,0,2,1:T(8,128)S(1)} %fusion.32), channel_id=1, source_target_pairs={{16,0},{32,16},{48,32},{64,48},{80,64},{96,80},{112,96},{128,112},... | collective-permute-start | bytes 3145736 | tf_op jit(solution)/shard_map/ppermute | solution.py:22
  321.7 18.0 %copy-start.4 = (s32[1,1,8192]{2,1,0:T(1,128)S(1)}, s32[1,1,8192]{2,1,0:T(1,128)}, u32[]{:S(2)}) copy-start(s32[1,1,8192]{2,1,0:T(1,128)} %param.7) | copy-start | bytes 98308
  321.9 13.4 %copy-start.1 = (f32[32,2,8,512]{3,0,2,1:T(8,128)}, f32[32,2,8,512]{3,0,2,1:T(8,128)S(1)}, u32[]{:S(2)}) copy-start(f32[32,2,8,512]{3,0,2,1:T(8,128)S(1)} %collective-permute-done.12) | copy-start | bytes 3145732
  333.9 1.5 copy-start.2
  335.3 12.0 %collective-permute-start.14 = (f32[32,6,2,512]{3,0,2,1:T(8,128)}, f32[32,6,2,512]{3,0,2,1:T(8,128)}, u32[]{:S(2)}, u32[]{:S(2)}) collective-permute-start(f32[32,6,2,512]{3,0,2,1:T(8,128)} %get-tuple-element.17), channel_id=1, source_target_pairs={{0,1},{1,2},{2,3},{3,4},{4,5},{5,6},{6,7},{7,8},{8,9},{9,10},{10,1... | collective-permute-start | bytes 2359304 | tf_op jit(solution)/shard_map/ppermute | solution.py:21
  338.4 14.2 %collective-permute-start.15 = (f32[32,6,2,512]{3,0,2,1:T(8,128)}, f32[32,6,2,512]{3,0,2,1:T(8,128)}, u32[]{:S(2)}, u32[]{:S(2)}) collective-permute-start(f32[32,6,2,512]{3,0,2,1:T(8,128)} %get-tuple-element.18), channel_id=1, source_target_pairs={{1,0},{2,1},{3,2},{4,3},{5,4},{6,5},{7,6},{8,7},{9,8},{10,9},{11,1... | collective-permute-start | bytes 2359304 | tf_op jit(solution)/shard_map/ppermute | solution.py:22
Sparse Core Ops, SparseCore 0:
  382.6 531.1 all-reduce.5
where the time goes:
time: 939 us; the launch traced here: 937 us
  waiting for transfers between devices  653 us (70%)
  starting transfers between devices  212 us (23%)
  local copies, waits for them, and re-layouts  27.5 us (3%)
  other arithmetic  20.5 us (2%)
  between operations  14.5 us (2%)
  matrix products  9.66 us (1%)
    psum x1, waiting for transfers between devices, shards(): total = lax.psum(term, ('gx', 'gy'))  531 us
    ppermute x8, starting transfers between devices, padded_2(): before = lax.ppermute(last, axis, up)  197 us
    ppermute x8, waiting for transfers between devices, padded_2(): after = lax.ppermute(initial, axis, down)  79.7 us
    ppermute x8, waiting for transfers between devices, padded_2(): before = lax.ppermute(last, axis, up)  42.7 us
  transfers between devices with their start and end apart: 17, of which 17 were waited for; matrix products, arithmetic and copies ran while one was open for 0% of the time, Pallas kernels for 0%

commit v1 on v0

--- a/solution.py
+++ b/solution.py
@@ -11,17 +11,48 @@
 filter_half = 4.25
 
 
-def padded_2(array, sides, width):
-    for axis, dim in sides:
-        size, length = (lax.axis_size(axis), array.shape[dim])
-        up = [(i, (i + 1) % size) for i in range(size - 1)]
-        down = [(j, i) for i, j in up]
-        last = lax.slice_in_dim(array, length - width, length, axis=dim)
-        initial = lax.slice_in_dim(array, 0, width, axis=dim)
-        before = lax.ppermute(last, axis, up)
-        after = lax.ppermute(initial, axis, down)
-        array = jnp.concatenate([before, array, after], axis=dim)
-    return array
+def halos(array, axis, dim, width):
+    size, length = (lax.axis_size(axis), array.shape[dim])
+    up = [(i, (i + 1) % size) for i in range(size - 1)]
+    down = [(j, i) for i, j in up]
+    last = lax.slice_in_dim(array, length - width, length, axis=dim)
+    initial = lax.slice_in_dim(array, 0, width, axis=dim)
+    before = lax.ppermute(last, axis, up)
+    after = lax.ppermute(initial, axis, down)
+    return before, after
+
+
+STAGES = (("gx", 0), ("gx", 1), ("gy", 0), ("gy", 2), ("gx", 2), ("gy", 1), ("gy", 3), ("gx", 3), ("gx", 4))
+
+
+def axis_bits(axis):
+    return lax.axis_size(axis).bit_length() - 1
+
+
+def butterfly_scatter(x):
+    n, cols = x.shape
+    nbx, nby = axis_bits("gx"), axis_bits("gy")
+    rest = cols >> (nbx + nby)
+    buf = x.reshape((n,) + (2,) * (nbx + nby) + (rest,))
+    dims = {("gx", b): nbx - b for b in range(nbx)}
+    dims.update({("gy", b): nbx + nby - b for b in range(nby)})
+    live = list(range(buf.ndim))
+    for axis, b in STAGES:
+        d = live.index(dims[(axis, b)])
+        mine = (lax.axis_index(axis) // (2**b)) % 2
+        keep = lax.dynamic_index_in_dim(buf, mine, d, keepdims=False)
+        send = lax.dynamic_index_in_dim(buf, 1 - mine, d, keepdims=False)
+        pairs = [(k, k ^ (2**b)) for k in range(lax.axis_size(axis))]
+        buf = keep + lax.ppermute(send, axis, pairs)
+        live.pop(d)
+    return buf.reshape(n, rest)
+
+
+def butterfly_sum(x):
+    for axis, b in STAGES:
+        pairs = [(k, k ^ (2**b)) for k in range(lax.axis_size(axis))]
+        x = x + lax.ppermute(x, axis, pairs)
+    return x
 
 
 def hadamard_table(order):
@@ -39,9 +70,10 @@
 
 
 def apply_ham(field, potential):
-    padded = padded_2(field, (("gx", 1), ("gy", 2)), 2)
-    x_padded = padded[:, :, 2:-2, :]
-    y_padded = padded[:, 2:-2, :, :]
+    x_before, x_after = halos(field, "gx", 1, 2)
+    y_before, y_after = halos(field, "gy", 2, 2)
+    x_padded = jnp.concatenate([x_before, field, x_after], axis=1)
+    y_padded = jnp.concatenate([y_before, field, y_after], axis=2)
     z_padded = jnp.pad(field, ((0, 0), (0, 0), (0, 0), (2, 2)))
     total = second_diff(x_padded, 1, field.shape[1])
     total = total + second_diff(y_padded, 2, field.shape[2])
@@ -65,12 +97,12 @@
     picked = jnp.take(mixed, sampled_rows[0, 0, :M], axis=1)
     devices = lax.axis_size("gx") * lax.axis_size("gy")
     term = (picked / jnp.sqrt(jnp.float32(M * devices))).reshape(2, count, M)
-    width = M // devices
-    total = lax.psum(term, ("gx", "gy"))
-    position = lax.axis_index("gx") * lax.axis_size("gy") + lax.axis_index("gy")
-    share = lax.dynamic_slice_in_dim(total, position * width, width, 2)
-    gram = jnp.dot(total[0], total[0].T, precision=HIGHEST) / cells
-    cross = jnp.dot(total[0], total[1].T, precision=HIGHEST) / cells
+    assert len(STAGES) == axis_bits("gx") + axis_bits("gy")
+    share = butterfly_scatter(term.reshape(2 * count, M)).reshape(2, count, -1)
+    part_gram = jnp.dot(share[0], share[0].T, precision=HIGHEST)
+    part_cross = jnp.dot(share[0], share[1].T, precision=HIGHEST)
+    parts = butterfly_sum(jnp.stack([part_gram, part_cross])) / cells
+    gram, cross = parts[0], parts[1]
     lower = jnp.linalg.cholesky(gram)
     inverse = lax.linalg.triangular_solve(
         lower, jnp.eye(count, dtype=jnp.float32), left_side=True, lower=True

time: 939 us -> 488 us (0.52)
  waiting for transfers between devices: 653 us -> 129 us
  starting transfers between devices: 212 us -> 299 us
  between operations: 14.5 us -> 1.7 us
    psum x1 -> x0, waiting for transfers between devices: 531 us -> none  [shards(): total = lax.psum(term, ('gx', 'gy'))]
    ppermute x16 -> x34, starting transfers between devices: 211 us -> 299 us  [the longest x8 163 us: halos(): before = lax.ppermute(last, axis, up)]
    ppermute x16 -> x34, waiting for transfers between devices: 122 us -> 129 us  [the longest x9 49.9 us: butterfly_scatter(): buf = keep + lax.ppermute(send, axis, pairs)]
  transfers between devices with their start and end apart: 17 -> 34, of which waited for: 17 -> 26; matrix products, arithmetic and copies ran while one was open for 0% -> 1% of each run, Pallas kernels for 0% -> 0%
where the time goes in v1:
time: 488 us; the launch traced here: 487 us
  starting transfers between devices  299 us (61%)
  waiting for transfers between devices  129 us (26%)
  local copies, waits for them, and re-layouts  30.9 us (6%)
  other arithmetic  20.3 us (4%)
  matrix products  6.65 us (1%)
    ppermute x8, starting transfers between devices, halos(): before = lax.ppermute(last, axis, up)  163 us
    ppermute x9, starting transfers between devices, butterfly_scatter(): buf = keep + lax.ppermute(send, axis, pairs)  88.1 us
    ppermute x9, waiting for transfers between devices, butterfly_scatter(): buf = keep + lax.ppermute(send, axis, pairs)  49.9 us
    ppermute x9, starting transfers between devices, butterfly_sum(): x = x + lax.ppermute(x, axis, pairs)  32.9 us
    ppermute x8, waiting for transfers between devices, halos(): after = lax.ppermute(initial, axis, down)  32.8 us
    ppermute x9, waiting for transfers between devices, butterfly_sum(): x = x + lax.ppermute(x, axis, pairs)  31.7 us
    gather x1, local copies, waits for them, and re-layouts, shards(): picked = jnp.take(mixed, sampled_rows[0, 0, :M], axis=1)  16.4 us
    ppermute x8, starting transfers between devices, halos(): after = lax.ppermute(initial, axis, down)  14.7 us
  transfers between devices with their start and end apart: 34, of which 26 were waited for; matrix products, arithmetic and copies ran while one was open for 1% of the time, Pallas kernels for 0%

profile of v1, /device:TPU:6, one launch (start us, length us, event | category | flops | bytes accessed | tf_op | source)
XLA Modules:
  0.0 487.2 jit_solution(10244362152905268598)
XLA Ops:
  13.4 5.4 %collective-permute-done.2 = f32[32,2,2,512]{3,0,2,1:T(8,128)S(1)} collective-permute-done((f32[32,2,2,512]{3,0,2,1:T(8,128)S(1)}, f32[32,2,2,512]{3,0,2,1:T(8,128)S(1)}, u32[]{:S(2)}, u32[]{:S(2)}) %collective-permute-start.2) | collective-permute-done | bytes 262176 | tf_op jit(solution)/shard_map/ppermute | solution.py:20
  19.4 4.8 collective-permute-done.3
  25.9 25.9 %collective-permute-start.4 = (f32[32,2,8,512]{3,0,2,1:T(8,128)S(1)}, f32[32,2,8,512]{3,0,2,1:T(8,128)S(1)}, u32[]{:S(2)}, u32[]{:S(2)}) collective-permute-start(f32[32,2,8,512]{3,0,2,1:T(8,128)S(1)} %get-tuple-element.21), channel_id=1, source_target_pairs={{0,16},{16,32},{32,48},{48,64},{64,80},{80,96},{96,112},{112,128},... | collective-permute-start | bytes 3145736 | tf_op jit(solution)/shard_map/ppermute | solution.py:20
  53.7 26.0 %collective-permute-start.6 = (f32[32,2,2,512]{3,0,2,1:T(8,128)S(1)}, f32[32,2,2,512]{3,0,2,1:T(8,128)S(1)}, u32[]{:S(2)}, u32[]{:S(2)}) collective-permute-start(f32[32,2,2,512]{3,0,2,1:T(8,128)S(1)} %get-tuple-element.29), channel_id=1, source_target_pairs={{0,1},{1,2},{2,3},{3,4},{4,5},{5,6},{6,7},{7,8},{8,9},{9,10},{10,1... | collective-permute-start | bytes 786440 | tf_op jit(solution)/shard_map/ppermute | solution.py:20
  90.8 44.1 %collective-permute-start.8 = (f32[32,2,8,512]{3,0,2,1:T(8,128)S(1)}, f32[32,2,8,512]{3,0,2,1:T(8,128)S(1)}, u32[]{:S(2)}, u32[]{:S(2)}) collective-permute-start(f32[32,2,8,512]{3,0,2,1:T(8,128)S(1)} %fusion.37), channel_id=1, source_target_pairs={{0,16},{16,32},{32,48},{48,64},{64,80},{80,96},{96,112},{112,128},... | collective-permute-start | bytes 3145736 | tf_op jit(solution)/shard_map/ppermute | solution.py:20
  142.7 17.9 %collective-permute-done.11 = f32[32,2,2,512]{3,0,2,1:T(8,128)S(1)} collective-permute-done((f32[32,2,2,512]{3,0,2,1:T(8,128)S(1)}, f32[32,2,2,512]{3,0,2,1:T(8,128)S(1)}, u32[]{:S(2)}, u32[]{:S(2)}) %collective-permute-start.11) | collective-permute-done | bytes 262176 | tf_op jit(solution)/shard_map/ppermute | solution.py:21
  162.4 26.8 %collective-permute-start.12 = (f32[32,2,8,512]{3,0,2,1:T(8,128)S(1)}, f32[32,2,8,512]{3,0,2,1:T(8,128)}, u32[]{:S(2)}, u32[]{:S(2)}) collective-permute-start(f32[32,2,8,512]{3,0,2,1:T(8,128)S(1)} %fusion.24), channel_id=1, source_target_pairs={{0,16},{16,32},{32,48},{48,64},{64,80},{80,96},{96,112},{112,128},... | collective-permute-start | bytes 3145736 | tf_op jit(solution)/shard_map/ppermute | solution.py:20
  192.0 32.2 %collective-permute-start.14 = (f32[32,2,2,512]{3,0,2,1:T(8,128)}, f32[32,2,2,512]{3,0,2,1:T(8,128)}, u32[]{:S(2)}, u32[]{:S(2)}) collective-permute-start(f32[32,2,2,512]{3,0,2,1:T(8,128)} %get-tuple-element.25), channel_id=1, source_target_pairs={{0,1},{1,2},{2,3},{3,4},{4,5},{5,6},{6,7},{7,8},{8,9},{9,10},{10,1... | collective-permute-start | bytes 786440 | tf_op jit(solution)/shard_map/ppermute | solution.py:20
  230.6 6.2 %collective-permute-done.15 = f32[32,2,2,512]{3,0,2,1:T(8,128)} collective-permute-done((f32[32,2,2,512]{3,0,2,1:T(8,128)}, f32[32,2,2,512]{3,0,2,1:T(8,128)}, u32[]{:S(2)}, u32[]{:S(2)}) %collective-permute-start.15) | collective-permute-done | bytes 262176 | tf_op jit(solution)/shard_map/ppermute | solution.py:21
  249.7 16.4 %gather_fusion = f32[4096,64]{1,0:T(8,128)} fusion(f32[64,8192]{0,1:T(8,128)} %bitcast.103, s32[4096]{0:T(1024)S(1)} %broadcast_clamp_fusion), kind=kCustom, calls=%fused_computation | custom fusion | bytes 2113536 | tf_op jit(solution)/shard_map/jit(_take)/gather | solution.py:97
  269.1 20.5 %collective-permute-start.16 = (f32[64,2,2,2,2,2,2,2,2,8]{0,9,8,7,6,5,4,3,2,1:T(8,128)}, f32[64,2,2,2,2,2,2,2,2,8]{0,9,8,7,6,5,4,3,2,1:T(8,128)}, u32[]{:S(2)}, u32[]{:S(2)}) collective-permute-start(f32[64,2,2,2,2,2,2,2,2,8]{0,9,8,7,6,5,4,3,2,1:T(8,128)} %dynamic-slice_bitcast_fusion), channel_id=1, source_target_pairs={{0,16},{16,0},{32,48},{48,32},{64,80},{80,64},{96,112},{112,96},{1... | collective-permute-start | bytes 1572872 | tf_op jit(solution)/shard_map/ppermute | solution.py:46
  295.7 14.1 %collective-permute-done.17 = f32[64,2,2,2,2,2,2,2,8]{0,8,6,5,4,3,2,1,7:T(8,128)S(1)} collective-permute-done((f32[64,2,2,2,2,2,2,2,8]{0,8,6,5,4,3,2,1,7:T(8,128)S(1)}, f32[64,2,2,2,2,2,2,2,8]{0,8,6,5,4,3,2,1,7:T(8,128)S(1)}, u32[]{:S(2)}, u32[]{:S(2)}) %collective-permute-start.17) | collective-permute-done | bytes 262176 | tf_op jit(solution)/shard_map/ppermute | solution.py:46
  310.0 26.1 %collective-permute-start.18 = (f32[64,2,2,2,2,2,2,8]{0,7,6,5,4,3,2,1:T(8,128)S(1)}, f32[64,2,2,2,2,2,2,8]{0,7,6,5,4,3,2,1:T(8,128)S(1)}, u32[]{:S(2)}, u32[]{:S(2)}) collective-permute-start(f32[64,2,2,2,2,2,2,8]{0,7,6,5,4,3,2,1:T(8,128)S(1)} %dynamic-slice_bitcast_fusion.1), channel_id=1, source_target_pairs={{0,1},{1,0},{2,3},{3,2},{4,5},{5,4},{6,7},{7,6},{8,9},{9,8},{10,11... | collective-permute-start | bytes 393224 | tf_op jit(solution)/shard_map/ppermute | solution.py:46
  336.1 6.0 %collective-permute-done.18 = f32[64,2,2,2,2,2,2,8]{0,7,6,5,4,3,2,1:T(8,128)S(1)} collective-permute-done((f32[64,2,2,2,2,2,2,8]{0,7,6,5,4,3,2,1:T(8,128)S(1)}, f32[64,2,2,2,2,2,2,8]{0,7,6,5,4,3,2,1:T(8,128)S(1)}, u32[]{:S(2)}, u32[]{:S(2)}) %collective-permute-start.18) | collective-permute-done | bytes 131104 | tf_op jit(solution)/shard_map/ppermute | solution.py:46
  344.1 4.9 %collective-permute-done.19 = f32[64,2,2,2,2,2,8]{0,6,5,4,3,2,1:T(8,128)S(1)} collective-permute-done((f32[64,2,2,2,2,2,8]{0,6,5,4,3,2,1:T(8,128)S(1)}, f32[64,2,2,2,2,2,8]{0,6,5,4,3,2,1:T(8,128)S(1)}, u32[]{:S(2)}, u32[]{:S(2)}) %collective-permute-start.19) | collective-permute-done | bytes 65568 | tf_op jit(solution)/shard_map/ppermute | solution.py:46
  351.0 5.7 %collective-permute-done.20 = f32[64,2,2,2,2,8]{0,5,4,3,2,1:T(8,128)S(1)} collective-permute-done((f32[64,2,2,2,2,8]{0,5,4,3,2,1:T(8,128)S(1)}, f32[64,2,2,2,2,8]{0,5,4,3,2,1:T(8,128)S(1)}, u32[]{:S(2)}, u32[]{:S(2)}) %collective-permute-start.20) | collective-permute-done | bytes 32800 | tf_op jit(solution)/shard_map/ppermute | solution.py:46
  365.5 5.2 %collective-permute-done.22 = f32[64,2,2,8]{0,3,2,1:T(8,128)S(1)} collective-permute-done((f32[64,2,2,8]{0,3,2,1:T(8,128)S(1)}, f32[64,2,2,8]{0,3,2,1:T(8,128)S(1)}, u32[]{:S(2)}, u32[]{:S(2)}) %collective-permute-start.22) | collective-permute-done | bytes 8224 | tf_op jit(solution)/shard_map/ppermute | solution.py:46
  370.6 22.9 %collective-permute-start.23 = (f32[64,2,8]{0,2,1:T(8,128)S(1)}, f32[64,2,8]{0,2,1:T(8,128)S(1)}, u32[]{:S(2)}, u32[]{:S(2)}) collective-permute-start(f32[64,2,8]{0,2,1:T(8,128)S(1)} %dynamic-slice_bitcast_fusion.6), channel_id=1, source_target_pairs={{0,128},{16,144},{32,160},{48,176},{64,192},{80,208},{96,224},{112... | collective-permute-start | bytes 12296 | tf_op jit(solution)/shard_map/ppermute | solution.py:46
  395.2 9.1 %collective-permute-start.24 = (f32[64,8]{0,1:T(8,128)S(1)}, f32[64,8]{0,1:T(8,128)S(1)}, u32[]{:S(2)}, u32[]{:S(2)}) collective-permute-start(f32[64,8]{0,1:T(8,128)S(1)} %fusion.150), channel_id=1, source_target_pairs={{0,256},{16,272},{32,288},{48,304},{64,320},{80,336},{96,352},{112... | collective-permute-start | bytes 6152 | tf_op jit(solution)/shard_map/ppermute | solution.py:46
  404.3 5.1 %collective-permute-done.24 = f32[64,8]{0,1:T(8,128)S(1)} collective-permute-done((f32[64,8]{0,1:T(8,128)S(1)}, f32[64,8]{0,1:T(8,128)S(1)}, u32[]{:S(2)}, u32[]{:S(2)}) %collective-permute-start.24) | collective-permute-done | bytes 2080 | tf_op jit(solution)/shard_map/ppermute | solution.py:46
  432.4 5.4 %collective-permute-done.29 = f32[2,32,32]{1,2,0:T(8,128)S(1)} collective-permute-done((f32[2,32,32]{1,2,0:T(8,128)S(1)}, f32[2,32,32]{1,2,0:T(8,128)S(1)}, u32[]{:S(2)}, u32[]{:S(2)}) %collective-permute-start.29) | collective-permute-done | bytes 8224 | tf_op jit(solution)/shard_map/ppermute | solution.py:54
  446.4 5.4 %collective-permute-done.31 = f32[2,32,32]{1,2,0:T(8,128)S(1)} collective-permute-done((f32[2,32,32]{1,2,0:T(8,128)S(1)}, f32[2,32,32]{1,2,0:T(8,128)S(1)}, u32[]{:S(2)}, u32[]{:S(2)}) %collective-permute-start.31) | collective-permute-done | bytes 8224 | tf_op jit(solution)/shard_map/ppermute | solution.py:54
  451.8 7.8 %collective-permute-start.32 = (f32[2,32,32]{1,2,0:T(8,128)S(1)}, f32[2,32,32]{1,2,0:T(8,128)S(1)}, u32[]{:S(2)}, u32[]{:S(2)}) collective-permute-start(f32[2,32,32]{1,2,0:T(8,128)S(1)} %add.829), channel_id=1, source_target_pairs={{0,128},{16,144},{32,160},{48,176},{64,192},{80,208},{96,224},{112... | collective-permute-start | bytes 24584 | tf_op jit(solution)/shard_map/ppermute | solution.py:54
  461.5 9.4 %collective-permute-start.33 = (f32[2,32,32]{1,2,0:T(8,128)S(1)}, f32[2,32,32]{1,2,0:T(8,128)S(1)}, u32[]{:S(2)}, u32[]{:S(2)}) collective-permute-start(f32[2,32,32]{1,2,0:T(8,128)S(1)} %add.830), channel_id=1, source_target_pairs={{0,256},{16,272},{32,288},{48,304},{64,320},{80,336},{96,352},{112... | collective-permute-start | bytes 24584 | tf_op jit(solution)/shard_map/ppermute | solution.py:54
  (137 shorter events, 132.3 us)
Async XLA Ops:
  2.5 21.8 %collective-permute-start = (f32[32,2,8,512]{3,0,2,1:T(8,128)S(1)}, f32[32,2,8,512]{3,0,2,1:T(8,128)S(1)}, u32[]{:S(2)}, u32[]{:S(2)}) collective-permute-start(f32[32,2,8,512]{3,0,2,1:T(8,128)S(1)} %copy.64), channel_id=1, source_target_pairs={{0,16},{16,32},{32,48},{48,64},{64,80},{80,96},{96,112},{112,128},... | collective-permute-start | bytes 3145736 | tf_op jit(solution)/shard_map/ppermute | solution.py:20
  4.5 19.7 %collective-permute-start.1 = (f32[32,2,8,512]{3,0,2,1:T(8,128)S(1)}, f32[32,2,8,512]{3,0,2,1:T(8,128)S(1)}, u32[]{:S(2)}, u32[]{:S(2)}) collective-permute-start(f32[32,2,8,512]{3,0,2,1:T(8,128)S(1)} %copy.64), channel_id=1, source_target_pairs={{16,0},{32,16},{48,32},{64,48},{80,64},{96,80},{112,96},{128,112},... | collective-permute-start | bytes 3145736 | tf_op jit(solution)/shard_map/ppermute | solution.py:21
  8.2 10.5 %collective-permute-start.2 = (f32[32,2,2,512]{3,0,2,1:T(8,128)S(1)}, f32[32,2,2,512]{3,0,2,1:T(8,128)S(1)}, u32[]{:S(2)}, u32[]{:S(2)}) collective-permute-start(f32[32,2,2,512]{3,0,2,1:T(8,128)S(1)} %get-tuple-element.33), channel_id=1, source_target_pairs={{0,1},{1,2},{2,3},{3,4},{4,5},{5,6},{6,7},{7,8},{8,9},{9,10},{10,1... | collective-permute-start | bytes 786440 | tf_op jit(solution)/shard_map/ppermute | solution.py:20
  12.1 12.2 %collective-permute-start.3 = (f32[32,2,2,512]{3,0,2,1:T(8,128)S(1)}, f32[32,2,2,512]{3,0,2,1:T(8,128)S(1)}, u32[]{:S(2)}, u32[]{:S(2)}) collective-permute-start(f32[32,2,2,512]{3,0,2,1:T(8,128)S(1)} %get-tuple-element.34), channel_id=1, source_target_pairs={{1,0},{2,1},{3,2},{4,3},{5,4},{6,5},{7,6},{8,7},{9,8},{10,9},{11,1... | collective-permute-start | bytes 786440 | tf_op jit(solution)/shard_map/ppermute | solution.py:21
  25.9 62.4 %collective-permute-start.4 = (f32[32,2,8,512]{3,0,2,1:T(8,128)S(1)}, f32[32,2,8,512]{3,0,2,1:T(8,128)S(1)}, u32[]{:S(2)}, u32[]{:S(2)}) collective-permute-start(f32[32,2,8,512]{3,0,2,1:T(8,128)S(1)} %get-tuple-element.21), channel_id=1, source_target_pairs={{0,16},{16,32},{32,48},{48,64},{64,80},{80,96},{96,112},{112,128},... | collective-permute-start | bytes 3145736 | tf_op jit(solution)/shard_map/ppermute | solution.py:20
  51.8 36.5 %collective-permute-start.5 = (f32[32,2,8,512]{3,0,2,1:T(8,128)S(1)}, f32[32,2,8,512]{3,0,2,1:T(8,128)S(1)}, u32[]{:S(2)}, u32[]{:S(2)}) collective-permute-start(f32[32,2,8,512]{3,0,2,1:T(8,128)S(1)} %get-tuple-element.21), channel_id=1, source_target_pairs={{16,0},{32,16},{48,32},{64,48},{80,64},{96,80},{112,96},{128,112},... | collective-permute-start | bytes 3145736 | tf_op jit(solution)/shard_map/ppermute | solution.py:21
  53.7 30.7 %collective-permute-start.6 = (f32[32,2,2,512]{3,0,2,1:T(8,128)S(1)}, f32[32,2,2,512]{3,0,2,1:T(8,128)S(1)}, u32[]{:S(2)}, u32[]{:S(2)}) collective-permute-start(f32[32,2,2,512]{3,0,2,1:T(8,128)S(1)} %get-tuple-element.29), channel_id=1, source_target_pairs={{0,1},{1,2},{2,3},{3,4},{4,5},{5,6},{6,7},{7,8},{8,9},{9,10},{10,1... | collective-permute-start | bytes 786440 | tf_op jit(solution)/shard_map/ppermute | solution.py:20
  79.8 8.5 %collective-permute-start.7 = (f32[32,2,2,512]{3,0,2,1:T(8,128)S(1)}, f32[32,2,2,512]{3,0,2,1:T(8,128)S(1)}, u32[]{:S(2)}, u32[]{:S(2)}) collective-permute-start(f32[32,2,2,512]{3,0,2,1:T(8,128)S(1)} %get-tuple-element.30), channel_id=1, source_target_pairs={{1,0},{2,1},{3,2},{4,3},{5,4},{6,5},{7,6},{8,7},{9,8},{10,9},{11,1... | collective-permute-start | bytes 786440 | tf_op jit(solution)/shard_map/ppermute | solution.py:21
  90.8 69.8 %collective-permute-start.8 = (f32[32,2,8,512]{3,0,2,1:T(8,128)S(1)}, f32[32,2,8,512]{3,0,2,1:T(8,128)S(1)}, u32[]{:S(2)}, u32[]{:S(2)}) collective-permute-start(f32[32,2,8,512]{3,0,2,1:T(8,128)S(1)} %fusion.37), channel_id=1, source_target_pairs={{0,16},{16,32},{32,48},{48,64},{64,80},{80,96},{96,112},{112,128},... | collective-permute-start | bytes 3145736 | tf_op jit(solution)/shard_map/ppermute | solution.py:20
  134.8 25.7 %collective-permute-start.9 = (f32[32,2,8,512]{3,0,2,1:T(8,128)S(1)}, f32[32,2,8,512]{3,0,2,1:T(8,128)S(1)}, u32[]{:S(2)}, u32[]{:S(2)}) collective-permute-start(f32[32,2,8,512]{3,0,2,1:T(8,128)S(1)} %fusion.37), channel_id=1, source_target_pairs={{16,0},{32,16},{48,32},{64,48},{80,64},{96,80},{112,96},{128,112},... | collective-permute-start | bytes 3145736 | tf_op jit(solution)/shard_map/ppermute | solution.py:21
  138.9 21.7 %collective-permute-start.11 = (f32[32,2,2,512]{3,0,2,1:T(8,128)S(1)}, f32[32,2,2,512]{3,0,2,1:T(8,128)S(1)}, u32[]{:S(2)}, u32[]{:S(2)}) collective-permute-start(f32[32,2,2,512]{3,0,2,1:T(8,128)S(1)} %get-tuple-element.28), channel_id=1, source_target_pairs={{1,0},{2,1},{3,2},{4,3},{5,4},{6,5},{7,6},{8,7},{9,8},{10,9},{11,1... | collective-permute-start | bytes 786440 | tf_op jit(solution)/shard_map/ppermute | solution.py:21
  162.4 74.4 %collective-permute-start.12 = (f32[32,2,8,512]{3,0,2,1:T(8,128)S(1)}, f32[32,2,8,512]{3,0,2,1:T(8,128)}, u32[]{:S(2)}, u32[]{:S(2)}) collective-permute-start(f32[32,2,8,512]{3,0,2,1:T(8,128)S(1)} %fusion.24), channel_id=1, source_target_pairs={{0,16},{16,32},{32,48},{48,64},{64,80},{80,96},{96,112},{112,128},... | collective-permute-start | bytes 3145736 | tf_op jit(solution)/shard_map/ppermute | solution.py:20
  189.2 47.6 %collective-permute-start.13 = (f32[32,2,8,512]{3,0,2,1:T(8,128)S(1)}, f32[32,2,8,512]{3,0,2,1:T(8,128)}, u32[]{:S(2)}, u32[]{:S(2)}) collective-permute-start(f32[32,2,8,512]{3,0,2,1:T(8,128)S(1)} %fusion.24), channel_id=1, source_target_pairs={{16,0},{32,16},{48,32},{64,48},{80,64},{96,80},{112,96},{128,112},... | collective-permute-start | bytes 3145736 | tf_op jit(solution)/shard_map/ppermute | solution.py:21
  192.0 38.6 %collective-permute-start.14 = (f32[32,2,2,512]{3,0,2,1:T(8,128)}, f32[32,2,2,512]{3,0,2,1:T(8,128)}, u32[]{:S(2)}, u32[]{:S(2)}) collective-permute-start(f32[32,2,2,512]{3,0,2,1:T(8,128)} %get-tuple-element.25), channel_id=1, source_target_pairs={{0,1},{1,2},{2,3},{3,4},{4,5},{5,6},{6,7},{7,8},{8,9},{9,10},{10,1... | collective-permute-start | bytes 786440 | tf_op jit(solution)/shard_map/ppermute | solution.py:20
  224.3 12.5 %collective-permute-start.15 = (f32[32,2,2,512]{3,0,2,1:T(8,128)}, f32[32,2,2,512]{3,0,2,1:T(8,128)}, u32[]{:S(2)}, u32[]{:S(2)}) collective-permute-start(f32[32,2,2,512]{3,0,2,1:T(8,128)} %get-tuple-element.26), channel_id=1, source_target_pairs={{1,0},{2,1},{3,2},{4,3},{5,4},{6,5},{7,6},{8,7},{9,8},{10,9},{11,1... | collective-permute-start | bytes 786440 | tf_op jit(solution)/shard_map/ppermute | solution.py:21
  269.1 23.1 %collective-permute-start.16 = (f32[64,2,2,2,2,2,2,2,2,8]{0,9,8,7,6,5,4,3,2,1:T(8,128)}, f32[64,2,2,2,2,2,2,2,2,8]{0,9,8,7,6,5,4,3,2,1:T(8,128)}, u32[]{:S(2)}, u32[]{:S(2)}) collective-permute-start(f32[64,2,2,2,2,2,2,2,2,8]{0,9,8,7,6,5,4,3,2,1:T(8,128)} %dynamic-slice_bitcast_fusion), channel_id=1, source_target_pairs={{0,16},{16,0},{32,48},{48,32},{64,80},{80,64},{96,112},{112,96},{1... | collective-permute-start | bytes 1572872 | tf_op jit(solution)/shard_map/ppermute | solution.py:46
  293.8 16.1 %collective-permute-start.17 = (f32[64,2,2,2,2,2,2,2,8]{0,8,6,5,4,3,2,1,7:T(8,128)S(1)}, f32[64,2,2,2,2,2,2,2,8]{0,8,6,5,4,3,2,1,7:T(8,128)S(1)}, u32[]{:S(2)}, u32[]{:S(2)}) collective-permute-start(f32[64,2,2,2,2,2,2,2,8]{0,8,6,5,4,3,2,1,7:T(8,128)S(1)} %bitcast.107), channel_id=1, source_target_pairs={{0,32},{16,48},{32,0},{48,16},{64,96},{80,112},{96,64},{112,80},{1... | collective-permute-start | bytes 786440 | tf_op jit(solution)/shard_map/ppermute | solution.py:46
  310.0 32.1 %collective-permute-start.18 = (f32[64,2,2,2,2,2,2,8]{0,7,6,5,4,3,2,1:T(8,128)S(1)}, f32[64,2,2,2,2,2,2,8]{0,7,6,5,4,3,2,1:T(8,128)S(1)}, u32[]{:S(2)}, u32[]{:S(2)}) collective-permute-start(f32[64,2,2,2,2,2,2,8]{0,7,6,5,4,3,2,1:T(8,128)S(1)} %dynamic-slice_bitcast_fusion.1), channel_id=1, source_target_pairs={{0,1},{1,0},{2,3},{3,2},{4,5},{5,4},{6,7},{7,6},{8,9},{9,8},{10,11... | collective-permute-start | bytes 393224 | tf_op jit(solution)/shard_map/ppermute | solution.py:46
  349.1 7.7 %collective-permute-start.20 = (f32[64,2,2,2,2,8]{0,5,4,3,2,1:T(8,128)S(1)}, f32[64,2,2,2,2,8]{0,5,4,3,2,1:T(8,128)S(1)}, u32[]{:S(2)}, u32[]{:S(2)}) collective-permute-start(f32[64,2,2,2,2,8]{0,5,4,3,2,1:T(8,128)S(1)} %dynamic-slice_bitcast_fusion.3), channel_id=1, source_target_pairs={{0,64},{16,80},{32,96},{48,112},{64,0},{80,16},{96,32},{112,48},{1... | collective-permute-start | bytes 98312 | tf_op jit(solution)/shard_map/ppermute | solution.py:46
  370.6 24.6 %collective-permute-start.23 = (f32[64,2,8]{0,2,1:T(8,128)S(1)}, f32[64,2,8]{0,2,1:T(8,128)S(1)}, u32[]{:S(2)}, u32[]{:S(2)}) collective-permute-start(f32[64,2,8]{0,2,1:T(8,128)S(1)} %dynamic-slice_bitcast_fusion.6), channel_id=1, source_target_pairs={{0,128},{16,144},{32,160},{48,176},{64,192},{80,208},{96,224},{112... | collective-permute-start | bytes 12296 | tf_op jit(solution)/shard_map/ppermute | solution.py:46
  395.2 14.2 %collective-permute-start.24 = (f32[64,8]{0,1:T(8,128)S(1)}, f32[64,8]{0,1:T(8,128)S(1)}, u32[]{:S(2)}, u32[]{:S(2)}) collective-permute-start(f32[64,8]{0,1:T(8,128)S(1)} %fusion.150), channel_id=1, source_target_pairs={{0,256},{16,272},{32,288},{48,304},{64,320},{80,336},{96,352},{112... | collective-permute-start | bytes 6152 | tf_op jit(solution)/shard_map/ppermute | solution.py:46
  430.5 7.3 %collective-permute-start.29 = (f32[2,32,32]{1,2,0:T(8,128)S(1)}, f32[2,32,32]{1,2,0:T(8,128)S(1)}, u32[]{:S(2)}, u32[]{:S(2)}) collective-permute-start(f32[2,32,32]{1,2,0:T(8,128)S(1)} %add.826), channel_id=1, source_target_pairs={{0,64},{16,80},{32,96},{48,112},{64,0},{80,16},{96,32},{112,48},{1... | collective-permute-start | bytes 24584 | tf_op jit(solution)/shard_map/ppermute | solution.py:54
  451.8 9.7 %collective-permute-start.32 = (f32[2,32,32]{1,2,0:T(8,128)S(1)}, f32[2,32,32]{1,2,0:T(8,128)S(1)}, u32[]{:S(2)}, u32[]{:S(2)}) collective-permute-start(f32[2,32,32]{1,2,0:T(8,128)S(1)} %add.829), channel_id=1, source_target_pairs={{0,128},{16,144},{32,160},{48,176},{64,192},{80,208},{96,224},{112... | collective-permute-start | bytes 24584 | tf_op jit(solution)/shard_map/ppermute | solution.py:54
  461.5 14.5 %collective-permute-start.33 = (f32[2,32,32]{1,2,0:T(8,128)S(1)}, f32[2,32,32]{1,2,0:T(8,128)S(1)}, u32[]{:S(2)}, u32[]{:S(2)}) collective-permute-start(f32[2,32,32]{1,2,0:T(8,128)S(1)} %add.830), channel_id=1, source_target_pairs={{0,256},{16,272},{32,288},{48,304},{64,320},{80,336},{96,352},{112... | collective-permute-start | bytes 24584 | tf_op jit(solution)/shard_map/ppermute | solution.py:54
  (14 other events, 182.3 us)

commit v2 on v1

--- a/solution.py
+++ b/solution.py
@@ -1,7 +1,7 @@
 import jax
 import jax.numpy as jnp
 from jax import lax
-from jax.sharding import PartitionSpec as P
+from jax.sharding import Mesh, PartitionSpec as P
 
 M = 4096
 
@@ -22,7 +22,8 @@
     return before, after
 
 
-STAGES = (("gx", 0), ("gx", 1), ("gy", 0), ("gy", 2), ("gx", 2), ("gy", 1), ("gy", 3), ("gx", 3), ("gx", 4))
+STAGES = (("xl", 0), ("xl", 1), ("gy", 0), ("gy", 2), ("xl", 2), ("gy", 1), ("gy", 3), ("zh", 0), ("zh", 1))
+BLOCK_AXES = ("zh", "xl", "gy")
 
 
 def axis_bits(axis):
@@ -31,11 +32,13 @@
 
 def butterfly_scatter(x):
     n, cols = x.shape
-    nbx, nby = axis_bits("gx"), axis_bits("gy")
-    rest = cols >> (nbx + nby)
-    buf = x.reshape((n,) + (2,) * (nbx + nby) + (rest,))
-    dims = {("gx", b): nbx - b for b in range(nbx)}
-    dims.update({("gy", b): nbx + nby - b for b in range(nby)})
+    bits = [axis_bits(axis) for axis in BLOCK_AXES]
+    rest = cols >> sum(bits)
+    buf = x.reshape((n,) + (2,) * sum(bits) + (rest,))
+    dims, offset = {}, 1
+    for axis, nb in zip(BLOCK_AXES, bits):
+        dims.update({(axis, b): offset + nb - 1 - b for b in range(nb)})
+        offset += nb
     live = list(range(buf.ndim))
     for axis, b in STAGES:
         d = live.index(dims[(axis, b)])
@@ -70,7 +73,7 @@
 
 
 def apply_ham(field, potential):
-    x_before, x_after = halos(field, "gx", 1, 2)
+    x_before, x_after = halos(field, "zh", 1, 2)
     y_before, y_after = halos(field, "gy", 2, 2)
     x_padded = jnp.concatenate([x_before, field, x_after], axis=1)
     y_padded = jnp.concatenate([y_before, field, y_after], axis=2)
@@ -82,10 +85,16 @@
 
 
 def shards(orbitals, potential, sign_bits, sampled_rows):
-    first = (apply_ham(orbitals, potential) - filter_center * orbitals) / filter_half
-    second = 2.0 * (apply_ham(first, potential) - filter_center * first) / filter_half - orbitals
-    filtered = 2.0 * (apply_ham(second, potential) - filter_center * second) / filter_half - first
-    applied = apply_ham(filtered, potential)
+    group_potential = lax.all_gather(potential, "xl", axis=0, tiled=True)
+    spread = lax.all_to_all(orbitals, "xl", 0, 1, tiled=True)
+    first = (apply_ham(spread, group_potential) - filter_center * spread) / filter_half
+    second = 2.0 * (apply_ham(first, group_potential) - filter_center * first) / filter_half - spread
+    spread_filtered = (
+        2.0 * (apply_ham(second, group_potential) - filter_center * second) / filter_half - first
+    )
+    spread_applied = apply_ham(spread_filtered, group_potential)
+    filtered = lax.all_to_all(spread_filtered, "xl", 1, 0, tiled=True)
+    applied = lax.all_to_all(spread_applied, "xl", 1, 0, tiled=True)
     count = orbitals.shape[0]
     cells = orbitals.shape[1] * orbitals.shape[2] * orbitals.shape[3]
     stacked = jnp.concatenate([filtered, applied], axis=0)
@@ -95,9 +104,9 @@
     mixed = jnp.einsum("ba,nac->nbc", hadamard_table(cells // 128), mixed, precision=HIGHEST)
     mixed = mixed.reshape(2 * count, cells)
     picked = jnp.take(mixed, sampled_rows[0, 0, :M], axis=1)
-    devices = lax.axis_size("gx") * lax.axis_size("gy")
+    devices = lax.axis_size("zh") * lax.axis_size("xl") * lax.axis_size("gy")
     term = (picked / jnp.sqrt(jnp.float32(M * devices))).reshape(2, count, M)
-    assert len(STAGES) == axis_bits("gx") + axis_bits("gy")
+    assert len(STAGES) == sum(axis_bits(axis) for axis in BLOCK_AXES)
     share = butterfly_scatter(term.reshape(2 * count, M)).reshape(2, count, -1)
     part_gram = jnp.dot(share[0], share[0].T, precision=HIGHEST)
     part_cross = jnp.dot(share[0], share[1].T, precision=HIGHEST)
@@ -116,11 +125,16 @@
 
 
 def solution(mesh):
+    groups = 4
+    inner = Mesh(
+        mesh.devices.reshape(groups, mesh.shape["gx"] // groups, mesh.shape["gy"]), ("zh", "xl", "gy")
+    )
+    gx = ("zh", "xl")
     in_specs = (
-        P(None, "gx", "gy", None),
-        P("gx", "gy", None),
-        P("gx", "gy", None),
-        P("gx", "gy", None),
+        P(None, gx, "gy", None),
+        P(gx, "gy", None),
+        P(gx, "gy", None),
+        P(gx, "gy", None),
     )
-    out_specs = (P(None, "gx", "gy", None), P(None, None, ("gx", "gy")), P())
-    return jax.shard_map(shards, mesh=mesh, in_specs=in_specs, out_specs=out_specs, check_vma=False)
+    out_specs = (P(None, gx, "gy", None), P(None, None, gx + ("gy",)), P())
+    return jax.shard_map(shards, mesh=inner, in_specs=in_specs, out_specs=out_specs, check_vma=False)

time: 488 us -> 380 us (0.78)
  starting transfers between devices: 299 us -> 158 us
  blocking collectives: 0 us -> 36.2 us
  waiting for transfers between devices: 129 us -> 122 us
    ppermute x8, starting transfers between devices: 163 us -> 56.3 us  [halos(): before = lax.ppermute(last, axis, up)]
    ppermute x9, starting transfers between devices: 88.1 us -> 48 us  [butterfly_scatter(): buf = keep + lax.ppermute(send, axis, pairs)]
    all_to_all x0 -> x1, blocking collectives: none -> 23.3 us  [shards(): spread = lax.all_to_all(orbitals, 'xl', 0, 1, tiled=True)]
    all_to_all x0 -> x2, waiting for transfers between devices: none -> 13 us  [the longest x1 13 us: shards(): applied = lax.all_to_all(spread_applied, 'xl', 1, 0, tiled=True)]
    all_gather x0 -> x1, blocking collectives: none -> 12.8 us  [shards(): group_potential = lax.all_gather(potential, 'xl', axis=0, tiled=True)]
    ppermute x8, waiting for transfers between devices: 14.6 us -> 4.06 us  [halos(): before = lax.ppermute(last, axis, up)]
    all_to_all x0 -> x2, starting transfers between devices: none -> 10.4 us  [the longest x1 5.58 us: shards(): filtered = lax.all_to_all(spread_filtered, 'xl', 1, 0, tiled=True)]
    ppermute x8, waiting for transfers between devices: 32.8 us -> 25.4 us  [halos(): after = lax.ppermute(initial, axis, down)]
  transfers between devices with their start and end apart: 34 -> 36, of which waited for: 26 -> 26; matrix products, arithmetic and copies ran while one was open for 1% -> 2% of each run, Pallas kernels for 0% -> 0%
where the time goes in v2:
time: 380 us; the launch traced here: 376 us
  starting transfers between devices  158 us (42%)
  waiting for transfers between devices  122 us (32%)
  blocking collectives  36.2 us (10%)
  local copies, waits for them, and re-layouts  30.8 us (8%)
  other arithmetic  20.9 us (6%)
  matrix products  6.65 us (2%)
    ppermute x8, starting transfers between devices, halos(): before = lax.ppermute(last, axis, up)  56.3 us
    ppermute x9, waiting for transfers between devices, butterfly_scatter(): buf = keep + lax.ppermute(send, axis, pairs)  48.2 us
    ppermute x9, starting transfers between devices, butterfly_scatter(): buf = keep + lax.ppermute(send, axis, pairs)  48 us
    ppermute x9, starting transfers between devices, butterfly_sum(): x = x + lax.ppermute(x, axis, pairs)  33.3 us
    ppermute x9, waiting for transfers between devices, butterfly_sum(): x = x + lax.ppermute(x, axis, pairs)  31.2 us
    ppermute x8, waiting for transfers between devices, halos(): after = lax.ppermute(initial, axis, down)  25.4 us
    all_to_all x1, blocking collectives, shards(): spread = lax.all_to_all(orbitals, 'xl', 0, 1, tiled=True)  23.3 us
    gather x1, local copies, waits for them, and re-layouts, shards(): picked = jnp.take(mixed, sampled_rows[0, 0, :M], axis=1)  16.4 us
  transfers between devices with their start and end apart: 36, of which 26 were waited for; matrix products, arithmetic and copies ran while one was open for 2% of the time, Pallas kernels for 0%

profile of v2, /device:TPU:6, one launch (start us, length us, event | category | flops | bytes accessed | tf_op | source)
XLA Modules:
  0.0 376.3 jit_solution(5287768509636988769)
XLA Ops:
  0.6 23.3 %all_to_all.48 = f32[32,2,8,512]{3,2,1,0:T(8,128)S(1)} all-to-all(f32[32,2,8,512]{3,2,1,0:T(8,128)} %param.4), channel_id=1, replica_groups=mesh['zh'=4,'xl'=8,'gy'=16] {'xl'}, dimensions={0} | all-to-all | bytes 2097152 | tf_op jit(solution)/shard_map/all_to_all | solution.py:89
  26.9 7.1 %collective-permute-start = (f32[4,2,8,512]{3,2,1,0:T(8,128)S(1)}, f32[4,2,8,512]{3,2,1,0:T(8,128)S(1)}, u32[]{:S(2)}, u32[]{:S(2)}) collective-permute-start(f32[4,2,8,512]{3,2,1,0:T(8,128)S(1)} %get-tuple-element.34), channel_id=1, source_target_pairs={{0,128},{128,256},{256,384},{1,129},{129,257},{257,385},{2,130},{1... | collective-permute-start | bytes 393224 | tf_op jit(solution)/shard_map/ppermute | solution.py:20
  35.4 12.8 %all_gather.3 = f32[16,8,512]{2,1,0:T(8,128)S(1)} all-gather(f32[2,8,512]{2,1,0:T(8,128)S(1)} %copy-done), channel_id=1, replica_groups=mesh['zh'=4,'xl'=8,'gy'=16] {'xl'}, dimensions={0}, use_global_device_ids=true | all-gather | bytes 294912 | tf_op jit(solution)/shard_map/all_gather | solution.py:88
  50.8 10.0 %collective-permute-start.6 = (f32[4,16,2,512]{3,2,1,0:T(2,128)S(1)}, f32[4,16,2,512]{3,2,1,0:T(2,128)S(1)}, u32[]{:S(2)}, u32[]{:S(2)}) collective-permute-start(f32[4,16,2,512]{3,2,1,0:T(2,128)S(1)} %get-tuple-element.30), channel_id=1, source_target_pairs={{0,1},{1,2},{2,3},{3,4},{4,5},{5,6},{6,7},{7,8},{8,9},{9,10},{10,1... | collective-permute-start | bytes 786440 | tf_op jit(solution)/shard_map/ppermute | solution.py:20
  62.1 7.7 %collective-permute-start.4 = (f32[4,2,8,512]{3,2,1,0:T(8,128)S(1)}, f32[4,2,8,512]{3,2,1,0:T(8,128)S(1)}, u32[]{:S(2)}, u32[]{:S(2)}) collective-permute-start(f32[4,2,8,512]{3,2,1,0:T(8,128)S(1)} %get-tuple-element.32), channel_id=1, source_target_pairs={{0,128},{128,256},{256,384},{1,129},{129,257},{257,385},{2,130},{1... | collective-permute-start | bytes 393224 | tf_op jit(solution)/shard_map/ppermute | solution.py:20
  72.4 8.3 %collective-permute-done.5 = f32[4,2,8,512]{3,2,1,0:T(8,128)S(1)} collective-permute-done((f32[4,2,8,512]{3,2,1,0:T(8,128)S(1)}, f32[4,2,8,512]{3,2,1,0:T(8,128)S(1)}, u32[]{:S(2)}, u32[]{:S(2)}) %collective-permute-start.5) | collective-permute-done | bytes 131104 | tf_op jit(solution)/shard_map/ppermute | solution.py:21
  83.3 12.0 %collective-permute-start.10 = (f32[4,16,2,512]{3,2,1,0:T(2,128)S(1)}, f32[4,16,2,512]{3,2,1,0:T(2,128)S(1)}, u32[]{:S(2)}, u32[]{:S(2)}) collective-permute-start(f32[4,16,2,512]{3,2,1,0:T(2,128)S(1)} %get-tuple-element.26), channel_id=1, source_target_pairs={{0,1},{1,2},{2,3},{3,4},{4,5},{5,6},{6,7},{7,8},{8,9},{9,10},{10,1... | collective-permute-start | bytes 786440 | tf_op jit(solution)/shard_map/ppermute | solution.py:20
  102.8 8.5 %collective-permute-done.9 = f32[4,2,8,512]{3,2,1,0:T(8,128)S(1)} collective-permute-done((f32[4,2,8,512]{3,2,1,0:T(8,128)S(1)}, f32[4,2,8,512]{3,2,1,0:T(8,128)S(1)}, u32[]{:S(2)}, u32[]{:S(2)}) %collective-permute-start.9) | collective-permute-done | bytes 131104 | tf_op jit(solution)/shard_map/ppermute | solution.py:21
  115.6 7.0 %collective-permute-start.14 = (f32[4,16,2,512]{3,2,1,0:T(2,128)S(1)}, f32[4,16,2,512]{3,2,1,0:T(2,128)S(1)}, u32[]{:S(2)}, u32[]{:S(2)}) collective-permute-start(f32[4,16,2,512]{3,2,1,0:T(2,128)S(1)} %get-tuple-element.22), channel_id=1, source_target_pairs={{0,1},{1,2},{2,3},{3,4},{4,5},{5,6},{6,7},{7,8},{8,9},{9,10},{10,1... | collective-permute-start | bytes 786440 | tf_op jit(solution)/shard_map/ppermute | solution.py:20
  123.9 5.6 %all-to-all-start.1 = ((f32[4,16,8,512]{3,2,0,1:T(8,128)}), f32[4,16,8,512]{3,2,0,1:T(8,128)S(1)}, u32[]{:S(2)}, u32[]{:S(2)}) async-start(f32[4,16,8,512]{3,2,0,1:T(8,128)} %copy.50), calls=%async_computation.1 | async-start | bytes 2097152 | tf_op jit(solution)/shard_map/all_to_all | solution.py:96
  129.5 7.5 %collective-permute-start.12 = (f32[4,2,8,512]{3,2,1,0:T(8,128)S(1)}, f32[4,2,8,512]{3,2,1,0:T(8,128)S(1)}, u32[]{:S(2)}, u32[]{:S(2)}) collective-permute-start(f32[4,2,8,512]{3,2,1,0:T(8,128)S(1)} %get-tuple-element.24), channel_id=1, source_target_pairs={{0,128},{128,256},{256,384},{1,129},{129,257},{257,385},{2,130},{1... | collective-permute-start | bytes 393224 | tf_op jit(solution)/shard_map/ppermute | solution.py:20
  140.0 8.0 %collective-permute-done.13 = f32[4,2,8,512]{3,2,1,0:T(8,128)S(1)} collective-permute-done((f32[4,2,8,512]{3,2,1,0:T(8,128)S(1)}, f32[4,2,8,512]{3,2,1,0:T(8,128)S(1)}, u32[]{:S(2)}, u32[]{:S(2)}) %collective-permute-start.13) | collective-permute-done | bytes 131104 | tf_op jit(solution)/shard_map/ppermute | solution.py:21
  157.2 13.0 %all-to-all-done.2 = f32[4,16,8,512]{3,2,0,1:T(8,128)} async-done(((f32[4,16,8,512]{3,2,0,1:T(8,128)}), f32[4,16,8,512]{3,2,0,1:T(8,128)}, u32[]{:S(2)}, u32[]{:S(2)}) %all-to-all-start.2) | async-done | bytes 1048608 | tf_op jit(solution)/shard_map/all_to_all | solution.py:97
  180.6 16.4 %gather_fusion = f32[4096,64]{1,0:T(8,128)} fusion(f32[64,8192]{0,1:T(8,128)} %bitcast.112, s32[4096]{0:T(1024)S(1)} %broadcast_clamp_fusion), kind=kCustom, calls=%fused_computation | custom fusion | bytes 2113536 | tf_op jit(solution)/shard_map/jit(_take)/gather | solution.py:106
  208.4 13.9 %collective-permute-done.17 = f32[64,2,2,2,2,2,2,2,8]{0,8,6,5,4,3,2,1,7:T(8,128)S(1)} collective-permute-done((f32[64,2,2,2,2,2,2,2,8]{0,8,6,5,4,3,2,1,7:T(8,128)S(1)}, f32[64,2,2,2,2,2,2,2,8]{0,8,6,5,4,3,2,1,7:T(8,128)S(1)}, u32[]{:S(2)}, u32[]{:S(2)}) %collective-permute-start.17) | collective-permute-done | bytes 262176 | tf_op jit(solution)/shard_map/ppermute | solution.py:49
  222.5 7.2 %collective-permute-start.18 = (f32[64,2,2,2,2,2,2,8]{0,7,6,5,4,3,2,1:T(8,128)S(1)}, f32[64,2,2,2,2,2,2,8]{0,7,6,5,4,3,2,1:T(8,128)S(1)}, u32[]{:S(2)}, u32[]{:S(2)}) collective-permute-start(f32[64,2,2,2,2,2,2,8]{0,7,6,5,4,3,2,1:T(8,128)S(1)} %dynamic-slice_bitcast_fusion.1), channel_id=1, source_target_pairs={{0,1},{1,0},{2,3},{3,2},{4,5},{5,4},{6,7},{7,6},{8,9},{9,8},{10,11... | collective-permute-start | bytes 393224 | tf_op jit(solution)/shard_map/ppermute | solution.py:49
  229.7 5.7 %collective-permute-done.18 = f32[64,2,2,2,2,2,2,8]{0,7,6,5,4,3,2,1:T(8,128)S(1)} collective-permute-done((f32[64,2,2,2,2,2,2,8]{0,7,6,5,4,3,2,1:T(8,128)S(1)}, f32[64,2,2,2,2,2,2,8]{0,7,6,5,4,3,2,1:T(8,128)S(1)}, u32[]{:S(2)}, u32[]{:S(2)}) %collective-permute-start.18) | collective-permute-done | bytes 131104 | tf_op jit(solution)/shard_map/ppermute | solution.py:49
  235.5 14.7 %collective-permute-start.19 = (f32[64,2,2,2,2,2,8]{0,6,5,4,3,2,1:T(8,128)S(1)}, f32[64,2,2,2,2,2,8]{0,6,5,4,3,2,1:T(8,128)S(1)}, u32[]{:S(2)}, u32[]{:S(2)}) collective-permute-start(f32[64,2,2,2,2,2,8]{0,6,5,4,3,2,1:T(8,128)S(1)} %dynamic-slice_bitcast_fusion.2), channel_id=1, source_target_pairs={{0,4},{1,5},{2,6},{3,7},{4,0},{5,1},{6,2},{7,3},{8,12},{9,13},{10,... | collective-permute-start | bytes 196616 | tf_op jit(solution)/shard_map/ppermute | solution.py:49
  260.8 4.8 %collective-permute-start.21 = (f32[64,2,2,2,8]{0,4,3,2,1:T(8,128)S(1)}, f32[64,2,2,2,8]{0,4,3,2,1:T(8,128)S(1)}, u32[]{:S(2)}, u32[]{:S(2)}) collective-permute-start(f32[64,2,2,2,8]{0,4,3,2,1:T(8,128)S(1)} %dynamic-slice_bitcast_fusion.4), channel_id=1, source_target_pairs={{0,2},{1,3},{2,0},{3,1},{4,6},{5,7},{6,4},{7,5},{8,10},{9,11},{10,... | collective-permute-start | bytes 49160 | tf_op jit(solution)/shard_map/ppermute | solution.py:49
  284.2 5.0 %collective-permute-start.24 = (f32[64,8]{0,1:T(8,128)S(1)}, f32[64,8]{0,1:T(8,128)S(1)}, u32[]{:S(2)}, u32[]{:S(2)}) collective-permute-start(f32[64,8]{0,1:T(8,128)S(1)} %fusion.166), channel_id=1, source_target_pairs={{0,256},{128,384},{256,0},{384,128},{1,257},{129,385},{257,1},{385... | collective-permute-start | bytes 6152 | tf_op jit(solution)/shard_map/ppermute | solution.py:49
  289.2 9.2 %collective-permute-done.24 = f32[64,8]{0,1:T(8,128)S(1)} collective-permute-done((f32[64,8]{0,1:T(8,128)S(1)}, f32[64,8]{0,1:T(8,128)S(1)}, u32[]{:S(2)}, u32[]{:S(2)}) %collective-permute-start.24) | collective-permute-done | bytes 2080 | tf_op jit(solution)/shard_map/ppermute | solution.py:49
  345.4 5.1 %collective-permute-done.32 = f32[2,32,32]{1,2,0:T(8,128)S(1)} collective-permute-done((f32[2,32,32]{1,2,0:T(8,128)S(1)}, f32[2,32,32]{1,2,0:T(8,128)S(1)}, u32[]{:S(2)}, u32[]{:S(2)}) %collective-permute-start.32) | collective-permute-done | bytes 8224 | tf_op jit(solution)/shard_map/ppermute | solution.py:57
  350.5 5.5 %collective-permute-start.33 = (f32[2,32,32]{1,2,0:T(8,128)S(1)}, f32[2,32,32]{1,2,0:T(8,128)S(1)}, u32[]{:S(2)}, u32[]{:S(2)}) collective-permute-start(f32[2,32,32]{1,2,0:T(8,128)S(1)} %add.830), channel_id=1, source_target_pairs={{0,256},{128,384},{256,0},{384,128},{1,257},{129,385},{257,1},{385... | collective-permute-start | bytes 24584 | tf_op jit(solution)/shard_map/ppermute | solution.py:57
  357.5 7.5 %collective-permute-done.33 = f32[2,32,32]{1,2,0:T(8,128)S(1)} collective-permute-done((f32[2,32,32]{1,2,0:T(8,128)S(1)}, f32[2,32,32]{1,2,0:T(8,128)S(1)}, u32[]{:S(2)}, u32[]{:S(2)}) %collective-permute-start.33) | collective-permute-done | bytes 8224 | tf_op jit(solution)/shard_map/ppermute | solution.py:57
  (145 shorter events, 148.7 us)
Async XLA Ops:
  24.3 23.9 %collective-permute-start.2 = (f32[4,16,2,512]{3,2,1,0:T(2,128)S(1)}, f32[4,16,2,512]{3,2,1,0:T(2,128)S(1)}, u32[]{:S(2)}, u32[]{:S(2)}) collective-permute-start(f32[4,16,2,512]{3,2,1,0:T(2,128)S(1)} %get-tuple-element.36), channel_id=1, source_target_pairs={{0,1},{1,2},{2,3},{3,4},{4,5},{5,6},{6,7},{7,8},{8,9},{9,10},{10,1... | collective-permute-start | bytes 786440 | tf_op jit(solution)/shard_map/ppermute | solution.py:20
  25.6 22.6 %collective-permute-start.3 = (f32[4,16,2,512]{3,2,1,0:T(2,128)S(1)}, f32[4,16,2,512]{3,2,1,0:T(2,128)S(1)}, u32[]{:S(2)}, u32[]{:S(2)}) collective-permute-start(f32[4,16,2,512]{3,2,1,0:T(2,128)S(1)} %get-tuple-element.37), channel_id=1, source_target_pairs={{1,0},{2,1},{3,2},{4,3},{5,4},{6,5},{7,6},{8,7},{9,8},{10,9},{11,1... | collective-permute-start | bytes 786440 | tf_op jit(solution)/shard_map/ppermute | solution.py:21
  26.9 21.3 %collective-permute-start = (f32[4,2,8,512]{3,2,1,0:T(8,128)S(1)}, f32[4,2,8,512]{3,2,1,0:T(8,128)S(1)}, u32[]{:S(2)}, u32[]{:S(2)}) collective-permute-start(f32[4,2,8,512]{3,2,1,0:T(8,128)S(1)} %get-tuple-element.34), channel_id=1, source_target_pairs={{0,128},{128,256},{256,384},{1,129},{129,257},{257,385},{2,130},{1... | collective-permute-start | bytes 393224 | tf_op jit(solution)/shard_map/ppermute | solution.py:20
  34.0 14.2 %collective-permute-start.1 = (f32[4,2,8,512]{3,2,1,0:T(8,128)S(1)}, f32[4,2,8,512]{3,2,1,0:T(8,128)S(1)}, u32[]{:S(2)}, u32[]{:S(2)}) collective-permute-start(f32[4,2,8,512]{3,2,1,0:T(8,128)S(1)} %get-tuple-element.35), channel_id=1, source_target_pairs={{128,0},{256,128},{384,256},{129,1},{257,129},{385,257},{130,2},{2... | collective-permute-start | bytes 393224 | tf_op jit(solution)/shard_map/ppermute | solution.py:21
  50.8 29.8 %collective-permute-start.6 = (f32[4,16,2,512]{3,2,1,0:T(2,128)S(1)}, f32[4,16,2,512]{3,2,1,0:T(2,128)S(1)}, u32[]{:S(2)}, u32[]{:S(2)}) collective-permute-start(f32[4,16,2,512]{3,2,1,0:T(2,128)S(1)} %get-tuple-element.30), channel_id=1, source_target_pairs={{0,1},{1,2},{2,3},{3,4},{4,5},{5,6},{6,7},{7,8},{8,9},{9,10},{10,1... | collective-permute-start | bytes 786440 | tf_op jit(solution)/shard_map/ppermute | solution.py:20
  60.8 19.8 %collective-permute-start.7 = (f32[4,16,2,512]{3,2,1,0:T(2,128)S(1)}, f32[4,16,2,512]{3,2,1,0:T(2,128)S(1)}, u32[]{:S(2)}, u32[]{:S(2)}) collective-permute-start(f32[4,16,2,512]{3,2,1,0:T(2,128)S(1)} %get-tuple-element.31), channel_id=1, source_target_pairs={{1,0},{2,1},{3,2},{4,3},{5,4},{6,5},{7,6},{8,7},{9,8},{10,9},{11,1... | collective-permute-start | bytes 786440 | tf_op jit(solution)/shard_map/ppermute | solution.py:21
  62.1 10.2 %collective-permute-start.4 = (f32[4,2,8,512]{3,2,1,0:T(8,128)S(1)}, f32[4,2,8,512]{3,2,1,0:T(8,128)S(1)}, u32[]{:S(2)}, u32[]{:S(2)}) collective-permute-start(f32[4,2,8,512]{3,2,1,0:T(8,128)S(1)} %get-tuple-element.32), channel_id=1, source_target_pairs={{0,128},{128,256},{256,384},{1,129},{129,257},{257,385},{2,130},{1... | collective-permute-start | bytes 393224 | tf_op jit(solution)/shard_map/ppermute | solution.py:20
  69.9 10.8 %collective-permute-start.5 = (f32[4,2,8,512]{3,2,1,0:T(8,128)S(1)}, f32[4,2,8,512]{3,2,1,0:T(8,128)S(1)}, u32[]{:S(2)}, u32[]{:S(2)}) collective-permute-start(f32[4,2,8,512]{3,2,1,0:T(8,128)S(1)} %get-tuple-element.33), channel_id=1, source_target_pairs={{128,0},{256,128},{384,256},{129,1},{257,129},{385,257},{130,2},{2... | collective-permute-start | bytes 393224 | tf_op jit(solution)/shard_map/ppermute | solution.py:21
  83.3 28.0 %collective-permute-start.10 = (f32[4,16,2,512]{3,2,1,0:T(2,128)S(1)}, f32[4,16,2,512]{3,2,1,0:T(2,128)S(1)}, u32[]{:S(2)}, u32[]{:S(2)}) collective-permute-start(f32[4,16,2,512]{3,2,1,0:T(2,128)S(1)} %get-tuple-element.26), channel_id=1, source_target_pairs={{0,1},{1,2},{2,3},{3,4},{4,5},{5,6},{6,7},{7,8},{8,9},{9,10},{10,1... | collective-permute-start | bytes 786440 | tf_op jit(solution)/shard_map/ppermute | solution.py:20
  95.3 16.6 %collective-permute-start.11 = (f32[4,16,2,512]{3,2,1,0:T(2,128)S(1)}, f32[4,16,2,512]{3,2,1,0:T(2,128)S(1)}, u32[]{:S(2)}, u32[]{:S(2)}) collective-permute-start(f32[4,16,2,512]{3,2,1,0:T(2,128)S(1)} %get-tuple-element.27), channel_id=1, source_target_pairs={{1,0},{2,1},{3,2},{4,3},{5,4},{6,5},{7,6},{8,7},{9,8},{10,9},{11,1... | collective-permute-start | bytes 786440 | tf_op jit(solution)/shard_map/ppermute | solution.py:21
  100.3 11.0 %collective-permute-start.9 = (f32[4,2,8,512]{3,2,1,0:T(8,128)S(1)}, f32[4,2,8,512]{3,2,1,0:T(8,128)S(1)}, u32[]{:S(2)}, u32[]{:S(2)}) collective-permute-start(f32[4,2,8,512]{3,2,1,0:T(8,128)S(1)} %get-tuple-element.29), channel_id=1, source_target_pairs={{128,0},{256,128},{384,256},{129,1},{257,129},{385,257},{130,2},{2... | collective-permute-start | bytes 393224 | tf_op jit(solution)/shard_map/ppermute | solution.py:21
  115.6 32.5 %collective-permute-start.14 = (f32[4,16,2,512]{3,2,1,0:T(2,128)S(1)}, f32[4,16,2,512]{3,2,1,0:T(2,128)S(1)}, u32[]{:S(2)}, u32[]{:S(2)}) collective-permute-start(f32[4,16,2,512]{3,2,1,0:T(2,128)S(1)} %get-tuple-element.22), channel_id=1, source_target_pairs={{0,1},{1,2},{2,3},{3,4},{4,5},{5,6},{6,7},{7,8},{8,9},{9,10},{10,1... | collective-permute-start | bytes 786440 | tf_op jit(solution)/shard_map/ppermute | solution.py:20
  122.6 25.5 %collective-permute-start.15 = (f32[4,16,2,512]{3,2,1,0:T(2,128)S(1)}, f32[4,16,2,512]{3,2,1,0:T(2,128)S(1)}, u32[]{:S(2)}, u32[]{:S(2)}) collective-permute-start(f32[4,16,2,512]{3,2,1,0:T(2,128)S(1)} %get-tuple-element.23), channel_id=1, source_target_pairs={{1,0},{2,1},{3,2},{4,3},{5,4},{6,5},{7,6},{8,7},{9,8},{10,9},{11,1... | collective-permute-start | bytes 786440 | tf_op jit(solution)/shard_map/ppermute | solution.py:21
  123.9 27.5 %all-to-all-start.1 = ((f32[4,16,8,512]{3,2,0,1:T(8,128)}), f32[4,16,8,512]{3,2,0,1:T(8,128)S(1)}, u32[]{:S(2)}, u32[]{:S(2)}) async-start(f32[4,16,8,512]{3,2,0,1:T(8,128)} %copy.50), calls=%async_computation.1 | async-start | bytes 2097152 | tf_op jit(solution)/shard_map/all_to_all | solution.py:96
  129.5 10.6 %collective-permute-start.12 = (f32[4,2,8,512]{3,2,1,0:T(8,128)S(1)}, f32[4,2,8,512]{3,2,1,0:T(8,128)S(1)}, u32[]{:S(2)}, u32[]{:S(2)}) collective-permute-start(f32[4,2,8,512]{3,2,1,0:T(8,128)S(1)} %get-tuple-element.24), channel_id=1, source_target_pairs={{0,128},{128,256},{256,384},{1,129},{129,257},{257,385},{2,130},{1... | collective-permute-start | bytes 393224 | tf_op jit(solution)/shard_map/ppermute | solution.py:20
  137.0 11.1 %collective-permute-start.13 = (f32[4,2,8,512]{3,2,1,0:T(8,128)S(1)}, f32[4,2,8,512]{3,2,1,0:T(8,128)S(1)}, u32[]{:S(2)}, u32[]{:S(2)}) collective-permute-start(f32[4,2,8,512]{3,2,1,0:T(8,128)S(1)} %get-tuple-element.25), channel_id=1, source_target_pairs={{128,0},{256,128},{384,256},{129,1},{257,129},{385,257},{130,2},{2... | collective-permute-start | bytes 393224 | tf_op jit(solution)/shard_map/ppermute | solution.py:21
  151.4 18.8 %all-to-all-start.2 = ((f32[4,16,8,512]{3,2,0,1:T(8,128)}), f32[4,16,8,512]{3,2,0,1:T(8,128)}, u32[]{:S(2)}, u32[]{:S(2)}) async-start(f32[4,16,8,512]{3,2,0,1:T(8,128)} %copy.52), calls=%async_computation.2 | async-start | bytes 2097152 | tf_op jit(solution)/shard_map/all_to_all | solution.py:97
  206.5 15.9 %collective-permute-start.17 = (f32[64,2,2,2,2,2,2,2,8]{0,8,6,5,4,3,2,1,7:T(8,128)S(1)}, f32[64,2,2,2,2,2,2,2,8]{0,8,6,5,4,3,2,1,7:T(8,128)S(1)}, u32[]{:S(2)}, u32[]{:S(2)}) collective-permute-start(f32[64,2,2,2,2,2,2,2,8]{0,8,6,5,4,3,2,1,7:T(8,128)S(1)} %bitcast.125), channel_id=1, source_target_pairs={{0,32},{16,48},{32,0},{48,16},{64,96},{80,112},{96,64},{112,80},{1... | collective-permute-start | bytes 786440 | tf_op jit(solution)/shard_map/ppermute | solution.py:49
  222.5 12.9 %collective-permute-start.18 = (f32[64,2,2,2,2,2,2,8]{0,7,6,5,4,3,2,1:T(8,128)S(1)}, f32[64,2,2,2,2,2,2,8]{0,7,6,5,4,3,2,1:T(8,128)S(1)}, u32[]{:S(2)}, u32[]{:S(2)}) collective-permute-start(f32[64,2,2,2,2,2,2,8]{0,7,6,5,4,3,2,1:T(8,128)S(1)} %dynamic-slice_bitcast_fusion.1), channel_id=1, source_target_pairs={{0,1},{1,0},{2,3},{3,2},{4,5},{5,4},{6,7},{7,6},{8,9},{9,8},{10,11... | collective-permute-start | bytes 393224 | tf_op jit(solution)/shard_map/ppermute | solution.py:49
  235.5 17.6 %collective-permute-start.19 = (f32[64,2,2,2,2,2,8]{0,6,5,4,3,2,1:T(8,128)S(1)}, f32[64,2,2,2,2,2,8]{0,6,5,4,3,2,1:T(8,128)S(1)}, u32[]{:S(2)}, u32[]{:S(2)}) collective-permute-start(f32[64,2,2,2,2,2,8]{0,6,5,4,3,2,1:T(8,128)S(1)} %dynamic-slice_bitcast_fusion.2), channel_id=1, source_target_pairs={{0,4},{1,5},{2,6},{3,7},{4,0},{5,1},{6,2},{7,3},{8,12},{9,13},{10,... | collective-permute-start | bytes 196616 | tf_op jit(solution)/shard_map/ppermute | solution.py:49
  274.8 9.4 %collective-permute-start.23 = (f32[64,2,8]{0,2,1:T(8,128)S(1)}, f32[64,2,8]{0,2,1:T(8,128)S(1)}, u32[]{:S(2)}, u32[]{:S(2)}) collective-permute-start(f32[64,2,8]{0,2,1:T(8,128)S(1)} %dynamic-slice_bitcast_fusion.6), channel_id=1, source_target_pairs={{0,128},{128,0},{256,384},{384,256},{1,129},{129,1},{257,385},{385... | collective-permute-start | bytes 12296 | tf_op jit(solution)/shard_map/ppermute | solution.py:49
  284.2 14.2 %collective-permute-start.24 = (f32[64,8]{0,1:T(8,128)S(1)}, f32[64,8]{0,1:T(8,128)S(1)}, u32[]{:S(2)}, u32[]{:S(2)}) collective-permute-start(f32[64,8]{0,1:T(8,128)S(1)} %fusion.166), channel_id=1, source_target_pairs={{0,256},{128,384},{256,0},{384,128},{1,257},{129,385},{257,1},{385... | collective-permute-start | bytes 6152 | tf_op jit(solution)/shard_map/ppermute | solution.py:49
  340.8 9.7 %collective-permute-start.32 = (f32[2,32,32]{1,2,0:T(8,128)S(1)}, f32[2,32,32]{1,2,0:T(8,128)S(1)}, u32[]{:S(2)}, u32[]{:S(2)}) collective-permute-start(f32[2,32,32]{1,2,0:T(8,128)S(1)} %add.829), channel_id=1, source_target_pairs={{0,128},{128,0},{256,384},{384,256},{1,129},{129,1},{257,385},{385... | collective-permute-start | bytes 24584 | tf_op jit(solution)/shard_map/ppermute | solution.py:57
  350.5 14.5 %collective-permute-start.33 = (f32[2,32,32]{1,2,0:T(8,128)S(1)}, f32[2,32,32]{1,2,0:T(8,128)S(1)}, u32[]{:S(2)}, u32[]{:S(2)}) collective-permute-start(f32[2,32,32]{1,2,0:T(8,128)S(1)} %add.830), channel_id=1, source_target_pairs={{0,256},{128,384},{256,0},{384,128},{1,257},{129,385},{257,1},{385... | collective-permute-start | bytes 24584 | tf_op jit(solution)/shard_map/ppermute | solution.py:57
  (15 other events, 118.1 us)

commit v3 on v2

--- a/solution.py
+++ b/solution.py
@@ -22,39 +22,23 @@
     return before, after
 
 
-STAGES = (("xl", 0), ("xl", 1), ("gy", 0), ("gy", 2), ("xl", 2), ("gy", 1), ("gy", 3), ("zh", 0), ("zh", 1))
 BLOCK_AXES = ("zh", "xl", "gy")
 
 
-def axis_bits(axis):
-    return lax.axis_size(axis).bit_length() - 1
+def exchange_scatter(x):
+    n = x.shape[0]
+    zh, xl, gy = (lax.axis_size(axis) for axis in BLOCK_AXES)
+    y = x.reshape(n, zh, xl, gy, -1).transpose(0, 2, 1, 3, 4)
+    y = lax.all_to_all(y, "xl", 1, 1, tiled=True).sum(1)
+    y = lax.all_to_all(y.transpose(0, 2, 1, 3), "gy", 1, 1, tiled=True).sum(1)
+    return lax.all_to_all(y, "zh", 1, 1, tiled=True).sum(1)
 
 
-def butterfly_scatter(x):
-    n, cols = x.shape
-    bits = [axis_bits(axis) for axis in BLOCK_AXES]
-    rest = cols >> sum(bits)
-    buf = x.reshape((n,) + (2,) * sum(bits) + (rest,))
-    dims, offset = {}, 1
-    for axis, nb in zip(BLOCK_AXES, bits):
-        dims.update({(axis, b): offset + nb - 1 - b for b in range(nb)})
-        offset += nb
-    live = list(range(buf.ndim))
-    for axis, b in STAGES:
-        d = live.index(dims[(axis, b)])
-        mine = (lax.axis_index(axis) // (2**b)) % 2
-        keep = lax.dynamic_index_in_dim(buf, mine, d, keepdims=False)
-        send = lax.dynamic_index_in_dim(buf, 1 - mine, d, keepdims=False)
-        pairs = [(k, k ^ (2**b)) for k in range(lax.axis_size(axis))]
-        buf = keep + lax.ppermute(send, axis, pairs)
-        live.pop(d)
-    return buf.reshape(n, rest)
-
-
-def butterfly_sum(x):
-    for axis, b in STAGES:
-        pairs = [(k, k ^ (2**b)) for k in range(lax.axis_size(axis))]
-        x = x + lax.ppermute(x, axis, pairs)
+def exchange_sum(x):
+    for axis in ("xl", "gy", "zh"):
+        size = lax.axis_size(axis)
+        copies = jnp.broadcast_to(x[None], (size,) + x.shape)
+        x = lax.all_to_all(copies, axis, 0, 0, tiled=True).sum(0)
     return x
 
 
@@ -85,8 +69,13 @@
 
 
 def shards(orbitals, potential, sign_bits, sampled_rows):
-    group_potential = lax.all_gather(potential, "xl", axis=0, tiled=True)
-    spread = lax.all_to_all(orbitals, "xl", 0, 1, tiled=True)
+    chunks = lax.axis_size("xl")
+    count = orbitals.shape[0]
+    rows = orbitals.reshape((chunks, count // chunks) + orbitals.shape[1:])
+    extra = jnp.broadcast_to(potential[None, None], (chunks, 1) + potential.shape)
+    both = jnp.concatenate([rows, extra], axis=1).reshape((-1,) + orbitals.shape[1:])
+    both = lax.all_to_all(both, "xl", 0, 1, tiled=True)
+    spread, group_potential = both[: count // chunks], both[count // chunks]
     first = (apply_ham(spread, group_potential) - filter_center * spread) / filter_half
     second = 2.0 * (apply_ham(first, group_potential) - filter_center * first) / filter_half - spread
     spread_filtered = (
@@ -106,11 +95,10 @@
     picked = jnp.take(mixed, sampled_rows[0, 0, :M], axis=1)
     devices = lax.axis_size("zh") * lax.axis_size("xl") * lax.axis_size("gy")
     term = (picked / jnp.sqrt(jnp.float32(M * devices))).reshape(2, count, M)
-    assert len(STAGES) == sum(axis_bits(axis) for axis in BLOCK_AXES)
-    share = butterfly_scatter(term.reshape(2 * count, M)).reshape(2, count, -1)
+    share = exchange_scatter(term.reshape(2 * count, M)).reshape(2, count, -1)
     part_gram = jnp.dot(share[0], share[0].T, precision=HIGHEST)
     part_cross = jnp.dot(share[0], share[1].T, precision=HIGHEST)
-    parts = butterfly_sum(jnp.stack([part_gram, part_cross])) / cells
+    parts = exchange_sum(jnp.stack([part_gram, part_cross])) / cells
     gram, cross = parts[0], parts[1]
     lower = jnp.linalg.cholesky(gram)
     inverse = lax.linalg.triangular_solve(

time: 380 us -> 333 us (0.88)
  starting transfers between devices: 158 us -> 88.4 us
  blocking collectives: 36.2 us -> 83.7 us
  waiting for transfers between devices: 122 us -> 82.2 us
  other arithmetic: 20.9 us -> 32 us
  local copies, waits for them, and re-layouts: 30.8 us -> 37.2 us
    ppermute x18 -> x0, starting transfers between devices: 81.3 us -> none  [the longest x9 48 us: butterfly_scatter(): buf = keep + lax.ppermute(send, axis, pairs)]
    ppermute x18 -> x0, waiting for transfers between devices: 79.3 us -> none  [the longest x9 48.2 us: butterfly_scatter(): buf = keep + lax.ppermute(send, axis, pairs)]
    all_to_all x1 -> x5, blocking collectives: 23.3 us -> 83.7 us  [the longest x1 27.8 us: exchange_scatter(): y = lax.all_to_all(y.transpose(0, 2, 1, 3), 'gy', 1, 1, tiled=True).sum(1)]
    all_to_all x0 -> x2, waiting for transfers between devices: none -> 27.8 us  [the longest x1 16.6 us: shards(): both = lax.all_to_all(both, 'xl', 0, 1, tiled=True)]
    all_gather x1 -> x0, blocking collectives: 12.8 us -> none  [shards(): group_potential = lax.all_gather(potential, 'xl', axis=0, tiled=True)]
    all_to_all x0 -> x2, starting transfers between devices: none -> 12.6 us  [the longest x1 9.36 us: shards(): both = lax.all_to_all(both, 'xl', 0, 1, tiled=True)]
    ppermute x8, waiting for transfers between devices: 25.4 us -> 37.6 us  [halos(): after = lax.ppermute(initial, axis, down)]
    all_to_all x0 -> x6, other arithmetic: none -> 8.6 us  [the longest x1 4.5 us: exchange_scatter(): y = lax.all_to_all(y, 'xl', 1, 1, tiled=True).sum(1)]
  transfers between devices with their start and end apart: 36 -> 20, of which waited for: 26 -> 11; matrix products, arithmetic and copies ran while one was open for 2% -> 2% of each run, Pallas kernels for 0% -> 0%
where the time goes in v3:
time: 333 us; the launch traced here: 331 us
  starting transfers between devices  88.4 us (27%)
  blocking collectives  83.7 us (25%)
  waiting for transfers between devices  82.2 us (25%)
  local copies, waits for them, and re-layouts  37.2 us (11%)
  other arithmetic  32 us (10%)
  matrix products  6.61 us (2%)
    ppermute x8, starting transfers between devices, halos(): before = lax.ppermute(last, axis, up)  55.1 us
    ppermute x8, waiting for transfers between devices, halos(): after = lax.ppermute(initial, axis, down)  37.6 us
    all_to_all x1, blocking collectives, exchange_scatter(): y = lax.all_to_all(y.transpose(0, 2, 1, 3), 'gy', 1, 1, tiled=True).sum(1)  27.8 us
    all_to_all x1, blocking collectives, exchange_scatter(): y = lax.all_to_all(y, 'xl', 1, 1, tiled=True).sum(1)  19.6 us
    all_to_all x2, blocking collectives, exchange_sum(): x = lax.all_to_all(copies, axis, 0, 0, tiled=True).sum(0)  19.2 us
    all_to_all x1, blocking collectives, exchange_scatter(): return lax.all_to_all(y, 'zh', 1, 1, tiled=True).sum(1)  17.1 us
    all_to_all x1, waiting for transfers between devices, shards(): both = lax.all_to_all(both, 'xl', 0, 1, tiled=True)  16.6 us
    gather x1, local copies, waits for them, and re-layouts, shards(): picked = jnp.take(mixed, sampled_rows[0, 0, :M], axis=1)  16.4 us
  transfers between devices with their start and end apart: 20, of which 11 were waited for; matrix products, arithmetic and copies ran while one was open for 2% of the time, Pallas kernels for 0%

profile of v3, /device:TPU:6, one launch (start us, length us, event | category | flops | bytes accessed | tf_op | source)
XLA Modules:
  0.0 331.4 jit_solution(8326747168366431138)
XLA Ops:
  3.9 9.4 %all-to-all-start = ((f32[40,2,8,512]{3,2,1,0:T(8,128)}), f32[40,2,8,512]{3,2,1,0:T(8,128)S(1)}, u32[]{:S(2)}, u32[]{:S(2)}) async-start(f32[40,2,8,512]{3,2,1,0:T(8,128)} %bitcast.1), calls=%async_computation | async-start | bytes 2621440 | tf_op jit(solution)/shard_map/all_to_all | solution.py:77
  13.3 16.6 %all-to-all-done = f32[40,2,8,512]{3,2,1,0:T(8,128)S(1)} async-done(((f32[40,2,8,512]{3,2,1,0:T(8,128)}), f32[40,2,8,512]{3,2,1,0:T(8,128)S(1)}, u32[]{:S(2)}, u32[]{:S(2)}) %all-to-all-start) | async-done | bytes 1310752 | tf_op jit(solution)/shard_map/all_to_all | solution.py:77
  32.9 7.1 %collective-permute-start = (f32[4,2,8,512]{3,2,1,0:T(8,128)S(1)}, f32[4,2,8,512]{3,2,1,0:T(8,128)S(1)}, u32[]{:S(2)}, u32[]{:S(2)}) collective-permute-start(f32[4,2,8,512]{3,2,1,0:T(8,128)S(1)} %get-tuple-element.32), channel_id=1, source_target_pairs={{0,128},{128,256},{256,384},{1,129},{129,257},{257,385},{2,130},{1... | collective-permute-start | bytes 393224 | tf_op jit(solution)/shard_map/ppermute | solution.py:20
  42.5 11.5 %collective-permute-done.1 = f32[4,2,8,512]{3,2,1,0:T(8,128)S(1)} collective-permute-done((f32[4,2,8,512]{3,2,1,0:T(8,128)S(1)}, f32[4,2,8,512]{3,2,1,0:T(8,128)S(1)}, u32[]{:S(2)}, u32[]{:S(2)}) %collective-permute-start.1) | collective-permute-done | bytes 131104 | tf_op jit(solution)/shard_map/ppermute | solution.py:21
  56.5 10.4 %collective-permute-start.6 = (f32[4,16,2,512]{3,2,1,0:T(2,128)S(1)}, f32[4,16,2,512]{3,2,1,0:T(2,128)S(1)}, u32[]{:S(2)}, u32[]{:S(2)}) collective-permute-start(f32[4,16,2,512]{3,2,1,0:T(2,128)S(1)} %get-tuple-element.28), channel_id=1, source_target_pairs={{0,1},{1,2},{2,3},{3,4},{4,5},{5,6},{6,7},{7,8},{8,9},{9,10},{10,1... | collective-permute-start | bytes 786440 | tf_op jit(solution)/shard_map/ppermute | solution.py:20
  68.3 7.7 %collective-permute-start.4 = (f32[4,2,8,512]{3,2,1,0:T(8,128)S(1)}, f32[4,2,8,512]{3,2,1,0:T(8,128)S(1)}, u32[]{:S(2)}, u32[]{:S(2)}) collective-permute-start(f32[4,2,8,512]{3,2,1,0:T(8,128)S(1)} %get-tuple-element.30), channel_id=1, source_target_pairs={{0,128},{128,256},{256,384},{1,129},{129,257},{257,385},{2,130},{1... | collective-permute-start | bytes 393224 | tf_op jit(solution)/shard_map/ppermute | solution.py:20
  78.5 8.3 %collective-permute-done.5 = f32[4,2,8,512]{3,2,1,0:T(8,128)S(1)} collective-permute-done((f32[4,2,8,512]{3,2,1,0:T(8,128)S(1)}, f32[4,2,8,512]{3,2,1,0:T(8,128)S(1)}, u32[]{:S(2)}, u32[]{:S(2)}) %collective-permute-start.5) | collective-permute-done | bytes 131104 | tf_op jit(solution)/shard_map/ppermute | solution.py:21
  89.4 11.6 %collective-permute-start.10 = (f32[4,16,2,512]{3,2,1,0:T(2,128)S(1)}, f32[4,16,2,512]{3,2,1,0:T(2,128)S(1)}, u32[]{:S(2)}, u32[]{:S(2)}) collective-permute-start(f32[4,16,2,512]{3,2,1,0:T(2,128)S(1)} %get-tuple-element.24), channel_id=1, source_target_pairs={{0,1},{1,2},{2,3},{3,4},{4,5},{5,6},{6,7},{7,8},{8,9},{9,10},{10,1... | collective-permute-start | bytes 786440 | tf_op jit(solution)/shard_map/ppermute | solution.py:20
  107.5 8.5 %collective-permute-done.9 = f32[4,2,8,512]{3,2,1,0:T(8,128)S(1)} collective-permute-done((f32[4,2,8,512]{3,2,1,0:T(8,128)S(1)}, f32[4,2,8,512]{3,2,1,0:T(8,128)S(1)}, u32[]{:S(2)}, u32[]{:S(2)}) %collective-permute-start.9) | collective-permute-done | bytes 131104 | tf_op jit(solution)/shard_map/ppermute | solution.py:21
  120.5 8.1 %collective-permute-start.14 = (f32[4,16,2,512]{3,2,1,0:T(2,128)S(1)}, f32[4,16,2,512]{3,2,1,0:T(2,128)S(1)}, u32[]{:S(2)}, u32[]{:S(2)}) collective-permute-start(f32[4,16,2,512]{3,2,1,0:T(2,128)S(1)} %get-tuple-element.20), channel_id=1, source_target_pairs={{0,1},{1,2},{2,3},{3,4},{4,5},{5,6},{6,7},{7,8},{8,9},{9,10},{10,1... | collective-permute-start | bytes 786440 | tf_op jit(solution)/shard_map/ppermute | solution.py:20
  129.9 5.6 %all-to-all-start.1 = ((f32[4,16,8,512]{3,2,0,1:T(8,128)}), f32[4,16,8,512]{3,2,0,1:T(8,128)S(1)}, u32[]{:S(2)}, u32[]{:S(2)}) async-start(f32[4,16,8,512]{3,2,0,1:T(8,128)} %copy.45), calls=%async_computation.1 | async-start | bytes 2097152 | tf_op jit(solution)/shard_map/all_to_all | solution.py:85
  136.2 6.3 %collective-permute-start.12 = (f32[4,2,8,512]{3,2,1,0:T(8,128)}, f32[4,2,8,512]{3,2,1,0:T(8,128)}, u32[]{:S(2)}, u32[]{:S(2)}) collective-permute-start(f32[4,2,8,512]{3,2,1,0:T(8,128)} %get-tuple-element.22), channel_id=1, source_target_pairs={{0,128},{128,256},{256,384},{1,129},{129,257},{257,385},{2,130},{1... | collective-permute-start | bytes 393224 | tf_op jit(solution)/shard_map/ppermute | solution.py:20
  145.2 8.6 %collective-permute-done.13 = f32[4,2,8,512]{3,2,1,0:T(8,128)} collective-permute-done((f32[4,2,8,512]{3,2,1,0:T(8,128)}, f32[4,2,8,512]{3,2,1,0:T(8,128)}, u32[]{:S(2)}, u32[]{:S(2)}) %collective-permute-start.13) | collective-permute-done | bytes 131104 | tf_op jit(solution)/shard_map/ppermute | solution.py:21
  157.6 4.8 %all-to-all-start.2 = ((f32[4,16,8,512]{3,2,0,1:T(8,128)}), f32[4,16,8,512]{3,2,0,1:T(8,128)S(1)}, u32[]{:S(2)}, u32[]{:S(2)}) async-start(f32[4,16,8,512]{3,2,0,1:T(8,128)} %copy.47), calls=%async_computation.2 | async-start | bytes 2097152 | tf_op jit(solution)/shard_map/all_to_all | solution.py:86
  162.6 13.7 %all-to-all-done.2 = f32[4,16,8,512]{3,2,0,1:T(8,128)S(1)} async-done(((f32[4,16,8,512]{3,2,0,1:T(8,128)}), f32[4,16,8,512]{3,2,0,1:T(8,128)S(1)}, u32[]{:S(2)}, u32[]{:S(2)}) %all-to-all-start.2) | async-done | bytes 1048608 | tf_op jit(solution)/shard_map/all_to_all | solution.py:86
  185.5 16.4 %gather_fusion = f32[4096,64]{1,0:T(8,128)} fusion(f32[64,8192]{0,1:T(8,128)} %bitcast.95, s32[4096]{0:T(1024)S(1)} %broadcast_clamp_fusion), kind=kCustom, calls=%fused_computation | custom fusion | bytes 2113536 | tf_op jit(solution)/shard_map/jit(_take)/gather | solution.py:95
  206.3 19.6 %all_to_all.75 = f32[8,1,32768]{2,1,0:T(1,128)S(1)} all-to-all(f32[8,1,32768]{2,1,0:T(1,128)} %reshape.1335), channel_id=1, replica_groups=mesh['zh'=4,'xl'=8,'gy'=16] {'xl'}, dimensions={0} | all-to-all | bytes 2097152 | tf_op jit(solution)/shard_map/all_to_all | solution.py:32
  226.4 4.5 %reduce.10 = f32[8,32768]{1,0:T(8,128)} reduce(f32[8,1,32768]{2,1,0:T(1,128)S(1)} %all_to_all.75, f32[]{:T(128)} %broadcast.1731), dimensions={1}, to_apply=%all_to_all.60.reduce_sub_computation | reduce | bytes 2097156 | tf_op jit(solution)/shard_map/all_to_all | solution.py:32
  233.4 27.8 %all_to_all.76 = f32[16,1,2048]{2,1,0:T(1,128)S(1)} all-to-all(f32[16,1,2048]{2,1,0:T(1,128)S(1)} %reshape.1337), channel_id=1, replica_groups=mesh['zh'=4,'xl'=8,'gy'=16] {'gy'}, dimensions={0} | all-to-all | bytes 262144 | tf_op jit(solution)/shard_map/all_to_all | solution.py:33
  262.3 17.1 %all_to_all.77 = f32[4,1,512]{2,1,0:T(1,128)S(1)} all-to-all(f32[4,1,512]{2,1,0:T(1,128)S(1)} %reshape.1339), channel_id=1, replica_groups=mesh['zh'=4,'xl'=8,'gy'=16] {'zh'}, dimensions={0} | all-to-all | bytes 16384 | tf_op jit(solution)/shard_map/all_to_all | solution.py:34
  280.9 8.0 %all_to_all.78 = f32[8,1,2048]{2,1,0:T(1,128)S(1)} all-to-all(f32[8,1,2048]{2,1,0:T(1,128)S(1)} %reshape.1341), channel_id=1, replica_groups=mesh['zh'=4,'xl'=8,'gy'=16] {'xl'}, dimensions={0} | all-to-all | bytes 131072 | tf_op jit(solution)/shard_map/all_to_all | solution.py:41
  290.2 11.2 %all_to_all.79 = f32[16,1,2048]{2,1,0:T(1,128)S(1)} all-to-all(f32[16,1,2048]{2,1,0:T(1,128)S(1)} %reshape.1343), channel_id=1, replica_groups=mesh['zh'=4,'xl'=8,'gy'=16] {'gy'}, dimensions={0} | all-to-all | bytes 262144 | tf_op jit(solution)/shard_map/all_to_all | solution.py:41
  303.3 3.3 all-to-all-start.8
  308.1 11.1 %all-to-all-done.8 = f32[4,1,2048]{2,1,0:T(1,128)S(1)} async-done(((f32[4,1,2048]{2,1,0:T(1,128)}), f32[4,1,2048]{2,1,0:T(1,128)S(1)}, u32[]{:S(2)}, u32[]{:S(2)}) %all-to-all-start.8) | async-done | bytes 32800 | tf_op jit(solution)/shard_map/all_to_all | solution.py:41
  (128 shorter events, 73.1 us)
Async XLA Ops:
  1.4 11.8 %copy-start.1 = (s32[2,8,512]{2,1,0:T(8,128)S(1)}, s32[2,8,512]{2,1,0:T(8,128)}, u32[]{:S(2)}) copy-start(s32[2,8,512]{2,1,0:T(8,128)} %param.6) | copy-start | bytes 98308
  3.9 26.0 %all-to-all-start = ((f32[40,2,8,512]{3,2,1,0:T(8,128)}), f32[40,2,8,512]{3,2,1,0:T(8,128)S(1)}, u32[]{:S(2)}, u32[]{:S(2)}) async-start(f32[40,2,8,512]{3,2,1,0:T(8,128)} %bitcast.1), calls=%async_computation | async-start | bytes 2621440 | tf_op jit(solution)/shard_map/all_to_all | solution.py:77
  30.3 23.7 %collective-permute-start.2 = (f32[4,16,2,512]{3,2,1,0:T(2,128)S(1)}, f32[4,16,2,512]{3,2,1,0:T(2,128)S(1)}, u32[]{:S(2)}, u32[]{:S(2)}) collective-permute-start(f32[4,16,2,512]{3,2,1,0:T(2,128)S(1)} %get-tuple-element.34), channel_id=1, source_target_pairs={{0,1},{1,2},{2,3},{3,4},{4,5},{5,6},{6,7},{7,8},{8,9},{9,10},{10,1... | collective-permute-start | bytes 786440 | tf_op jit(solution)/shard_map/ppermute | solution.py:20
  31.6 22.4 %collective-permute-start.3 = (f32[4,16,2,512]{3,2,1,0:T(2,128)S(1)}, f32[4,16,2,512]{3,2,1,0:T(2,128)S(1)}, u32[]{:S(2)}, u32[]{:S(2)}) collective-permute-start(f32[4,16,2,512]{3,2,1,0:T(2,128)S(1)} %get-tuple-element.35), channel_id=1, source_target_pairs={{1,0},{2,1},{3,2},{4,3},{5,4},{6,5},{7,6},{8,7},{9,8},{10,9},{11,1... | collective-permute-start | bytes 786440 | tf_op jit(solution)/shard_map/ppermute | solution.py:21
  32.9 9.6 %collective-permute-start = (f32[4,2,8,512]{3,2,1,0:T(8,128)S(1)}, f32[4,2,8,512]{3,2,1,0:T(8,128)S(1)}, u32[]{:S(2)}, u32[]{:S(2)}) collective-permute-start(f32[4,2,8,512]{3,2,1,0:T(8,128)S(1)} %get-tuple-element.32), channel_id=1, source_target_pairs={{0,128},{128,256},{256,384},{1,129},{129,257},{257,385},{2,130},{1... | collective-permute-start | bytes 393224 | tf_op jit(solution)/shard_map/ppermute | solution.py:20
  40.0 13.9 %collective-permute-start.1 = (f32[4,2,8,512]{3,2,1,0:T(8,128)S(1)}, f32[4,2,8,512]{3,2,1,0:T(8,128)S(1)}, u32[]{:S(2)}, u32[]{:S(2)}) collective-permute-start(f32[4,2,8,512]{3,2,1,0:T(8,128)S(1)} %get-tuple-element.33), channel_id=1, source_target_pairs={{128,0},{256,128},{384,256},{129,1},{257,129},{385,257},{130,2},{2... | collective-permute-start | bytes 393224 | tf_op jit(solution)/shard_map/ppermute | solution.py:21
  56.5 30.2 %collective-permute-start.6 = (f32[4,16,2,512]{3,2,1,0:T(2,128)S(1)}, f32[4,16,2,512]{3,2,1,0:T(2,128)S(1)}, u32[]{:S(2)}, u32[]{:S(2)}) collective-permute-start(f32[4,16,2,512]{3,2,1,0:T(2,128)S(1)} %get-tuple-element.28), channel_id=1, source_target_pairs={{0,1},{1,2},{2,3},{3,4},{4,5},{5,6},{6,7},{7,8},{8,9},{9,10},{10,1... | collective-permute-start | bytes 786440 | tf_op jit(solution)/shard_map/ppermute | solution.py:20
  67.0 19.8 %collective-permute-start.7 = (f32[4,16,2,512]{3,2,1,0:T(2,128)S(1)}, f32[4,16,2,512]{3,2,1,0:T(2,128)S(1)}, u32[]{:S(2)}, u32[]{:S(2)}) collective-permute-start(f32[4,16,2,512]{3,2,1,0:T(2,128)S(1)} %get-tuple-element.29), channel_id=1, source_target_pairs={{1,0},{2,1},{3,2},{4,3},{5,4},{6,5},{7,6},{8,7},{9,8},{10,9},{11,1... | collective-permute-start | bytes 786440 | tf_op jit(solution)/shard_map/ppermute | solution.py:21
  68.3 10.2 %collective-permute-start.4 = (f32[4,2,8,512]{3,2,1,0:T(8,128)S(1)}, f32[4,2,8,512]{3,2,1,0:T(8,128)S(1)}, u32[]{:S(2)}, u32[]{:S(2)}) collective-permute-start(f32[4,2,8,512]{3,2,1,0:T(8,128)S(1)} %get-tuple-element.30), channel_id=1, source_target_pairs={{0,128},{128,256},{256,384},{1,129},{129,257},{257,385},{2,130},{1... | collective-permute-start | bytes 393224 | tf_op jit(solution)/shard_map/ppermute | solution.py:20
  76.0 10.8 %collective-permute-start.5 = (f32[4,2,8,512]{3,2,1,0:T(8,128)S(1)}, f32[4,2,8,512]{3,2,1,0:T(8,128)S(1)}, u32[]{:S(2)}, u32[]{:S(2)}) collective-permute-start(f32[4,2,8,512]{3,2,1,0:T(8,128)S(1)} %get-tuple-element.31), channel_id=1, source_target_pairs={{128,0},{256,128},{384,256},{129,1},{257,129},{385,257},{130,2},{2... | collective-permute-start | bytes 393224 | tf_op jit(solution)/shard_map/ppermute | solution.py:21
  86.8 20.0 %copy-start.2 = (s32[1,1,8192]{2,1,0:T(1,128)S(1)}, s32[1,1,8192]{2,1,0:T(1,128)}, u32[]{:S(2)}) copy-start(s32[1,1,8192]{2,1,0:T(1,128)} %param.7) | copy-start | bytes 98308
  89.4 26.6 %collective-permute-start.10 = (f32[4,16,2,512]{3,2,1,0:T(2,128)S(1)}, f32[4,16,2,512]{3,2,1,0:T(2,128)S(1)}, u32[]{:S(2)}, u32[]{:S(2)}) collective-permute-start(f32[4,16,2,512]{3,2,1,0:T(2,128)S(1)} %get-tuple-element.24), channel_id=1, source_target_pairs={{0,1},{1,2},{2,3},{3,4},{4,5},{5,6},{6,7},{7,8},{8,9},{9,10},{10,1... | collective-permute-start | bytes 786440 | tf_op jit(solution)/shard_map/ppermute | solution.py:20
  101.0 15.8 %collective-permute-start.11 = (f32[4,16,2,512]{3,2,1,0:T(2,128)S(1)}, f32[4,16,2,512]{3,2,1,0:T(2,128)S(1)}, u32[]{:S(2)}, u32[]{:S(2)}) collective-permute-start(f32[4,16,2,512]{3,2,1,0:T(2,128)S(1)} %get-tuple-element.25), channel_id=1, source_target_pairs={{1,0},{2,1},{3,2},{4,3},{5,4},{6,5},{7,6},{8,7},{9,8},{10,9},{11,1... | collective-permute-start | bytes 786440 | tf_op jit(solution)/shard_map/ppermute | solution.py:21
  102.3 5.2 %collective-permute-start.8 = (f32[4,2,8,512]{3,2,1,0:T(8,128)S(1)}, f32[4,2,8,512]{3,2,1,0:T(8,128)S(1)}, u32[]{:S(2)}, u32[]{:S(2)}) collective-permute-start(f32[4,2,8,512]{3,2,1,0:T(8,128)S(1)} %get-tuple-element.26), channel_id=1, source_target_pairs={{0,128},{128,256},{256,384},{1,129},{129,257},{257,385},{2,130},{1... | collective-permute-start | bytes 393224 | tf_op jit(solution)/shard_map/ppermute | solution.py:20
  105.0 11.0 %collective-permute-start.9 = (f32[4,2,8,512]{3,2,1,0:T(8,128)S(1)}, f32[4,2,8,512]{3,2,1,0:T(8,128)S(1)}, u32[]{:S(2)}, u32[]{:S(2)}) collective-permute-start(f32[4,2,8,512]{3,2,1,0:T(8,128)S(1)} %get-tuple-element.27), channel_id=1, source_target_pairs={{128,0},{256,128},{384,256},{129,1},{257,129},{385,257},{130,2},{2... | collective-permute-start | bytes 393224 | tf_op jit(solution)/shard_map/ppermute | solution.py:21
  120.5 33.3 %collective-permute-start.14 = (f32[4,16,2,512]{3,2,1,0:T(2,128)S(1)}, f32[4,16,2,512]{3,2,1,0:T(2,128)S(1)}, u32[]{:S(2)}, u32[]{:S(2)}) collective-permute-start(f32[4,16,2,512]{3,2,1,0:T(2,128)S(1)} %get-tuple-element.20), channel_id=1, source_target_pairs={{0,1},{1,2},{2,3},{3,4},{4,5},{5,6},{6,7},{7,8},{8,9},{9,10},{10,1... | collective-permute-start | bytes 786440 | tf_op jit(solution)/shard_map/ppermute | solution.py:20
  128.6 25.2 %collective-permute-start.15 = (f32[4,16,2,512]{3,2,1,0:T(2,128)S(1)}, f32[4,16,2,512]{3,2,1,0:T(2,128)S(1)}, u32[]{:S(2)}, u32[]{:S(2)}) collective-permute-start(f32[4,16,2,512]{3,2,1,0:T(2,128)S(1)} %get-tuple-element.21), channel_id=1, source_target_pairs={{1,0},{2,1},{3,2},{4,3},{5,4},{6,5},{7,6},{8,7},{9,8},{10,9},{11,1... | collective-permute-start | bytes 786440 | tf_op jit(solution)/shard_map/ppermute | solution.py:21
  129.9 27.7 %all-to-all-start.1 = ((f32[4,16,8,512]{3,2,0,1:T(8,128)}), f32[4,16,8,512]{3,2,0,1:T(8,128)S(1)}, u32[]{:S(2)}, u32[]{:S(2)}) async-start(f32[4,16,8,512]{3,2,0,1:T(8,128)} %copy.45), calls=%async_computation.1 | async-start | bytes 2097152 | tf_op jit(solution)/shard_map/all_to_all | solution.py:85
  136.2 9.0 %collective-permute-start.12 = (f32[4,2,8,512]{3,2,1,0:T(8,128)}, f32[4,2,8,512]{3,2,1,0:T(8,128)}, u32[]{:S(2)}, u32[]{:S(2)}) collective-permute-start(f32[4,2,8,512]{3,2,1,0:T(8,128)} %get-tuple-element.22), channel_id=1, source_target_pairs={{0,128},{128,256},{256,384},{1,129},{129,257},{257,385},{2,130},{1... | collective-permute-start | bytes 393224 | tf_op jit(solution)/shard_map/ppermute | solution.py:20
  142.5 11.4 %collective-permute-start.13 = (f32[4,2,8,512]{3,2,1,0:T(8,128)}, f32[4,2,8,512]{3,2,1,0:T(8,128)}, u32[]{:S(2)}, u32[]{:S(2)}) collective-permute-start(f32[4,2,8,512]{3,2,1,0:T(8,128)} %get-tuple-element.23), channel_id=1, source_target_pairs={{128,0},{256,128},{384,256},{129,1},{257,129},{385,257},{130,2},{2... | collective-permute-start | bytes 393224 | tf_op jit(solution)/shard_map/ppermute | solution.py:21
  157.6 18.7 %all-to-all-start.2 = ((f32[4,16,8,512]{3,2,0,1:T(8,128)}), f32[4,16,8,512]{3,2,0,1:T(8,128)S(1)}, u32[]{:S(2)}, u32[]{:S(2)}) async-start(f32[4,16,8,512]{3,2,0,1:T(8,128)} %copy.47), calls=%async_computation.2 | async-start | bytes 2097152 | tf_op jit(solution)/shard_map/all_to_all | solution.py:86
  176.3 2.4 copy-start.5
  185.5 16.4 %copy-start = (s32[4,8,16,8]{3,2,1,0:T(8,128)S(1)}, s32[4,8,16,8]{3,2,1,0:T(8,128)}, u32[]{:S(2)}) copy-start(s32[4,8,16,8]{3,2,1,0:T(8,128)} %squeeze.15) | copy-start | bytes 49156
  303.3 15.9 %all-to-all-start.8 = ((f32[4,1,2048]{2,1,0:T(1,128)}), f32[4,1,2048]{2,1,0:T(1,128)S(1)}, u32[]{:S(2)}, u32[]{:S(2)}) async-start(f32[4,1,2048]{2,1,0:T(1,128)} %reshape.1345), calls=%async_computation.8 | async-start | bytes 65536 | tf_op jit(solution)/shard_map/all_to_all | solution.py:41
  (2 other events, 4.1 us)

commit v4 on v3

--- a/solution.py
+++ b/solution.py
@@ -20,6 +20,50 @@
     before = lax.ppermute(last, axis, up)
     after = lax.ppermute(initial, axis, down)
     return before, after
+
+
+def corner(array, dx, dy, width):
+    sx, sy = lax.axis_size("zh"), lax.axis_size("gy")
+    xs = slice(array.shape[1] - width, None) if dx > 0 else slice(0, width)
+    ys = slice(array.shape[2] - width, None) if dy > 0 else slice(0, width)
+    pairs = [
+        (k * sy + j, (k + dx) * sy + (j + dy))
+        for k in range(sx)
+        for j in range(sy)
+        if 0 <= k + dx < sx and 0 <= j + dy < sy
+    ]
+    return lax.ppermute(array[:, xs, ys], ("zh", "gy"), pairs)
+
+
+def exchange(field, width):
+    x_before, x_after = halos(field, "zh", 1, width)
+    y_before, y_after = halos(field, "gy", 2, width)
+    top = [corner(field, 1, 1, width), x_before, corner(field, 1, -1, width)]
+    bottom = [corner(field, -1, 1, width), x_after, corner(field, -1, -1, width)]
+    rows = [
+        jnp.concatenate(top, axis=2),
+        jnp.concatenate([y_before, field, y_after], axis=2),
+        jnp.concatenate(bottom, axis=2),
+    ]
+    return jnp.concatenate(rows, axis=1)
+
+
+def on_grid(field, width):
+    sx, sy = lax.axis_size("zh"), lax.axis_size("gy")
+    inner_x, inner_y = field.shape[1] - 2 * width, field.shape[2] - 2 * width
+    x = lax.axis_index("zh") * inner_x - width + lax.broadcasted_iota(jnp.int32, field.shape[1:3], 0)
+    y = lax.axis_index("gy") * inner_y - width + lax.broadcasted_iota(jnp.int32, field.shape[1:3], 1)
+    inside = (x >= 0) & (x < sx * inner_x) & (y >= 0) & (y < sy * inner_y)
+    return jnp.where(inside[None, :, :, None], field, 0.0)
+
+
+def ham_inside(padded, potential):
+    core = padded[:, 2:-2, 2:-2]
+    total = second_diff(padded[:, :, 2:-2], 1, core.shape[1])
+    total = total + second_diff(padded[:, 2:-2, :], 2, core.shape[2])
+    z_padded = jnp.pad(core, ((0, 0), (0, 0), (0, 0), (2, 2)))
+    total = total + second_diff(z_padded, 3, core.shape[3])
+    return -0.5 * total + potential[None] * core
 
 
 BLOCK_AXES = ("zh", "xl", "gy")
@@ -76,12 +120,25 @@
     both = jnp.concatenate([rows, extra], axis=1).reshape((-1,) + orbitals.shape[1:])
     both = lax.all_to_all(both, "xl", 0, 1, tiled=True)
     spread, group_potential = both[: count // chunks], both[count // chunks]
-    first = (apply_ham(spread, group_potential) - filter_center * spread) / filter_half
-    second = 2.0 * (apply_ham(first, group_potential) - filter_center * first) / filter_half - spread
-    spread_filtered = (
-        2.0 * (apply_ham(second, group_potential) - filter_center * second) / filter_half - first
+    wide = exchange(jnp.concatenate([spread, group_potential[None]], axis=0), 4)
+    rings, wide_potential = wide[: count // chunks], wide[count // chunks, 2:-2, 2:-2]
+    inner_potential = group_potential
+    near = rings[:, 2:-2, 2:-2]
+    first = on_grid((ham_inside(rings, wide_potential) - filter_center * near) / filter_half, 2)
+    inner_first = first[:, 2:-2, 2:-2]
+    second = (
+        2.0 * (ham_inside(first, inner_potential) - filter_center * inner_first) / filter_half - spread
     )
-    spread_applied = apply_ham(spread_filtered, group_potential)
+    wide = exchange(jnp.concatenate([second, inner_first], axis=0), 4)
+    second_rings, first_rings = wide[: count // chunks], wide[count // chunks :]
+    near = second_rings[:, 2:-2, 2:-2]
+    spread_filtered = on_grid(
+        2.0 * (ham_inside(second_rings, wide_potential) - filter_center * near) / filter_half
+        - first_rings[:, 2:-2, 2:-2],
+        2,
+    )
+    spread_applied = ham_inside(spread_filtered, inner_potential)
+    spread_filtered = spread_filtered[:, 2:-2, 2:-2]
     filtered = lax.all_to_all(spread_filtered, "xl", 1, 0, tiled=True)
     applied = lax.all_to_all(spread_applied, "xl", 1, 0, tiled=True)
     count = orbitals.shape[0]

time: 333 us -> 546 us (1.64)
  waiting for transfers between devices: 82.2 us -> 160 us
  starting transfers between devices: 88.4 us -> 152 us
  blocking collectives: 83.7 us -> 119 us
  other arithmetic: 32 us -> 66.8 us
    ppermute x0 -> x8, waiting for transfers between devices: none -> 106 us  [corner(): return lax.ppermute(array[:, xs, ys], ('zh', 'gy'), pairs)]
    ppermute x0 -> x8, starting transfers between devices: none -> 59.4 us  [corner(): return lax.ppermute(array[:, xs, ys], ('zh', 'gy'), pairs)]
    ppermute x8 -> x4, waiting for transfers between devices: 37.6 us -> 0.01 us  [halos(): after = lax.ppermute(initial, axis, down)]
    select_n x0 -> x2, other arithmetic: none -> 28.7 us  [on_grid(): return jnp.where(inside[None, :, :, None], field, 0.0)]
    all_to_all x1, blocking collectives: 27.8 us -> 47.8 us  [exchange_scatter(): y = lax.all_to_all(y.transpose(0, 2, 1, 3), 'gy', 1, 1, tiled=True).sum(1)]
    all_to_all x1, blocking collectives: 17.1 us -> 32.2 us  [exchange_scatter(): return lax.all_to_all(y, 'zh', 1, 1, tiled=True).sum(1)]
    all_to_all x1, waiting for transfers between devices: 0.01 us -> 13.7 us  [shards(): filtered = lax.all_to_all(spread_filtered, 'xl', 1, 0, tiled=True)]
    ppermute x8 -> x4, starting transfers between devices: 55.1 us -> 63.6 us  [halos(): before = lax.ppermute(last, axis, up)]
  transfers between devices with their start and end apart: 20 -> 20, of which waited for: 11 -> 8; matrix products, arithmetic and copies ran while one was open for 2% -> 1% of each run, Pallas kernels for 0% -> 0%
where the time goes in v4:
time: 546 us; the launch traced here: 544 us
  waiting for transfers between devices  160 us (29%)
  starting transfers between devices  152 us (28%)
  blocking collectives  119 us (22%)
  other arithmetic  66.8 us (12%)
  local copies, waits for them, and re-layouts  38.8 us (7%)
  matrix products  6.6 us (1%)
    ppermute x8, waiting for transfers between devices, corner(): return lax.ppermute(array[:, xs, ys], ('zh', 'gy'), pairs)  106 us
    ppermute x4, starting transfers between devices, halos(): before = lax.ppermute(last, axis, up)  63.6 us
    ppermute x8, starting transfers between devices, corner(): return lax.ppermute(array[:, xs, ys], ('zh', 'gy'), pairs)  59.4 us
    all_to_all x1, blocking collectives, exchange_scatter(): y = lax.all_to_all(y.transpose(0, 2, 1, 3), 'gy', 1, 1, tiled=True).sum(1)  47.8 us
    all_to_all x1, blocking collectives, exchange_scatter(): return lax.all_to_all(y, 'zh', 1, 1, tiled=True).sum(1)  32.2 us
    select_n x2, other arithmetic, on_grid(): return jnp.where(inside[None, :, :, None], field, 0.0)  28.7 us
    all_to_all x1, blocking collectives, exchange_scatter(): y = lax.all_to_all(y, 'xl', 1, 1, tiled=True).sum(1)  19.6 us
    all_to_all x2, blocking collectives, exchange_sum(): x = lax.all_to_all(copies, axis, 0, 0, tiled=True).sum(0)  19.2 us
  transfers between devices with their start and end apart: 20, of which 8 were waited for; matrix products, arithmetic and copies ran while one was open for 1% of the time, Pallas kernels for 0%

profile of v4, /device:TPU:6, one launch (start us, length us, event | category | flops | bytes accessed | tf_op | source)
XLA Modules:
  0.0 543.8 jit_solution(4778125973930224326)
XLA Ops:
  3.9 9.4 %all-to-all-start = ((f32[40,2,8,512]{3,2,1,0:T(8,128)}), f32[40,2,8,512]{3,2,1,0:T(8,128)S(1)}, u32[]{:S(2)}, u32[]{:S(2)}) async-start(f32[40,2,8,512]{3,2,1,0:T(8,128)} %bitcast.1), calls=%async_computation | async-start | bytes 2621440 | tf_op jit(solution)/shard_map/all_to_all | solution.py:121
  13.2 16.7 %all-to-all-done = f32[40,2,8,512]{3,2,1,0:T(8,128)S(1)} async-done(((f32[40,2,8,512]{3,2,1,0:T(8,128)}), f32[40,2,8,512]{3,2,1,0:T(8,128)S(1)}, u32[]{:S(2)}, u32[]{:S(2)}) %all-to-all-start) | async-done | bytes 1310752 | tf_op jit(solution)/shard_map/all_to_all | solution.py:121
  34.7 9.1 %collective-permute-start = (f32[5,4,4,512]{3,2,1,0:T(4,128)}, f32[5,4,4,512]{3,2,1,0:T(4,128)S(1)}, u32[]{:S(2)}, u32[]{:S(2)}) collective-permute-start(f32[5,4,4,512]{3,2,1,0:T(4,128)} %get-tuple-element.26), channel_id=1, source_target_pairs={{0,129},{1,130},{2,131},{3,132},{4,133},{5,134},{6,135},{7,136},{8... | collective-permute-start | bytes 491528 | tf_op jit(solution)/shard_map/ppermute | solution.py:35
  50.5 21.5 %collective-permute-start.1 = (f32[5,4,8,512]{3,2,1,0:T(8,128)S(1)}, f32[5,4,8,512]{3,2,1,0:T(8,128)S(1)}, u32[]{:S(2)}, u32[]{:S(2)}) collective-permute-start(f32[5,4,8,512]{3,2,1,0:T(8,128)S(1)} %get-tuple-element.30), channel_id=1, source_target_pairs={{0,128},{128,256},{256,384},{1,129},{129,257},{257,385},{2,130},{1... | collective-permute-start | bytes 983048 | tf_op jit(solution)/shard_map/ppermute | solution.py:20
  74.7 48.5 %collective-permute-done.7 = f32[5,4,4,512]{3,2,1,0:T(4,128)S(1)} collective-permute-done((f32[5,4,4,512]{3,2,1,0:T(4,128)}, f32[5,4,4,512]{3,2,1,0:T(4,128)S(1)}, u32[]{:S(2)}, u32[]{:S(2)}) %collective-permute-start.7) | collective-permute-done | bytes 163872 | tf_op jit(solution)/shard_map/ppermute | solution.py:35
  127.1 12.9 %fusion.9 = f32[4,20,12,512]{3,2,1,0:T(8,128)S(1)} fusion(f32[4,20,12,512]{3,2,1,0:T(8,128)} %slice.428, f32[5,24,16,512]{3,2,1,0:T(8,128)S(1)} %maximum_maximum_fusion.1, f32[5,4,4,512]{3,2,1,0:T(4,128)S(1)} %collective-permute-done.7, f32[5,16,4,512]{3,2,1,0:T(4,128)S(1)} %collective-permute-done.4, f32[5,4,8,512]{3,2,1,0:T(8,128)S(1)} %collective-permute-done.6, ...), kind=kLoop, calls=%fused_computation.41 | loop fusion | flops 18186240 | bytes 20152560 | tf_op jit(solution)/shard_map/jit(_where)/select_n | solution.py:57
  142.8 9.0 %collective-permute-start.11 = (f32[8,16,4,512]{3,2,1,0:T(4,128)S(1)}, f32[8,16,4,512]{3,2,1,0:T(4,128)S(1)}, u32[]{:S(2)}, u32[]{:S(2)}) collective-permute-start(f32[8,16,4,512]{3,2,1,0:T(4,128)S(1)} %get-tuple-element.24), channel_id=1, source_target_pairs={{0,1},{1,2},{2,3},{3,4},{4,5},{5,6},{6,7},{7,8},{8,9},{9,10},{10,1... | collective-permute-start | bytes 3145736 | tf_op jit(solution)/shard_map/ppermute | solution.py:20
  157.4 31.8 %collective-permute-start.9 = (f32[8,4,8,512]{3,2,1,0:T(8,128)S(1)}, f32[8,4,8,512]{3,2,1,0:T(8,128)S(1)}, u32[]{:S(2)}, u32[]{:S(2)}) collective-permute-start(f32[8,4,8,512]{3,2,1,0:T(8,128)S(1)} %get-tuple-element.22), channel_id=1, source_target_pairs={{0,128},{128,256},{256,384},{1,129},{129,257},{257,385},{2,130},{1... | collective-permute-start | bytes 1572872 | tf_op jit(solution)/shard_map/ppermute | solution.py:20
  189.2 47.2 %collective-permute-done.15 = f32[8,4,4,512]{3,2,1,0:T(4,128)S(1)} collective-permute-done((f32[8,4,4,512]{3,2,1,0:T(4,128)S(1)}, f32[8,4,4,512]{3,2,1,0:T(4,128)S(1)}, u32[]{:S(2)}, u32[]{:S(2)}) %collective-permute-start.15) | collective-permute-done | bytes 262176 | tf_op jit(solution)/shard_map/ppermute | solution.py:35
  236.4 44.4 %collective-permute-start.8 = (f32[8,4,4,512]{3,2,1,0:T(4,128)S(1)}, f32[8,4,4,512]{3,2,1,0:T(4,128)S(1)}, u32[]{:S(2)}, u32[]{:S(2)}) collective-permute-start(f32[8,4,4,512]{3,2,1,0:T(4,128)S(1)} %get-tuple-element.18), channel_id=1, source_target_pairs={{0,129},{1,130},{2,131},{3,132},{4,133},{5,134},{6,135},{7,136},{8... | collective-permute-start | bytes 786440 | tf_op jit(solution)/shard_map/ppermute | solution.py:35
  280.8 5.3 collective-permute-done.8
  289.8 15.7 %fusion.21 = f32[4,20,12,512]{3,2,1,0:T(8,128)} fusion(f32[4,20,12,512]{3,2,1,0:T(8,128)} %slice.459, f32[8,24,16,512]{3,2,1,0:T(8,128)S(1)} %maximum_maximum_fusion, f32[8,4,4,512]{3,2,1,0:T(4,128)} %copy-done.7, f32[8,16,4,512]{3,2,1,0:T(4,128)} %copy-done.2, f32[8,4,8,512]{3,2,1,0:T(8,128)} %copy-done.3, f32[8,4,4,512]{3,2,1,0:T(4,128)} %copy-done.6, ...), kind=kLoop, calls=%fused_computation.53 | loop fusion | flops 18677760 | bytes 24477936 | tf_op jit(solution)/shard_map/jit(_where)/select_n | solution.py:57
  307.4 8.8 %fusion.65 = f32[4,16,8,512]{3,2,1,0:T(8,128)S(1)} fusion(f32[4,16,8,512]{3,2,1,0:T(8,128)S(1)} %slice.465, f32[4,20,12,512]{3,2,1,0:T(8,128)} %fusion.21, f32[16,8,512]{2,1,0:T(8,128)S(1)} %bitcast.110), kind=kLoop, calls=%fused_computation.144 | loop fusion | flops 5505024 | bytes 10747904 | tf_op jit(solution)/shard_map/add | solution.py:66
  317.3 5.6 %all-to-all-start.2 = ((f32[4,16,8,512]{3,2,0,1:T(8,128)}), f32[4,16,8,512]{3,2,0,1:T(8,128)S(1)}, u32[]{:S(2)}, u32[]{:S(2)}) async-start(f32[4,16,8,512]{3,2,0,1:T(8,128)} %copy.47), calls=%async_computation.2 | async-start | bytes 2097152 | tf_op jit(solution)/shard_map/all_to_all | solution.py:143
  324.2 12.5 %all-to-all-done.2 = f32[4,16,8,512]{3,2,0,1:T(8,128)S(1)} async-done(((f32[4,16,8,512]{3,2,0,1:T(8,128)}), f32[4,16,8,512]{3,2,0,1:T(8,128)S(1)}, u32[]{:S(2)}, u32[]{:S(2)}) %all-to-all-start.2) | async-done | bytes 1048608 | tf_op jit(solution)/shard_map/all_to_all | solution.py:143
  336.7 5.6 %all-to-all-start.1 = ((f32[4,16,8,512]{3,2,0,1:T(8,128)}), f32[4,16,8,512]{3,2,0,1:T(8,128)S(1)}, u32[]{:S(2)}, u32[]{:S(2)}) async-start(f32[4,16,8,512]{3,2,0,1:T(8,128)} %copy.45), calls=%async_computation.1 | async-start | bytes 2097152 | tf_op jit(solution)/shard_map/all_to_all | solution.py:142
  342.5 13.7 %all-to-all-done.1 = f32[4,16,8,512]{3,2,0,1:T(8,128)S(1)} async-done(((f32[4,16,8,512]{3,2,0,1:T(8,128)}), f32[4,16,8,512]{3,2,0,1:T(8,128)S(1)}, u32[]{:S(2)}, u32[]{:S(2)}) %all-to-all-start.1) | async-done | bytes 1048608 | tf_op jit(solution)/shard_map/all_to_all | solution.py:142
  363.2 16.2 %gather_fusion = f32[4096,64]{1,0:T(8,128)} fusion(f32[64,8192]{0,1:T(8,128)} %bitcast.103, s32[4096]{0:T(1024)S(1)} %broadcast_clamp_fusion), kind=kCustom, calls=%fused_computation | custom fusion | bytes 2113536 | tf_op jit(solution)/shard_map/jit(_take)/gather | solution.py:152
  383.8 19.6 %all_to_all.75 = f32[8,1,32768]{2,1,0:T(1,128)S(1)} all-to-all(f32[8,1,32768]{2,1,0:T(1,128)} %reshape.1378), channel_id=1, replica_groups=mesh['zh'=4,'xl'=8,'gy'=16] {'xl'}, dimensions={0} | all-to-all | bytes 2097152 | tf_op jit(solution)/shard_map/all_to_all | solution.py:76
  410.9 47.8 %all_to_all.76 = f32[16,1,2048]{2,1,0:T(1,128)S(1)} all-to-all(f32[16,1,2048]{2,1,0:T(1,128)S(1)} %reshape.1380), channel_id=1, replica_groups=mesh['zh'=4,'xl'=8,'gy'=16] {'gy'}, dimensions={0} | all-to-all | bytes 262144 | tf_op jit(solution)/shard_map/all_to_all | solution.py:77
  459.8 32.2 %all_to_all.77 = f32[4,1,512]{2,1,0:T(1,128)S(1)} all-to-all(f32[4,1,512]{2,1,0:T(1,128)S(1)} %reshape.1382), channel_id=1, replica_groups=mesh['zh'=4,'xl'=8,'gy'=16] {'zh'}, dimensions={0} | all-to-all | bytes 16384 | tf_op jit(solution)/shard_map/all_to_all | solution.py:78
  493.4 8.0 %all_to_all.78 = f32[8,1,2048]{2,1,0:T(1,128)S(1)} all-to-all(f32[8,1,2048]{2,1,0:T(1,128)S(1)} %reshape.1384), channel_id=1, replica_groups=mesh['zh'=4,'xl'=8,'gy'=16] {'xl'}, dimensions={0} | all-to-all | bytes 131072 | tf_op jit(solution)/shard_map/all_to_all | solution.py:85
  502.7 11.2 %all_to_all.79 = f32[16,1,2048]{2,1,0:T(1,128)S(1)} all-to-all(f32[16,1,2048]{2,1,0:T(1,128)S(1)} %reshape.1386), channel_id=1, replica_groups=mesh['zh'=4,'xl'=8,'gy'=16] {'gy'}, dimensions={0} | all-to-all | bytes 262144 | tf_op jit(solution)/shard_map/all_to_all | solution.py:85
  520.6 11.1 %all-to-all-done.8 = f32[4,1,2048]{2,1,0:T(1,128)S(1)} async-done(((f32[4,1,2048]{2,1,0:T(1,128)}), f32[4,1,2048]{2,1,0:T(1,128)S(1)}, u32[]{:S(2)}, u32[]{:S(2)}) %all-to-all-start.8) | async-done | bytes 32800 | tf_op jit(solution)/shard_map/all_to_all | solution.py:85
  (145 shorter events, 78.7 us)
Async XLA Ops:
  3.9 26.0 %all-to-all-start = ((f32[40,2,8,512]{3,2,1,0:T(8,128)}), f32[40,2,8,512]{3,2,1,0:T(8,128)S(1)}, u32[]{:S(2)}, u32[]{:S(2)}) async-start(f32[40,2,8,512]{3,2,1,0:T(8,128)} %bitcast.1), calls=%async_computation | async-start | bytes 2621440 | tf_op jit(solution)/shard_map/all_to_all | solution.py:121
  31.2 91.9 %collective-permute-start.3 = (f32[5,16,4,512]{3,2,1,0:T(4,128)}, f32[5,16,4,512]{3,2,1,0:T(4,128)S(1)}, u32[]{:S(2)}, u32[]{:S(2)}) collective-permute-start(f32[5,16,4,512]{3,2,1,0:T(4,128)} %get-tuple-element.32), channel_id=1, source_target_pairs={{0,1},{1,2},{2,3},{3,4},{4,5},{5,6},{6,7},{7,8},{8,9},{9,10},{10,1... | collective-permute-start | bytes 1966088 | tf_op jit(solution)/shard_map/ppermute | solution.py:20
  32.6 90.6 %collective-permute-start.4 = (f32[5,16,4,512]{3,2,1,0:T(4,128)S(1)}, f32[5,16,4,512]{3,2,1,0:T(4,128)S(1)}, u32[]{:S(2)}, u32[]{:S(2)}) collective-permute-start(f32[5,16,4,512]{3,2,1,0:T(4,128)S(1)} %get-tuple-element.33), channel_id=1, source_target_pairs={{1,0},{2,1},{3,2},{4,3},{5,4},{6,5},{7,6},{8,7},{9,8},{10,9},{11,1... | collective-permute-start | bytes 1966088 | tf_op jit(solution)/shard_map/ppermute | solution.py:21
  34.7 15.7 %collective-permute-start = (f32[5,4,4,512]{3,2,1,0:T(4,128)}, f32[5,4,4,512]{3,2,1,0:T(4,128)S(1)}, u32[]{:S(2)}, u32[]{:S(2)}) collective-permute-start(f32[5,4,4,512]{3,2,1,0:T(4,128)} %get-tuple-element.26), channel_id=1, source_target_pairs={{0,129},{1,130},{2,131},{3,132},{4,133},{5,134},{6,135},{7,136},{8... | collective-permute-start | bytes 491528 | tf_op jit(solution)/shard_map/ppermute | solution.py:35
  43.9 28.1 %collective-permute-start.2 = (f32[5,4,4,512]{3,2,1,0:T(4,128)}, f32[5,4,4,512]{3,2,1,0:T(4,128)}, u32[]{:S(2)}, u32[]{:S(2)}) collective-permute-start(f32[5,4,4,512]{3,2,1,0:T(4,128)} %get-tuple-element.27), channel_id=1, source_target_pairs={{1,128},{2,129},{3,130},{4,131},{5,132},{6,133},{7,134},{8,135},{9... | collective-permute-start | bytes 491528 | tf_op jit(solution)/shard_map/ppermute | solution.py:35
  45.2 28.0 %collective-permute-start.5 = (f32[5,4,4,512]{3,2,1,0:T(4,128)}, f32[5,4,4,512]{3,2,1,0:T(4,128)S(1)}, u32[]{:S(2)}, u32[]{:S(2)}) collective-permute-start(f32[5,4,4,512]{3,2,1,0:T(4,128)} %get-tuple-element.28), channel_id=1, source_target_pairs={{128,1},{129,2},{130,3},{131,4},{132,5},{133,6},{134,7},{135,8},{1... | collective-permute-start | bytes 491528 | tf_op jit(solution)/shard_map/ppermute | solution.py:35
  50.5 72.7 %collective-permute-start.1 = (f32[5,4,8,512]{3,2,1,0:T(8,128)S(1)}, f32[5,4,8,512]{3,2,1,0:T(8,128)S(1)}, u32[]{:S(2)}, u32[]{:S(2)}) collective-permute-start(f32[5,4,8,512]{3,2,1,0:T(8,128)S(1)} %get-tuple-element.30), channel_id=1, source_target_pairs={{0,128},{128,256},{256,384},{1,129},{129,257},{257,385},{2,130},{1... | collective-permute-start | bytes 983048 | tf_op jit(solution)/shard_map/ppermute | solution.py:20
  72.0 51.2 %collective-permute-start.6 = (f32[5,4,8,512]{3,2,1,0:T(8,128)S(1)}, f32[5,4,8,512]{3,2,1,0:T(8,128)S(1)}, u32[]{:S(2)}, u32[]{:S(2)}) collective-permute-start(f32[5,4,8,512]{3,2,1,0:T(8,128)S(1)} %get-tuple-element.31), channel_id=1, source_target_pairs={{128,0},{256,128},{384,256},{129,1},{257,129},{385,257},{130,2},{2... | collective-permute-start | bytes 983048 | tf_op jit(solution)/shard_map/ppermute | solution.py:21
  73.3 49.9 %collective-permute-start.7 = (f32[5,4,4,512]{3,2,1,0:T(4,128)}, f32[5,4,4,512]{3,2,1,0:T(4,128)S(1)}, u32[]{:S(2)}, u32[]{:S(2)}) collective-permute-start(f32[5,4,4,512]{3,2,1,0:T(4,128)} %get-tuple-element.29), channel_id=1, source_target_pairs={{129,0},{130,1},{131,2},{132,3},{133,4},{134,5},{135,6},{136,7},{1... | collective-permute-start | bytes 491528 | tf_op jit(solution)/shard_map/ppermute | solution.py:35
  142.3 143.9 %copy-start = (f32[4,16,8,512]{3,2,1,0:T(8,128)}, f32[4,16,8,512]{3,2,1,0:T(8,128)S(1)}, u32[]{:S(2)}) copy-start(f32[4,16,8,512]{3,2,1,0:T(8,128)S(1)} %fusion.57) | copy-start | bytes 3145732
  142.8 143.3 %collective-permute-start.11 = (f32[8,16,4,512]{3,2,1,0:T(4,128)S(1)}, f32[8,16,4,512]{3,2,1,0:T(4,128)S(1)}, u32[]{:S(2)}, u32[]{:S(2)}) collective-permute-start(f32[8,16,4,512]{3,2,1,0:T(4,128)S(1)} %get-tuple-element.24), channel_id=1, source_target_pairs={{0,1},{1,2},{2,3},{3,4},{4,5},{5,6},{6,7},{7,8},{8,9},{9,10},{10,1... | collective-permute-start | bytes 3145736 | tf_op jit(solution)/shard_map/ppermute | solution.py:20
  151.8 134.4 %collective-permute-start.12 = (f32[8,16,4,512]{3,2,1,0:T(4,128)S(1)}, f32[8,16,4,512]{3,2,1,0:T(4,128)S(1)}, u32[]{:S(2)}, u32[]{:S(2)}) collective-permute-start(f32[8,16,4,512]{3,2,1,0:T(4,128)S(1)} %get-tuple-element.25), channel_id=1, source_target_pairs={{1,0},{2,1},{3,2},{4,3},{5,4},{6,5},{7,6},{8,7},{9,8},{10,9},{11,1... | collective-permute-start | bytes 3145736 | tf_op jit(solution)/shard_map/ppermute | solution.py:21
  153.3 2.8 collective-permute-start.10
  154.0 3.4 collective-permute-start.13
  154.6 81.8 %collective-permute-start.15 = (f32[8,4,4,512]{3,2,1,0:T(4,128)S(1)}, f32[8,4,4,512]{3,2,1,0:T(4,128)S(1)}, u32[]{:S(2)}, u32[]{:S(2)}) collective-permute-start(f32[8,4,4,512]{3,2,1,0:T(4,128)S(1)} %get-tuple-element.21), channel_id=1, source_target_pairs={{129,0},{130,1},{131,2},{132,3},{133,4},{134,5},{135,6},{136,7},{1... | collective-permute-start | bytes 786440 | tf_op jit(solution)/shard_map/ppermute | solution.py:35
  156.0 131.7 %copy-start.5 = (f32[8,4,4,512]{3,2,1,0:T(4,128)}, f32[8,4,4,512]{3,2,1,0:T(4,128)S(1)}, u32[]{:S(2)}) copy-start(f32[8,4,4,512]{3,2,1,0:T(4,128)S(1)} %collective-permute-done.10) | copy-start | bytes 786436
  156.0 130.1 %collective-permute-start.14 = (f32[8,4,8,512]{3,2,1,0:T(8,128)S(1)}, f32[8,4,8,512]{3,2,1,0:T(8,128)S(1)}, u32[]{:S(2)}, u32[]{:S(2)}) collective-permute-start(f32[8,4,8,512]{3,2,1,0:T(8,128)S(1)} %get-tuple-element.23), channel_id=1, source_target_pairs={{128,0},{256,128},{384,256},{129,1},{257,129},{385,257},{130,2},{2... | collective-permute-start | bytes 1572872 | tf_op jit(solution)/shard_map/ppermute | solution.py:21
  157.4 130.4 %copy-start.6 = (f32[8,4,4,512]{3,2,1,0:T(4,128)}, f32[8,4,4,512]{3,2,1,0:T(4,128)S(1)}, u32[]{:S(2)}) copy-start(f32[8,4,4,512]{3,2,1,0:T(4,128)S(1)} %collective-permute-done.13) | copy-start | bytes 786436
  157.4 128.8 %collective-permute-start.9 = (f32[8,4,8,512]{3,2,1,0:T(8,128)S(1)}, f32[8,4,8,512]{3,2,1,0:T(8,128)S(1)}, u32[]{:S(2)}, u32[]{:S(2)}) collective-permute-start(f32[8,4,8,512]{3,2,1,0:T(8,128)S(1)} %get-tuple-element.22), channel_id=1, source_target_pairs={{0,128},{128,256},{256,384},{1,129},{129,257},{257,385},{2,130},{1... | collective-permute-start | bytes 1572872 | tf_op jit(solution)/shard_map/ppermute | solution.py:20
  236.4 51.3 %copy-start.7 = (f32[8,4,4,512]{3,2,1,0:T(4,128)}, f32[8,4,4,512]{3,2,1,0:T(4,128)S(1)}, u32[]{:S(2)}) copy-start(f32[8,4,4,512]{3,2,1,0:T(4,128)S(1)} %collective-permute-done.15) | copy-start | bytes 786436
  236.4 49.7 %collective-permute-start.8 = (f32[8,4,4,512]{3,2,1,0:T(4,128)S(1)}, f32[8,4,4,512]{3,2,1,0:T(4,128)S(1)}, u32[]{:S(2)}, u32[]{:S(2)}) collective-permute-start(f32[8,4,4,512]{3,2,1,0:T(4,128)S(1)} %get-tuple-element.18), channel_id=1, source_target_pairs={{0,129},{1,130},{2,131},{3,132},{4,133},{5,134},{6,135},{7,136},{8... | collective-permute-start | bytes 786440 | tf_op jit(solution)/shard_map/ppermute | solution.py:35
  317.3 19.4 %all-to-all-start.2 = ((f32[4,16,8,512]{3,2,0,1:T(8,128)}), f32[4,16,8,512]{3,2,0,1:T(8,128)S(1)}, u32[]{:S(2)}, u32[]{:S(2)}) async-start(f32[4,16,8,512]{3,2,0,1:T(8,128)} %copy.47), calls=%async_computation.2 | async-start | bytes 2097152 | tf_op jit(solution)/shard_map/all_to_all | solution.py:143
  336.7 19.5 %all-to-all-start.1 = ((f32[4,16,8,512]{3,2,0,1:T(8,128)}), f32[4,16,8,512]{3,2,0,1:T(8,128)S(1)}, u32[]{:S(2)}, u32[]{:S(2)}) async-start(f32[4,16,8,512]{3,2,0,1:T(8,128)} %copy.45), calls=%async_computation.1 | async-start | bytes 2097152 | tf_op jit(solution)/shard_map/all_to_all | solution.py:142
  515.8 15.9 %all-to-all-start.8 = ((f32[4,1,2048]{2,1,0:T(1,128)}), f32[4,1,2048]{2,1,0:T(1,128)S(1)}, u32[]{:S(2)}, u32[]{:S(2)}) async-start(f32[4,1,2048]{2,1,0:T(1,128)} %reshape.1388), calls=%async_computation.8 | async-start | bytes 65536 | tf_op jit(solution)/shard_map/all_to_all | solution.py:85
  (7 other events, 21.6 us)

commit v5 on v3

--- a/solution.py
+++ b/solution.py
@@ -71,11 +71,18 @@
 def shards(orbitals, potential, sign_bits, sampled_rows):
     chunks = lax.axis_size("xl")
     count = orbitals.shape[0]
-    rows = orbitals.reshape((chunks, count // chunks) + orbitals.shape[1:])
-    extra = jnp.broadcast_to(potential[None, None], (chunks, 1) + potential.shape)
+    own = count // chunks
+    cells = orbitals.shape[1] * orbitals.shape[2] * orbitals.shape[3]
+    sign_block = (2 * sign_bits - 1).astype(jnp.float32)
+    picks = sampled_rows.reshape(potential.shape).astype(jnp.float32)
+    rows = orbitals.reshape((chunks, own) + orbitals.shape[1:])
+    extra = jnp.broadcast_to(
+        jnp.stack([potential, sign_block, picks])[None], (chunks, 3) + potential.shape
+    )
     both = jnp.concatenate([rows, extra], axis=1).reshape((-1,) + orbitals.shape[1:])
     both = lax.all_to_all(both, "xl", 0, 1, tiled=True)
-    spread, group_potential = both[: count // chunks], both[count // chunks]
+    spread, group_potential, group_sign = both[:own], both[own], both[own + 1]
+    group_picks = both[own + 2].reshape(chunks, cells)[:, :M].astype(jnp.int32)
     first = (apply_ham(spread, group_potential) - filter_center * spread) / filter_half
     second = 2.0 * (apply_ham(first, group_potential) - filter_center * first) / filter_half - spread
     spread_filtered = (
@@ -83,19 +90,25 @@
     )
     spread_applied = apply_ham(spread_filtered, group_potential)
     filtered = lax.all_to_all(spread_filtered, "xl", 1, 0, tiled=True)
-    applied = lax.all_to_all(spread_applied, "xl", 1, 0, tiled=True)
-    count = orbitals.shape[0]
-    cells = orbitals.shape[1] * orbitals.shape[2] * orbitals.shape[3]
-    stacked = jnp.concatenate([filtered, applied], axis=0)
-    sign_block = (2 * sign_bits - 1).astype(jnp.float32)
-    flat = (stacked * sign_block[None]).reshape(2 * count, -1, 128)
+
+    fields = jnp.concatenate([spread_filtered, spread_applied], axis=0) * group_sign[None]
+    flat = fields.reshape((2 * own, chunks, cells)).transpose(1, 0, 2).reshape(-1, cells // 128, 128)
     mixed = jnp.einsum("nac,cd->nad", flat, hadamard_table(128), precision=HIGHEST)
     mixed = jnp.einsum("ba,nac->nbc", hadamard_table(cells // 128), mixed, precision=HIGHEST)
-    mixed = mixed.reshape(2 * count, cells)
-    picked = jnp.take(mixed, sampled_rows[0, 0, :M], axis=1)
-    devices = lax.axis_size("zh") * lax.axis_size("xl") * lax.axis_size("gy")
-    term = (picked / jnp.sqrt(jnp.float32(M * devices))).reshape(2, count, M)
-    share = exchange_scatter(term.reshape(2 * count, M)).reshape(2, count, -1)
+    mixed = mixed.reshape(chunks, 2 * own, cells)
+    index = jnp.broadcast_to(group_picks[:, None, :], (chunks, 2 * own, M))
+    picked = jnp.take_along_axis(mixed, index, axis=2).sum(0)
+    devices = lax.axis_size("zh") * chunks * lax.axis_size("gy")
+    term = picked / jnp.sqrt(jnp.float32(M * devices))
+
+    zh, gy = lax.axis_size("zh"), lax.axis_size("gy")
+    term = term.reshape(2 * own, zh, chunks, gy, -1).transpose(2, 0, 1, 3, 4)
+    term = lax.all_to_all(term, "xl", 0, 0, tiled=True)
+    term = term.reshape((chunks, 2, own) + term.shape[2:]).transpose(1, 0, 2, 3, 4, 5)
+    term = term.reshape(2 * count, zh, gy, -1).transpose(0, 2, 1, 3)
+    term = lax.all_to_all(term, "gy", 1, 1, tiled=True).sum(1)
+    term = lax.all_to_all(term, "zh", 1, 1, tiled=True).sum(1)
+    share = term.reshape(2, count, -1)
     part_gram = jnp.dot(share[0], share[0].T, precision=HIGHEST)
     part_cross = jnp.dot(share[0], share[1].T, precision=HIGHEST)
     parts = exchange_sum(jnp.stack([part_gram, part_cross])) / cells

time: 333 us -> 3440 us (10.33)
  local copies, waits for them, and re-layouts: 37.2 us -> 3160 us
    gather x1 -> x2, local copies, waits for them, and re-layouts: 16.4 us -> 3140 us  [shards(): picked = jnp.take_along_axis(mixed, index, axis=2).sum(0)]
  transfers between devices with their start and end apart: 20 -> 20, of which waited for: 11 -> 13; matrix products, arithmetic and copies ran while one was open for 2% -> 0% of each run, Pallas kernels for 0% -> 0%
where the time goes in v5:
time: 3440 us
  local copies, waits for them, and re-layouts  3160 us (92%)
  waiting for transfers between devices  90.2 us (3%)
  starting transfers between devices  87.4 us (3%)
  blocking collectives  58.3 us (2%)
    gather x2, local copies, waits for them, and re-layouts, shards(): picked = jnp.take_along_axis(mixed, index, axis=2).sum(0)  3140 us
  transfers between devices with their start and end apart: 20, of which 13 were waited for; matrix products, arithmetic and copies ran while one was open for 0% of the time, Pallas kernels for 0%

profile of v5, /device:TPU:6, one launch (start us, length us, event | category | flops | bytes accessed | tf_op | source)
XLA Modules:
  0.0 3438.6 jit_solution(6545561577842527801)
XLA Ops:
  5.8 9.4 all-to-all-start
  18.0 19.5 all-to-all-done
  40.6 7.1 collective-permute-start
  50.2 11.4 collective-permute-done.1
  64.2 10.5 collective-permute-start.6
  76.0 7.7 collective-permute-start.4
  86.2 8.3 collective-permute-done.5
  97.1 11.6 collective-permute-start.10
  115.2 8.5 collective-permute-done.9
  128.0 8.8 collective-permute-start.14
  138.8 5.6 collective-permute-start.12
  149.6 6.2 collective-permute-done.13
  158.5 3.7 fusion.9
  169.9 3.4 convolution_bitcast_fusion
  175.1 3134.5 %gather_fusion = f32[262144]{0:T(1024)} fusion(f32[8,8,8192]{2,1,0:T(8,128)S(1)} %reshape.1309, s32[262144]{0:T(1024)S(1)} %bitcast.104), kind=kCustom, calls=%fused_computation | custom fusion | bytes 5242880 | tf_op jit(solution)/shard_map/jit(take_along_axis)/gather | solution.py:100
  3313.5 8.5 all_to_all.60
  3324.8 24.0 all_to_all.61
  3350.1 17.8 all_to_all.62
  3369.3 8.0 all_to_all.63
  3379.2 3.5 all-to-all-start.5
  3383.8 7.3 all-to-all-done.5
  3391.1 5.6 all-to-all-start.7
  3398.6 11.9 all-to-all-done.7
  3415.4 11.0 all-to-all-done.6
  (162 shorter events, 83.4 us)
Async XLA Ops:
  5.8 31.7 all-to-all-start
  38.0 23.6 collective-permute-start.2
  39.3 22.3 collective-permute-start.3
  40.6 9.6 collective-permute-start
  47.7 13.9 collective-permute-start.1
  49.1 96.8 %copy-start.2 = (s32[8,4096]{1,0:T(8,128)}, s32[8,4096]{1,0:T(8,128)S(1)}, u32[]{:S(2)}) copy-start(s32[8,4096]{1,0:T(8,128)S(1)} %broadcast_add_fusion) | copy-start | bytes 393220
  49.2 96.8 %copy-start.4 = (s32[8,4096]{1,0:T(8,128)}, s32[8,4096]{1,0:T(8,128)S(1)}, u32[]{:S(2)}) copy-start(s32[8,4096]{1,0:T(8,128)S(1)} %slice_convert_fusion) | copy-start | bytes 393220
  64.2 30.3 collective-permute-start.6
  74.6 19.8 collective-permute-start.7
  76.0 10.2 collective-permute-start.4
  83.7 10.8 collective-permute-start.5
  97.1 26.6 collective-permute-start.10
  108.7 15.8 collective-permute-start.11
  110.0 5.2 collective-permute-start.8
  112.6 11.0 collective-permute-start.9
  114.0 32.0 copy-start.7
  128.0 27.8 collective-permute-start.14
  136.8 21.7 collective-permute-start.15
  138.8 10.7 collective-permute-start.12
  144.5 11.3 collective-permute-start.13
  3348.8 33.9 copy-start.1
  3379.2 11.9 all-to-all-start.5
  3391.1 19.4 all-to-all-start.7
  3410.6 15.9 all-to-all-start.6
  (14 other events, 50.5 us)

commit v6 on v3

--- a/solution.py
+++ b/solution.py
@@ -31,11 +31,11 @@
     y = x.reshape(n, zh, xl, gy, -1).transpose(0, 2, 1, 3, 4)
     y = lax.all_to_all(y, "xl", 1, 1, tiled=True).sum(1)
     y = lax.all_to_all(y.transpose(0, 2, 1, 3), "gy", 1, 1, tiled=True).sum(1)
-    return lax.all_to_all(y, "zh", 1, 1, tiled=True).sum(1)
+    return exchange_sum(y, ("zh",))
 
 
-def exchange_sum(x):
-    for axis in ("xl", "gy", "zh"):
+def exchange_sum(x, axes):
+    for axis in axes:
         size = lax.axis_size(axis)
         copies = jnp.broadcast_to(x[None], (size,) + x.shape)
         x = lax.all_to_all(copies, axis, 0, 0, tiled=True).sum(0)
@@ -95,10 +95,13 @@
     picked = jnp.take(mixed, sampled_rows[0, 0, :M], axis=1)
     devices = lax.axis_size("zh") * lax.axis_size("xl") * lax.axis_size("gy")
     term = (picked / jnp.sqrt(jnp.float32(M * devices))).reshape(2, count, M)
-    share = exchange_scatter(term.reshape(2 * count, M)).reshape(2, count, -1)
-    part_gram = jnp.dot(share[0], share[0].T, precision=HIGHEST)
-    part_cross = jnp.dot(share[0], share[1].T, precision=HIGHEST)
-    parts = exchange_sum(jnp.stack([part_gram, part_cross])) / cells
+    summed = exchange_scatter(term.reshape(2 * count, M))
+    share = lax.dynamic_index_in_dim(summed, lax.axis_index("zh"), 1, keepdims=False)
+    share = share.reshape(2, count, -1)
+    both = summed.reshape(2, count, -1)
+    part_gram = jnp.dot(both[0], both[0].T, precision=HIGHEST)
+    part_cross = jnp.dot(both[0], both[1].T, precision=HIGHEST)
+    parts = exchange_sum(jnp.stack([part_gram, part_cross]), ("xl", "gy")) / cells
     gram, cross = parts[0], parts[1]
     lower = jnp.linalg.cholesky(gram)
     inverse = lax.linalg.triangular_solve(

time: 333 us -> 318 us (0.955)
  blocking collectives: 83.7 us -> 72.6 us
  waiting for transfers between devices: 82.2 us -> 77.9 us
    all_to_all x1 -> x0, blocking collectives: 17.1 us -> none  [exchange_scatter(): return lax.all_to_all(y, 'zh', 1, 1, tiled=True).sum(1)]
    all_to_all x2, blocking collectives: 19.2 us -> 25.3 us  [exchange_sum(): x = lax.all_to_all(copies, axis, 0, 0, tiled=True).sum(0)]
    all_to_all x1, waiting for transfers between devices: 11.1 us -> 6.82 us  [exchange_sum(): x = lax.all_to_all(copies, axis, 0, 0, tiled=True).sum(0)]
    unnamed x28 -> x27, local copies, waits for them, and re-layouts: 9 us -> 8.87 us
  transfers between devices with their start and end apart: 20 -> 20, of which waited for: 11 -> 12; matrix products, arithmetic and copies ran while one was open for 2% -> 3% of each run, Pallas kernels for 0% -> 0%
where the time goes in v6:
time: 318 us; the launch traced here: 315 us
  starting transfers between devices  88.7 us (28%)
  waiting for transfers between devices  77.9 us (24%)
  blocking collectives  72.6 us (23%)
  local copies, waits for them, and re-layouts  37.1 us (12%)
  other arithmetic  31.3 us (10%)
  matrix products  6.6 us (2%)
    ppermute x8, starting transfers between devices, halos(): before = lax.ppermute(last, axis, up)  55.1 us
    ppermute x8, waiting for transfers between devices, halos(): after = lax.ppermute(initial, axis, down)  37.6 us
    all_to_all x1, blocking collectives, exchange_scatter(): y = lax.all_to_all(y.transpose(0, 2, 1, 3), 'gy', 1, 1, tiled=True).sum(1)  27.8 us
    all_to_all x2, blocking collectives, exchange_sum(): x = lax.all_to_all(copies, axis, 0, 0, tiled=True).sum(0)  25.3 us
    all_to_all x1, blocking collectives, exchange_scatter(): y = lax.all_to_all(y, 'xl', 1, 1, tiled=True).sum(1)  19.6 us
    all_to_all x1, waiting for transfers between devices, shards(): both = lax.all_to_all(both, 'xl', 0, 1, tiled=True)  16.6 us
    gather x1, local copies, waits for them, and re-layouts, shards(): picked = jnp.take(mixed, sampled_rows[0, 0, :M], axis=1)  16.4 us
    all_to_all x1, waiting for transfers between devices, shards(): applied = lax.all_to_all(spread_applied, 'xl', 1, 0, tiled=True)  13.7 us
  transfers between devices with their start and end apart: 20, of which 12 were waited for; matrix products, arithmetic and copies ran while one was open for 3% of the time, Pallas kernels for 0%

profile of v6, /device:TPU:6, one launch (start us, length us, event | category | flops | bytes accessed | tf_op | source)
XLA Modules:
  0.0 315.4 jit_solution(15206069789198123035)
XLA Ops:
  3.9 9.4 %all-to-all-start = ((f32[40,2,8,512]{3,2,1,0:T(8,128)}), f32[40,2,8,512]{3,2,1,0:T(8,128)S(1)}, u32[]{:S(2)}, u32[]{:S(2)}) async-start(f32[40,2,8,512]{3,2,1,0:T(8,128)} %bitcast.1), calls=%async_computation | async-start | bytes 2621440 | tf_op jit(solution)/shard_map/all_to_all | solution.py:77
  13.3 16.6 %all-to-all-done = f32[40,2,8,512]{3,2,1,0:T(8,128)S(1)} async-done(((f32[40,2,8,512]{3,2,1,0:T(8,128)}), f32[40,2,8,512]{3,2,1,0:T(8,128)S(1)}, u32[]{:S(2)}, u32[]{:S(2)}) %all-to-all-start) | async-done | bytes 1310752 | tf_op jit(solution)/shard_map/all_to_all | solution.py:77
  32.9 7.1 %collective-permute-start = (f32[4,2,8,512]{3,2,1,0:T(8,128)S(1)}, f32[4,2,8,512]{3,2,1,0:T(8,128)S(1)}, u32[]{:S(2)}, u32[]{:S(2)}) collective-permute-start(f32[4,2,8,512]{3,2,1,0:T(8,128)S(1)} %get-tuple-element.32), channel_id=1, source_target_pairs={{0,128},{128,256},{256,384},{1,129},{129,257},{257,385},{2,130},{1... | collective-permute-start | bytes 393224 | tf_op jit(solution)/shard_map/ppermute | solution.py:20
  42.5 11.5 %collective-permute-done.1 = f32[4,2,8,512]{3,2,1,0:T(8,128)S(1)} collective-permute-done((f32[4,2,8,512]{3,2,1,0:T(8,128)S(1)}, f32[4,2,8,512]{3,2,1,0:T(8,128)S(1)}, u32[]{:S(2)}, u32[]{:S(2)}) %collective-permute-start.1) | collective-permute-done | bytes 131104 | tf_op jit(solution)/shard_map/ppermute | solution.py:21
  56.6 10.4 %collective-permute-start.6 = (f32[4,16,2,512]{3,2,1,0:T(2,128)S(1)}, f32[4,16,2,512]{3,2,1,0:T(2,128)S(1)}, u32[]{:S(2)}, u32[]{:S(2)}) collective-permute-start(f32[4,16,2,512]{3,2,1,0:T(2,128)S(1)} %get-tuple-element.28), channel_id=1, source_target_pairs={{0,1},{1,2},{2,3},{3,4},{4,5},{5,6},{6,7},{7,8},{8,9},{9,10},{10,1... | collective-permute-start | bytes 786440 | tf_op jit(solution)/shard_map/ppermute | solution.py:20
  68.3 7.7 %collective-permute-start.4 = (f32[4,2,8,512]{3,2,1,0:T(8,128)S(1)}, f32[4,2,8,512]{3,2,1,0:T(8,128)S(1)}, u32[]{:S(2)}, u32[]{:S(2)}) collective-permute-start(f32[4,2,8,512]{3,2,1,0:T(8,128)S(1)} %get-tuple-element.30), channel_id=1, source_target_pairs={{0,128},{128,256},{256,384},{1,129},{129,257},{257,385},{2,130},{1... | collective-permute-start | bytes 393224 | tf_op jit(solution)/shard_map/ppermute | solution.py:20
  78.5 8.3 %collective-permute-done.5 = f32[4,2,8,512]{3,2,1,0:T(8,128)S(1)} collective-permute-done((f32[4,2,8,512]{3,2,1,0:T(8,128)S(1)}, f32[4,2,8,512]{3,2,1,0:T(8,128)S(1)}, u32[]{:S(2)}, u32[]{:S(2)}) %collective-permute-start.5) | collective-permute-done | bytes 131104 | tf_op jit(solution)/shard_map/ppermute | solution.py:21
  89.4 11.6 %collective-permute-start.10 = (f32[4,16,2,512]{3,2,1,0:T(2,128)S(1)}, f32[4,16,2,512]{3,2,1,0:T(2,128)S(1)}, u32[]{:S(2)}, u32[]{:S(2)}) collective-permute-start(f32[4,16,2,512]{3,2,1,0:T(2,128)S(1)} %get-tuple-element.24), channel_id=1, source_target_pairs={{0,1},{1,2},{2,3},{3,4},{4,5},{5,6},{6,7},{7,8},{8,9},{9,10},{10,1... | collective-permute-start | bytes 786440 | tf_op jit(solution)/shard_map/ppermute | solution.py:20
  107.5 8.5 %collective-permute-done.9 = f32[4,2,8,512]{3,2,1,0:T(8,128)S(1)} collective-permute-done((f32[4,2,8,512]{3,2,1,0:T(8,128)S(1)}, f32[4,2,8,512]{3,2,1,0:T(8,128)S(1)}, u32[]{:S(2)}, u32[]{:S(2)}) %collective-permute-start.9) | collective-permute-done | bytes 131104 | tf_op jit(solution)/shard_map/ppermute | solution.py:21
  120.5 8.1 %collective-permute-start.14 = (f32[4,16,2,512]{3,2,1,0:T(2,128)S(1)}, f32[4,16,2,512]{3,2,1,0:T(2,128)S(1)}, u32[]{:S(2)}, u32[]{:S(2)}) collective-permute-start(f32[4,16,2,512]{3,2,1,0:T(2,128)S(1)} %get-tuple-element.20), channel_id=1, source_target_pairs={{0,1},{1,2},{2,3},{3,4},{4,5},{5,6},{6,7},{7,8},{8,9},{9,10},{10,1... | collective-permute-start | bytes 786440 | tf_op jit(solution)/shard_map/ppermute | solution.py:20
  129.9 5.6 %all-to-all-start.1 = ((f32[4,16,8,512]{3,2,0,1:T(8,128)}), f32[4,16,8,512]{3,2,0,1:T(8,128)S(1)}, u32[]{:S(2)}, u32[]{:S(2)}) async-start(f32[4,16,8,512]{3,2,0,1:T(8,128)} %copy.45), calls=%async_computation.1 | async-start | bytes 2097152 | tf_op jit(solution)/shard_map/all_to_all | solution.py:85
  136.2 6.3 %collective-permute-start.12 = (f32[4,2,8,512]{3,2,1,0:T(8,128)}, f32[4,2,8,512]{3,2,1,0:T(8,128)}, u32[]{:S(2)}, u32[]{:S(2)}) collective-permute-start(f32[4,2,8,512]{3,2,1,0:T(8,128)} %get-tuple-element.22), channel_id=1, source_target_pairs={{0,128},{128,256},{256,384},{1,129},{129,257},{257,385},{2,130},{1... | collective-permute-start | bytes 393224 | tf_op jit(solution)/shard_map/ppermute | solution.py:20
  145.2 8.7 %collective-permute-done.13 = f32[4,2,8,512]{3,2,1,0:T(8,128)} collective-permute-done((f32[4,2,8,512]{3,2,1,0:T(8,128)}, f32[4,2,8,512]{3,2,1,0:T(8,128)}, u32[]{:S(2)}, u32[]{:S(2)}) %collective-permute-start.13) | collective-permute-done | bytes 131104 | tf_op jit(solution)/shard_map/ppermute | solution.py:21
  157.6 4.8 %all-to-all-start.2 = ((f32[4,16,8,512]{3,2,0,1:T(8,128)}), f32[4,16,8,512]{3,2,0,1:T(8,128)S(1)}, u32[]{:S(2)}, u32[]{:S(2)}) async-start(f32[4,16,8,512]{3,2,0,1:T(8,128)} %copy.47), calls=%async_computation.2 | async-start | bytes 2097152 | tf_op jit(solution)/shard_map/all_to_all | solution.py:86
  162.6 13.7 %all-to-all-done.2 = f32[4,16,8,512]{3,2,0,1:T(8,128)S(1)} async-done(((f32[4,16,8,512]{3,2,0,1:T(8,128)}), f32[4,16,8,512]{3,2,0,1:T(8,128)S(1)}, u32[]{:S(2)}, u32[]{:S(2)}) %all-to-all-start.2) | async-done | bytes 1048608 | tf_op jit(solution)/shard_map/all_to_all | solution.py:86
  185.5 16.4 %gather_fusion = f32[4096,64]{1,0:T(8,128)} fusion(f32[64,8192]{0,1:T(8,128)} %bitcast.98, s32[4096]{0:T(1024)S(1)} %broadcast_clamp_fusion), kind=kCustom, calls=%fused_computation | custom fusion | bytes 2113536 | tf_op jit(solution)/shard_map/jit(_take)/gather | solution.py:95
  206.3 19.6 %all_to_all.70 = f32[8,1,32768]{2,1,0:T(1,128)S(1)} all-to-all(f32[8,1,32768]{2,1,0:T(1,128)} %reshape.1339), channel_id=1, replica_groups=mesh['zh'=4,'xl'=8,'gy'=16] {'xl'}, dimensions={0} | all-to-all | bytes 2097152 | tf_op jit(solution)/shard_map/all_to_all | solution.py:32
  226.4 4.5 %reduce.10 = f32[8,32768]{1,0:T(8,128)} reduce(f32[8,1,32768]{2,1,0:T(1,128)S(1)} %all_to_all.70, f32[]{:T(128)} %broadcast.1731), dimensions={1}, to_apply=%all_to_all.57.reduce_sub_computation | reduce | bytes 2097156 | tf_op jit(solution)/shard_map/all_to_all | solution.py:32
  233.4 27.8 %all_to_all.71 = f32[16,1,2048]{2,1,0:T(1,128)S(1)} all-to-all(f32[16,1,2048]{2,1,0:T(1,128)S(1)} %reshape.1341), channel_id=1, replica_groups=mesh['zh'=4,'xl'=8,'gy'=16] {'gy'}, dimensions={0} | all-to-all | bytes 262144 | tf_op jit(solution)/shard_map/all_to_all | solution.py:33
  262.4 17.3 %all_to_all.72 = f32[4,1,2048]{2,1,0:T(1,128)S(1)} all-to-all(f32[4,1,2048]{2,1,0:T(1,128)S(1)} %reshape.1343), channel_id=1, replica_groups=mesh['zh'=4,'xl'=8,'gy'=16] {'zh'}, dimensions={0} | all-to-all | bytes 65536 | tf_op jit(solution)/shard_map/all_to_all | solution.py:41
  281.2 8.0 %all_to_all.73 = f32[8,1,2048]{2,1,0:T(1,128)S(1)} all-to-all(f32[8,1,2048]{2,1,0:T(1,128)S(1)} %reshape.1345), channel_id=1, replica_groups=mesh['zh'=4,'xl'=8,'gy'=16] {'xl'}, dimensions={0} | all-to-all | bytes 131072 | tf_op jit(solution)/shard_map/all_to_all | solution.py:41
  291.1 3.5 %all-to-all-start.7 = ((f32[16,1,2048]{2,1,0:T(1,128)}), f32[16,1,2048]{2,1,0:T(1,128)S(1)}, u32[]{:S(2)}, u32[]{:S(2)}) async-start(f32[16,1,2048]{2,1,0:T(1,128)} %reshape.1347), calls=%async_computation.7 | async-start | bytes 262144 | tf_op jit(solution)/shard_map/all_to_all | solution.py:41
  296.1 6.8 %all-to-all-done.7 = f32[16,1,2048]{2,1,0:T(1,128)S(1)} async-done(((f32[16,1,2048]{2,1,0:T(1,128)}), f32[16,1,2048]{2,1,0:T(1,128)S(1)}, u32[]{:S(2)}, u32[]{:S(2)}) %all-to-all-start.7) | async-done | bytes 131104 | tf_op jit(solution)/shard_map/all_to_all | solution.py:41
  304.3 2.9 cholesky.17
  (124 shorter events, 69.3 us)
Async XLA Ops:
  1.4 11.9 %copy-start.1 = (s32[2,8,512]{2,1,0:T(8,128)S(1)}, s32[2,8,512]{2,1,0:T(8,128)}, u32[]{:S(2)}) copy-start(s32[2,8,512]{2,1,0:T(8,128)} %param.6) | copy-start | bytes 98308
  3.9 26.0 %all-to-all-start = ((f32[40,2,8,512]{3,2,1,0:T(8,128)}), f32[40,2,8,512]{3,2,1,0:T(8,128)S(1)}, u32[]{:S(2)}, u32[]{:S(2)}) async-start(f32[40,2,8,512]{3,2,1,0:T(8,128)} %bitcast.1), calls=%async_computation | async-start | bytes 2621440 | tf_op jit(solution)/shard_map/all_to_all | solution.py:77
  30.3 23.7 %collective-permute-start.2 = (f32[4,16,2,512]{3,2,1,0:T(2,128)S(1)}, f32[4,16,2,512]{3,2,1,0:T(2,128)S(1)}, u32[]{:S(2)}, u32[]{:S(2)}) collective-permute-start(f32[4,16,2,512]{3,2,1,0:T(2,128)S(1)} %get-tuple-element.34), channel_id=1, source_target_pairs={{0,1},{1,2},{2,3},{3,4},{4,5},{5,6},{6,7},{7,8},{8,9},{9,10},{10,1... | collective-permute-start | bytes 786440 | tf_op jit(solution)/shard_map/ppermute | solution.py:20
  31.6 22.4 %collective-permute-start.3 = (f32[4,16,2,512]{3,2,1,0:T(2,128)S(1)}, f32[4,16,2,512]{3,2,1,0:T(2,128)S(1)}, u32[]{:S(2)}, u32[]{:S(2)}) collective-permute-start(f32[4,16,2,512]{3,2,1,0:T(2,128)S(1)} %get-tuple-element.35), channel_id=1, source_target_pairs={{1,0},{2,1},{3,2},{4,3},{5,4},{6,5},{7,6},{8,7},{9,8},{10,9},{11,1... | collective-permute-start | bytes 786440 | tf_op jit(solution)/shard_map/ppermute | solution.py:21
  32.9 9.6 %collective-permute-start = (f32[4,2,8,512]{3,2,1,0:T(8,128)S(1)}, f32[4,2,8,512]{3,2,1,0:T(8,128)S(1)}, u32[]{:S(2)}, u32[]{:S(2)}) collective-permute-start(f32[4,2,8,512]{3,2,1,0:T(8,128)S(1)} %get-tuple-element.32), channel_id=1, source_target_pairs={{0,128},{128,256},{256,384},{1,129},{129,257},{257,385},{2,130},{1... | collective-permute-start | bytes 393224 | tf_op jit(solution)/shard_map/ppermute | solution.py:20
  40.0 13.9 %collective-permute-start.1 = (f32[4,2,8,512]{3,2,1,0:T(8,128)S(1)}, f32[4,2,8,512]{3,2,1,0:T(8,128)S(1)}, u32[]{:S(2)}, u32[]{:S(2)}) collective-permute-start(f32[4,2,8,512]{3,2,1,0:T(8,128)S(1)} %get-tuple-element.33), channel_id=1, source_target_pairs={{128,0},{256,128},{384,256},{129,1},{257,129},{385,257},{130,2},{2... | collective-permute-start | bytes 393224 | tf_op jit(solution)/shard_map/ppermute | solution.py:21
  56.6 30.2 %collective-permute-start.6 = (f32[4,16,2,512]{3,2,1,0:T(2,128)S(1)}, f32[4,16,2,512]{3,2,1,0:T(2,128)S(1)}, u32[]{:S(2)}, u32[]{:S(2)}) collective-permute-start(f32[4,16,2,512]{3,2,1,0:T(2,128)S(1)} %get-tuple-element.28), channel_id=1, source_target_pairs={{0,1},{1,2},{2,3},{3,4},{4,5},{5,6},{6,7},{7,8},{8,9},{9,10},{10,1... | collective-permute-start | bytes 786440 | tf_op jit(solution)/shard_map/ppermute | solution.py:20
  67.0 19.8 %collective-permute-start.7 = (f32[4,16,2,512]{3,2,1,0:T(2,128)S(1)}, f32[4,16,2,512]{3,2,1,0:T(2,128)S(1)}, u32[]{:S(2)}, u32[]{:S(2)}) collective-permute-start(f32[4,16,2,512]{3,2,1,0:T(2,128)S(1)} %get-tuple-element.29), channel_id=1, source_target_pairs={{1,0},{2,1},{3,2},{4,3},{5,4},{6,5},{7,6},{8,7},{9,8},{10,9},{11,1... | collective-permute-start | bytes 786440 | tf_op jit(solution)/shard_map/ppermute | solution.py:21
  68.3 10.2 %collective-permute-start.4 = (f32[4,2,8,512]{3,2,1,0:T(8,128)S(1)}, f32[4,2,8,512]{3,2,1,0:T(8,128)S(1)}, u32[]{:S(2)}, u32[]{:S(2)}) collective-permute-start(f32[4,2,8,512]{3,2,1,0:T(8,128)S(1)} %get-tuple-element.30), channel_id=1, source_target_pairs={{0,128},{128,256},{256,384},{1,129},{129,257},{257,385},{2,130},{1... | collective-permute-start | bytes 393224 | tf_op jit(solution)/shard_map/ppermute | solution.py:20
  76.0 10.8 %collective-permute-start.5 = (f32[4,2,8,512]{3,2,1,0:T(8,128)S(1)}, f32[4,2,8,512]{3,2,1,0:T(8,128)S(1)}, u32[]{:S(2)}, u32[]{:S(2)}) collective-permute-start(f32[4,2,8,512]{3,2,1,0:T(8,128)S(1)} %get-tuple-element.31), channel_id=1, source_target_pairs={{128,0},{256,128},{384,256},{129,1},{257,129},{385,257},{130,2},{2... | collective-permute-start | bytes 393224 | tf_op jit(solution)/shard_map/ppermute | solution.py:21
  86.8 20.1 %copy-start.2 = (s32[1,1,8192]{2,1,0:T(1,128)S(1)}, s32[1,1,8192]{2,1,0:T(1,128)}, u32[]{:S(2)}) copy-start(s32[1,1,8192]{2,1,0:T(1,128)} %param.7) | copy-start | bytes 98308
  89.4 26.6 %collective-permute-start.10 = (f32[4,16,2,512]{3,2,1,0:T(2,128)S(1)}, f32[4,16,2,512]{3,2,1,0:T(2,128)S(1)}, u32[]{:S(2)}, u32[]{:S(2)}) collective-permute-start(f32[4,16,2,512]{3,2,1,0:T(2,128)S(1)} %get-tuple-element.24), channel_id=1, source_target_pairs={{0,1},{1,2},{2,3},{3,4},{4,5},{5,6},{6,7},{7,8},{8,9},{9,10},{10,1... | collective-permute-start | bytes 786440 | tf_op jit(solution)/shard_map/ppermute | solution.py:20
  101.0 15.8 %collective-permute-start.11 = (f32[4,16,2,512]{3,2,1,0:T(2,128)S(1)}, f32[4,16,2,512]{3,2,1,0:T(2,128)S(1)}, u32[]{:S(2)}, u32[]{:S(2)}) collective-permute-start(f32[4,16,2,512]{3,2,1,0:T(2,128)S(1)} %get-tuple-element.25), channel_id=1, source_target_pairs={{1,0},{2,1},{3,2},{4,3},{5,4},{6,5},{7,6},{8,7},{9,8},{10,9},{11,1... | collective-permute-start | bytes 786440 | tf_op jit(solution)/shard_map/ppermute | solution.py:21
  102.3 5.2 %collective-permute-start.8 = (f32[4,2,8,512]{3,2,1,0:T(8,128)S(1)}, f32[4,2,8,512]{3,2,1,0:T(8,128)S(1)}, u32[]{:S(2)}, u32[]{:S(2)}) collective-permute-start(f32[4,2,8,512]{3,2,1,0:T(8,128)S(1)} %get-tuple-element.26), channel_id=1, source_target_pairs={{0,128},{128,256},{256,384},{1,129},{129,257},{257,385},{2,130},{1... | collective-permute-start | bytes 393224 | tf_op jit(solution)/shard_map/ppermute | solution.py:20
  105.0 11.0 %collective-permute-start.9 = (f32[4,2,8,512]{3,2,1,0:T(8,128)S(1)}, f32[4,2,8,512]{3,2,1,0:T(8,128)S(1)}, u32[]{:S(2)}, u32[]{:S(2)}) collective-permute-start(f32[4,2,8,512]{3,2,1,0:T(8,128)S(1)} %get-tuple-element.27), channel_id=1, source_target_pairs={{128,0},{256,128},{384,256},{129,1},{257,129},{385,257},{130,2},{2... | collective-permute-start | bytes 393224 | tf_op jit(solution)/shard_map/ppermute | solution.py:21
  120.5 33.4 %collective-permute-start.14 = (f32[4,16,2,512]{3,2,1,0:T(2,128)S(1)}, f32[4,16,2,512]{3,2,1,0:T(2,128)S(1)}, u32[]{:S(2)}, u32[]{:S(2)}) collective-permute-start(f32[4,16,2,512]{3,2,1,0:T(2,128)S(1)} %get-tuple-element.20), channel_id=1, source_target_pairs={{0,1},{1,2},{2,3},{3,4},{4,5},{5,6},{6,7},{7,8},{8,9},{9,10},{10,1... | collective-permute-start | bytes 786440 | tf_op jit(solution)/shard_map/ppermute | solution.py:20
  128.6 25.3 %collective-permute-start.15 = (f32[4,16,2,512]{3,2,1,0:T(2,128)S(1)}, f32[4,16,2,512]{3,2,1,0:T(2,128)S(1)}, u32[]{:S(2)}, u32[]{:S(2)}) collective-permute-start(f32[4,16,2,512]{3,2,1,0:T(2,128)S(1)} %get-tuple-element.21), channel_id=1, source_target_pairs={{1,0},{2,1},{3,2},{4,3},{5,4},{6,5},{7,6},{8,7},{9,8},{10,9},{11,1... | collective-permute-start | bytes 786440 | tf_op jit(solution)/shard_map/ppermute | solution.py:21
  129.9 27.7 %all-to-all-start.1 = ((f32[4,16,8,512]{3,2,0,1:T(8,128)}), f32[4,16,8,512]{3,2,0,1:T(8,128)S(1)}, u32[]{:S(2)}, u32[]{:S(2)}) async-start(f32[4,16,8,512]{3,2,0,1:T(8,128)} %copy.45), calls=%async_computation.1 | async-start | bytes 2097152 | tf_op jit(solution)/shard_map/all_to_all | solution.py:85
  136.2 9.0 %collective-permute-start.12 = (f32[4,2,8,512]{3,2,1,0:T(8,128)}, f32[4,2,8,512]{3,2,1,0:T(8,128)}, u32[]{:S(2)}, u32[]{:S(2)}) collective-permute-start(f32[4,2,8,512]{3,2,1,0:T(8,128)} %get-tuple-element.22), channel_id=1, source_target_pairs={{0,128},{128,256},{256,384},{1,129},{129,257},{257,385},{2,130},{1... | collective-permute-start | bytes 393224 | tf_op jit(solution)/shard_map/ppermute | solution.py:20
  142.5 11.4 %collective-permute-start.13 = (f32[4,2,8,512]{3,2,1,0:T(8,128)}, f32[4,2,8,512]{3,2,1,0:T(8,128)}, u32[]{:S(2)}, u32[]{:S(2)}) collective-permute-start(f32[4,2,8,512]{3,2,1,0:T(8,128)} %get-tuple-element.23), channel_id=1, source_target_pairs={{128,0},{256,128},{384,256},{129,1},{257,129},{385,257},{130,2},{2... | collective-permute-start | bytes 393224 | tf_op jit(solution)/shard_map/ppermute | solution.py:21
  157.6 18.7 %all-to-all-start.2 = ((f32[4,16,8,512]{3,2,0,1:T(8,128)}), f32[4,16,8,512]{3,2,0,1:T(8,128)S(1)}, u32[]{:S(2)}, u32[]{:S(2)}) async-start(f32[4,16,8,512]{3,2,0,1:T(8,128)} %copy.47), calls=%async_computation.2 | async-start | bytes 2097152 | tf_op jit(solution)/shard_map/all_to_all | solution.py:86
  176.3 2.4 copy-start.5
  185.5 16.4 %copy-start = (s32[4,8,16,8]{3,2,1,0:T(8,128)S(1)}, s32[4,8,16,8]{3,2,1,0:T(8,128)}, u32[]{:S(2)}) copy-start(s32[4,8,16,8]{3,2,1,0:T(8,128)} %squeeze.17) | copy-start | bytes 49156
  291.1 11.9 %all-to-all-start.7 = ((f32[16,1,2048]{2,1,0:T(1,128)}), f32[16,1,2048]{2,1,0:T(1,128)S(1)}, u32[]{:S(2)}, u32[]{:S(2)}) async-start(f32[16,1,2048]{2,1,0:T(1,128)} %reshape.1347), calls=%async_computation.7 | async-start | bytes 262144 | tf_op jit(solution)/shard_map/all_to_all | solution.py:41
  (2 other events, 4.1 us)

commit v7 on v6

--- a/solution.py
+++ b/solution.py
@@ -28,9 +28,8 @@
 def exchange_scatter(x):
     n = x.shape[0]
     zh, xl, gy = (lax.axis_size(axis) for axis in BLOCK_AXES)
-    y = x.reshape(n, zh, xl, gy, -1).transpose(0, 2, 1, 3, 4)
-    y = lax.all_to_all(y, "xl", 1, 1, tiled=True).sum(1)
-    y = lax.all_to_all(y.transpose(0, 2, 1, 3), "gy", 1, 1, tiled=True).sum(1)
+    y = x.reshape(n, zh, xl * gy, -1).transpose(0, 2, 1, 3)
+    y = lax.all_to_all(y, ("xl", "gy"), 1, 1, tiled=True).sum(1)
     return exchange_sum(y, ("zh",))
 
 

time: 318 us -> 323 us (1.016)
  blocking collectives: 72.6 us -> 78.1 us
    all_to_all x2 -> x1, blocking collectives: 47.3 us -> 52 us  [exchange_scatter(): y = lax.all_to_all(y, ('xl', 'gy'), 1, 1, tiled=True).sum(1)]
    unnamed x27 -> x34, local copies, waits for them, and re-layouts: 8.87 us -> 8.66 us
where the time goes in v7:
time: 323 us; the launch traced here: 320 us
  starting transfers between devices  88.3 us (27%)
  blocking collectives  78.1 us (24%)
  waiting for transfers between devices  76.7 us (24%)
  local copies, waits for them, and re-layouts  36.8 us (11%)
  other arithmetic  32.5 us (10%)
  matrix products  6.6 us (2%)
    ppermute x8, starting transfers between devices, halos(): before = lax.ppermute(last, axis, up)  54.5 us
    all_to_all x1, blocking collectives, exchange_scatter(): y = lax.all_to_all(y, ('xl', 'gy'), 1, 1, tiled=True).sum(1)  52 us
    ppermute x8, waiting for transfers between devices, halos(): after = lax.ppermute(initial, axis, down)  37 us
    all_to_all x2, blocking collectives, exchange_sum(): x = lax.all_to_all(copies, axis, 0, 0, tiled=True).sum(0)  26.1 us
    all_to_all x1, waiting for transfers between devices, shards(): both = lax.all_to_all(both, 'xl', 0, 1, tiled=True)  16.4 us
    gather x1, local copies, waits for them, and re-layouts, shards(): picked = jnp.take(mixed, sampled_rows[0, 0, :M], axis=1)  16.3 us
    all_to_all x1, waiting for transfers between devices, shards(): applied = lax.all_to_all(spread_applied, 'xl', 1, 0, tiled=True)  13.7 us
    ppermute x8, starting transfers between devices, halos(): after = lax.ppermute(initial, axis, down)  10.3 us
  transfers between devices with their start and end apart: 20, of which 12 were waited for; matrix products, arithmetic and copies ran while one was open for 3% of the time, Pallas kernels for 0%

profile of v7, /device:TPU:6, one launch (start us, length us, event | category | flops | bytes accessed | tf_op | source)
XLA Modules:
  0.0 320.2 jit_solution(12684735893390082214)
XLA Ops:
  3.9 9.5 %all-to-all-start = ((f32[40,2,8,512]{3,2,1,0:T(8,128)}), f32[40,2,8,512]{3,2,1,0:T(8,128)S(1)}, u32[]{:S(2)}, u32[]{:S(2)}) async-start(f32[40,2,8,512]{3,2,1,0:T(8,128)} %bitcast.1), calls=%async_computation | async-start | bytes 2621440 | tf_op jit(solution)/shard_map/all_to_all | solution.py:76
  13.7 16.4 %all-to-all-done = f32[40,2,8,512]{3,2,1,0:T(8,128)S(1)} async-done(((f32[40,2,8,512]{3,2,1,0:T(8,128)}), f32[40,2,8,512]{3,2,1,0:T(8,128)S(1)}, u32[]{:S(2)}, u32[]{:S(2)}) %all-to-all-start) | async-done | bytes 1310752 | tf_op jit(solution)/shard_map/all_to_all | solution.py:76
  33.1 7.1 %collective-permute-start = (f32[4,2,8,512]{3,2,1,0:T(8,128)S(1)}, f32[4,2,8,512]{3,2,1,0:T(8,128)S(1)}, u32[]{:S(2)}, u32[]{:S(2)}) collective-permute-start(f32[4,2,8,512]{3,2,1,0:T(8,128)S(1)} %get-tuple-element.32), channel_id=1, source_target_pairs={{0,128},{128,256},{256,384},{1,129},{129,257},{257,385},{2,130},{1... | collective-permute-start | bytes 393224 | tf_op jit(solution)/shard_map/ppermute | solution.py:20
  42.6 11.5 %collective-permute-done.1 = f32[4,2,8,512]{3,2,1,0:T(8,128)S(1)} collective-permute-done((f32[4,2,8,512]{3,2,1,0:T(8,128)S(1)}, f32[4,2,8,512]{3,2,1,0:T(8,128)S(1)}, u32[]{:S(2)}, u32[]{:S(2)}) %collective-permute-start.1) | collective-permute-done | bytes 131104 | tf_op jit(solution)/shard_map/ppermute | solution.py:21
  56.7 10.4 %collective-permute-start.6 = (f32[4,16,2,512]{3,2,1,0:T(2,128)S(1)}, f32[4,16,2,512]{3,2,1,0:T(2,128)S(1)}, u32[]{:S(2)}, u32[]{:S(2)}) collective-permute-start(f32[4,16,2,512]{3,2,1,0:T(2,128)S(1)} %get-tuple-element.28), channel_id=1, source_target_pairs={{0,1},{1,2},{2,3},{3,4},{4,5},{5,6},{6,7},{7,8},{8,9},{9,10},{10,1... | collective-permute-start | bytes 786440 | tf_op jit(solution)/shard_map/ppermute | solution.py:20
  68.4 7.7 %collective-permute-start.4 = (f32[4,2,8,512]{3,2,1,0:T(8,128)S(1)}, f32[4,2,8,512]{3,2,1,0:T(8,128)S(1)}, u32[]{:S(2)}, u32[]{:S(2)}) collective-permute-start(f32[4,2,8,512]{3,2,1,0:T(8,128)S(1)} %get-tuple-element.30), channel_id=1, source_target_pairs={{0,128},{128,256},{256,384},{1,129},{129,257},{257,385},{2,130},{1... | collective-permute-start | bytes 393224 | tf_op jit(solution)/shard_map/ppermute | solution.py:20
  78.7 8.3 %collective-permute-done.5 = f32[4,2,8,512]{3,2,1,0:T(8,128)S(1)} collective-permute-done((f32[4,2,8,512]{3,2,1,0:T(8,128)S(1)}, f32[4,2,8,512]{3,2,1,0:T(8,128)S(1)}, u32[]{:S(2)}, u32[]{:S(2)}) %collective-permute-start.5) | collective-permute-done | bytes 131104 | tf_op jit(solution)/shard_map/ppermute | solution.py:21
  89.5 11.6 %collective-permute-start.10 = (f32[4,16,2,512]{3,2,1,0:T(2,128)S(1)}, f32[4,16,2,512]{3,2,1,0:T(2,128)S(1)}, u32[]{:S(2)}, u32[]{:S(2)}) collective-permute-start(f32[4,16,2,512]{3,2,1,0:T(2,128)S(1)} %get-tuple-element.24), channel_id=1, source_target_pairs={{0,1},{1,2},{2,3},{3,4},{4,5},{5,6},{6,7},{7,8},{8,9},{9,10},{10,1... | collective-permute-start | bytes 786440 | tf_op jit(solution)/shard_map/ppermute | solution.py:20
  107.7 8.5 %collective-permute-done.9 = f32[4,2,8,512]{3,2,1,0:T(8,128)S(1)} collective-permute-done((f32[4,2,8,512]{3,2,1,0:T(8,128)S(1)}, f32[4,2,8,512]{3,2,1,0:T(8,128)S(1)}, u32[]{:S(2)}, u32[]{:S(2)}) %collective-permute-start.9) | collective-permute-done | bytes 131104 | tf_op jit(solution)/shard_map/ppermute | solution.py:21
  121.3 8.1 %collective-permute-start.14 = (f32[4,16,2,512]{3,2,1,0:T(2,128)}, f32[4,16,2,512]{3,2,1,0:T(2,128)S(1)}, u32[]{:S(2)}, u32[]{:S(2)}) collective-permute-start(f32[4,16,2,512]{3,2,1,0:T(2,128)} %get-tuple-element.20), channel_id=1, source_target_pairs={{0,1},{1,2},{2,3},{3,4},{4,5},{5,6},{6,7},{7,8},{8,9},{9,10},{10,1... | collective-permute-start | bytes 786440 | tf_op jit(solution)/shard_map/ppermute | solution.py:20
  130.7 5.6 %all-to-all-start.1 = ((f32[4,16,8,512]{3,2,0,1:T(8,128)}), f32[4,16,8,512]{3,2,0,1:T(8,128)S(1)}, u32[]{:S(2)}, u32[]{:S(2)}) async-start(f32[4,16,8,512]{3,2,0,1:T(8,128)} %copy.44), calls=%async_computation.1 | async-start | bytes 2097152 | tf_op jit(solution)/shard_map/all_to_all | solution.py:84
  137.0 5.6 %collective-permute-start.12 = (f32[4,2,8,512]{3,2,1,0:T(8,128)}, f32[4,2,8,512]{3,2,1,0:T(8,128)S(1)}, u32[]{:S(2)}, u32[]{:S(2)}) collective-permute-start(f32[4,2,8,512]{3,2,1,0:T(8,128)} %get-tuple-element.22), channel_id=1, source_target_pairs={{0,128},{128,256},{256,384},{1,129},{129,257},{257,385},{2,130},{1... | collective-permute-start | bytes 393224 | tf_op jit(solution)/shard_map/ppermute | solution.py:20
  146.0 8.0 %collective-permute-done.13 = f32[4,2,8,512]{3,2,1,0:T(8,128)} collective-permute-done((f32[4,2,8,512]{3,2,1,0:T(8,128)}, f32[4,2,8,512]{3,2,1,0:T(8,128)}, u32[]{:S(2)}, u32[]{:S(2)}) %collective-permute-start.13) | collective-permute-done | bytes 131104 | tf_op jit(solution)/shard_map/ppermute | solution.py:21
  157.7 4.8 %all-to-all-start.2 = ((f32[4,16,8,512]{3,2,0,1:T(8,128)}), f32[4,16,8,512]{3,2,0,1:T(8,128)S(1)}, u32[]{:S(2)}, u32[]{:S(2)}) async-start(f32[4,16,8,512]{3,2,0,1:T(8,128)} %copy.46), calls=%async_computation.2 | async-start | bytes 2097152 | tf_op jit(solution)/shard_map/all_to_all | solution.py:85
  162.7 13.7 %all-to-all-done.2 = f32[4,16,8,512]{3,2,0,1:T(8,128)S(1)} async-done(((f32[4,16,8,512]{3,2,0,1:T(8,128)}), f32[4,16,8,512]{3,2,0,1:T(8,128)S(1)}, u32[]{:S(2)}, u32[]{:S(2)}) %all-to-all-start.2) | async-done | bytes 1048608 | tf_op jit(solution)/shard_map/all_to_all | solution.py:85
  185.8 16.3 %gather_fusion = f32[4096,64]{1,0:T(8,128)} fusion(f32[64,8192]{0,1:T(8,128)} %bitcast.91, s32[4096]{0:T(1024)S(1)} %broadcast_clamp_fusion), kind=kCustom, calls=%fused_computation | custom fusion | bytes 2113536 | tf_op jit(solution)/shard_map/jit(_take)/gather | solution.py:94
  202.0 2.8 fusion.196
  207.1 52.0 %all_to_all.65 = f32[128,1,2048]{2,1,0:T(1,128)S(1)} all-to-all(f32[128,1,2048]{2,1,0:T(1,128)} %reshape.1339), channel_id=1, replica_groups=mesh['zh'=4,'xl'=8,'gy'=16] {'xl','gy'}, dimensions={0} | all-to-all | bytes 2097152 | tf_op jit(solution)/shard_map/all_to_all | solution.py:32
  259.6 4.3 %reduce.10 = f32[128,2048]{1,0:T(8,128)} reduce(f32[128,1,2048]{2,1,0:T(1,128)S(1)} %all_to_all.65, f32[]{:T(128)} %broadcast.1731), dimensions={1}, to_apply=%all_to_all.54.reduce_sub_computation | reduce | bytes 2097156 | tf_op jit(solution)/shard_map/all_to_all | solution.py:32
  266.2 17.9 %all_to_all.66 = f32[4,1,2048]{2,1,0:T(1,128)S(1)} all-to-all(f32[4,1,2048]{2,1,0:T(1,128)S(1)} %reshape.1341), channel_id=1, replica_groups=mesh['zh'=4,'xl'=8,'gy'=16] {'zh'}, dimensions={0} | all-to-all | bytes 65536 | tf_op jit(solution)/shard_map/all_to_all | solution.py:40
  285.6 8.2 %all_to_all.67 = f32[8,1,2048]{2,1,0:T(1,128)S(1)} all-to-all(f32[8,1,2048]{2,1,0:T(1,128)S(1)} %reshape.1343), channel_id=1, replica_groups=mesh['zh'=4,'xl'=8,'gy'=16] {'xl'}, dimensions={0} | all-to-all | bytes 131072 | tf_op jit(solution)/shard_map/all_to_all | solution.py:40
  295.7 3.6 %all-to-all-start.6 = ((f32[16,1,2048]{2,1,0:T(1,128)}), f32[16,1,2048]{2,1,0:T(1,128)S(1)}, u32[]{:S(2)}, u32[]{:S(2)}) async-start(f32[16,1,2048]{2,1,0:T(1,128)} %reshape.1345), calls=%async_computation.6 | async-start | bytes 262144 | tf_op jit(solution)/shard_map/all_to_all | solution.py:40
  300.9 6.9 %all-to-all-done.6 = f32[16,1,2048]{2,1,0:T(1,128)S(1)} async-done(((f32[16,1,2048]{2,1,0:T(1,128)}), f32[16,1,2048]{2,1,0:T(1,128)S(1)}, u32[]{:S(2)}, u32[]{:S(2)}) %all-to-all-start.6) | async-done | bytes 131104 | tf_op jit(solution)/shard_map/all_to_all | solution.py:40
  309.1 2.9 cholesky.17
  (130 shorter events, 67.5 us)
Async XLA Ops:
  1.4 12.0 %copy-start.1 = (s32[1,1,8192]{2,1,0:T(1,128)S(1)}, s32[1,1,8192]{2,1,0:T(1,128)}, u32[]{:S(2)}) copy-start(s32[1,1,8192]{2,1,0:T(1,128)} %param.7) | copy-start | bytes 98308
  3.9 9.7 %copy-start = (s32[2,8,512]{2,1,0:T(8,128)S(1)}, s32[2,8,512]{2,1,0:T(8,128)}, u32[]{:S(2)}) copy-start(s32[2,8,512]{2,1,0:T(8,128)} %param.6) | copy-start | bytes 98308
  3.9 26.2 %all-to-all-start = ((f32[40,2,8,512]{3,2,1,0:T(8,128)}), f32[40,2,8,512]{3,2,1,0:T(8,128)S(1)}, u32[]{:S(2)}, u32[]{:S(2)}) async-start(f32[40,2,8,512]{3,2,1,0:T(8,128)} %bitcast.1), calls=%async_computation | async-start | bytes 2621440 | tf_op jit(solution)/shard_map/all_to_all | solution.py:76
  30.4 23.7 %collective-permute-start.2 = (f32[4,16,2,512]{3,2,1,0:T(2,128)S(1)}, f32[4,16,2,512]{3,2,1,0:T(2,128)S(1)}, u32[]{:S(2)}, u32[]{:S(2)}) collective-permute-start(f32[4,16,2,512]{3,2,1,0:T(2,128)S(1)} %get-tuple-element.34), channel_id=1, source_target_pairs={{0,1},{1,2},{2,3},{3,4},{4,5},{5,6},{6,7},{7,8},{8,9},{9,10},{10,1... | collective-permute-start | bytes 786440 | tf_op jit(solution)/shard_map/ppermute | solution.py:20
  31.7 22.4 %collective-permute-start.3 = (f32[4,16,2,512]{3,2,1,0:T(2,128)S(1)}, f32[4,16,2,512]{3,2,1,0:T(2,128)S(1)}, u32[]{:S(2)}, u32[]{:S(2)}) collective-permute-start(f32[4,16,2,512]{3,2,1,0:T(2,128)S(1)} %get-tuple-element.35), channel_id=1, source_target_pairs={{1,0},{2,1},{3,2},{4,3},{5,4},{6,5},{7,6},{8,7},{9,8},{10,9},{11,1... | collective-permute-start | bytes 786440 | tf_op jit(solution)/shard_map/ppermute | solution.py:21
  33.1 9.6 %collective-permute-start = (f32[4,2,8,512]{3,2,1,0:T(8,128)S(1)}, f32[4,2,8,512]{3,2,1,0:T(8,128)S(1)}, u32[]{:S(2)}, u32[]{:S(2)}) collective-permute-start(f32[4,2,8,512]{3,2,1,0:T(8,128)S(1)} %get-tuple-element.32), channel_id=1, source_target_pairs={{0,128},{128,256},{256,384},{1,129},{129,257},{257,385},{2,130},{1... | collective-permute-start | bytes 393224 | tf_op jit(solution)/shard_map/ppermute | solution.py:20
  40.1 13.9 %collective-permute-start.1 = (f32[4,2,8,512]{3,2,1,0:T(8,128)S(1)}, f32[4,2,8,512]{3,2,1,0:T(8,128)S(1)}, u32[]{:S(2)}, u32[]{:S(2)}) collective-permute-start(f32[4,2,8,512]{3,2,1,0:T(8,128)S(1)} %get-tuple-element.33), channel_id=1, source_target_pairs={{128,0},{256,128},{384,256},{129,1},{257,129},{385,257},{130,2},{2... | collective-permute-start | bytes 393224 | tf_op jit(solution)/shard_map/ppermute | solution.py:21
  56.7 30.2 %collective-permute-start.6 = (f32[4,16,2,512]{3,2,1,0:T(2,128)S(1)}, f32[4,16,2,512]{3,2,1,0:T(2,128)S(1)}, u32[]{:S(2)}, u32[]{:S(2)}) collective-permute-start(f32[4,16,2,512]{3,2,1,0:T(2,128)S(1)} %get-tuple-element.28), channel_id=1, source_target_pairs={{0,1},{1,2},{2,3},{3,4},{4,5},{5,6},{6,7},{7,8},{8,9},{9,10},{10,1... | collective-permute-start | bytes 786440 | tf_op jit(solution)/shard_map/ppermute | solution.py:20
  67.1 19.8 %collective-permute-start.7 = (f32[4,16,2,512]{3,2,1,0:T(2,128)S(1)}, f32[4,16,2,512]{3,2,1,0:T(2,128)S(1)}, u32[]{:S(2)}, u32[]{:S(2)}) collective-permute-start(f32[4,16,2,512]{3,2,1,0:T(2,128)S(1)} %get-tuple-element.29), channel_id=1, source_target_pairs={{1,0},{2,1},{3,2},{4,3},{5,4},{6,5},{7,6},{8,7},{9,8},{10,9},{11,1... | collective-permute-start | bytes 786440 | tf_op jit(solution)/shard_map/ppermute | solution.py:21
  68.4 10.2 %collective-permute-start.4 = (f32[4,2,8,512]{3,2,1,0:T(8,128)S(1)}, f32[4,2,8,512]{3,2,1,0:T(8,128)S(1)}, u32[]{:S(2)}, u32[]{:S(2)}) collective-permute-start(f32[4,2,8,512]{3,2,1,0:T(8,128)S(1)} %get-tuple-element.30), channel_id=1, source_target_pairs={{0,128},{128,256},{256,384},{1,129},{129,257},{257,385},{2,130},{1... | collective-permute-start | bytes 393224 | tf_op jit(solution)/shard_map/ppermute | solution.py:20
  76.1 10.8 %collective-permute-start.5 = (f32[4,2,8,512]{3,2,1,0:T(8,128)S(1)}, f32[4,2,8,512]{3,2,1,0:T(8,128)S(1)}, u32[]{:S(2)}, u32[]{:S(2)}) collective-permute-start(f32[4,2,8,512]{3,2,1,0:T(8,128)S(1)} %get-tuple-element.31), channel_id=1, source_target_pairs={{128,0},{256,128},{384,256},{129,1},{257,129},{385,257},{130,2},{2... | collective-permute-start | bytes 393224 | tf_op jit(solution)/shard_map/ppermute | solution.py:21
  89.5 26.6 %collective-permute-start.10 = (f32[4,16,2,512]{3,2,1,0:T(2,128)S(1)}, f32[4,16,2,512]{3,2,1,0:T(2,128)S(1)}, u32[]{:S(2)}, u32[]{:S(2)}) collective-permute-start(f32[4,16,2,512]{3,2,1,0:T(2,128)S(1)} %get-tuple-element.24), channel_id=1, source_target_pairs={{0,1},{1,2},{2,3},{3,4},{4,5},{5,6},{6,7},{7,8},{8,9},{9,10},{10,1... | collective-permute-start | bytes 786440 | tf_op jit(solution)/shard_map/ppermute | solution.py:20
  101.1 15.8 %collective-permute-start.11 = (f32[4,16,2,512]{3,2,1,0:T(2,128)S(1)}, f32[4,16,2,512]{3,2,1,0:T(2,128)S(1)}, u32[]{:S(2)}, u32[]{:S(2)}) collective-permute-start(f32[4,16,2,512]{3,2,1,0:T(2,128)S(1)} %get-tuple-element.25), channel_id=1, source_target_pairs={{1,0},{2,1},{3,2},{4,3},{5,4},{6,5},{7,6},{8,7},{9,8},{10,9},{11,1... | collective-permute-start | bytes 786440 | tf_op jit(solution)/shard_map/ppermute | solution.py:21
  102.4 5.2 %collective-permute-start.8 = (f32[4,2,8,512]{3,2,1,0:T(8,128)S(1)}, f32[4,2,8,512]{3,2,1,0:T(8,128)S(1)}, u32[]{:S(2)}, u32[]{:S(2)}) collective-permute-start(f32[4,2,8,512]{3,2,1,0:T(8,128)S(1)} %get-tuple-element.26), channel_id=1, source_target_pairs={{0,128},{128,256},{256,384},{1,129},{129,257},{257,385},{2,130},{1... | collective-permute-start | bytes 393224 | tf_op jit(solution)/shard_map/ppermute | solution.py:20
  105.1 11.0 %collective-permute-start.9 = (f32[4,2,8,512]{3,2,1,0:T(8,128)S(1)}, f32[4,2,8,512]{3,2,1,0:T(8,128)S(1)}, u32[]{:S(2)}, u32[]{:S(2)}) collective-permute-start(f32[4,2,8,512]{3,2,1,0:T(8,128)S(1)} %get-tuple-element.27), channel_id=1, source_target_pairs={{128,0},{256,128},{384,256},{129,1},{257,129},{385,257},{130,2},{2... | collective-permute-start | bytes 393224 | tf_op jit(solution)/shard_map/ppermute | solution.py:21
  121.3 32.7 %collective-permute-start.14 = (f32[4,16,2,512]{3,2,1,0:T(2,128)}, f32[4,16,2,512]{3,2,1,0:T(2,128)S(1)}, u32[]{:S(2)}, u32[]{:S(2)}) collective-permute-start(f32[4,16,2,512]{3,2,1,0:T(2,128)} %get-tuple-element.20), channel_id=1, source_target_pairs={{0,1},{1,2},{2,3},{3,4},{4,5},{5,6},{6,7},{7,8},{8,9},{9,10},{10,1... | collective-permute-start | bytes 786440 | tf_op jit(solution)/shard_map/ppermute | solution.py:20
  129.4 24.6 %collective-permute-start.15 = (f32[4,16,2,512]{3,2,1,0:T(2,128)S(1)}, f32[4,16,2,512]{3,2,1,0:T(2,128)S(1)}, u32[]{:S(2)}, u32[]{:S(2)}) collective-permute-start(f32[4,16,2,512]{3,2,1,0:T(2,128)S(1)} %get-tuple-element.21), channel_id=1, source_target_pairs={{1,0},{2,1},{3,2},{4,3},{5,4},{6,5},{7,6},{8,7},{9,8},{10,9},{11,1... | collective-permute-start | bytes 786440 | tf_op jit(solution)/shard_map/ppermute | solution.py:21
  130.7 27.0 %all-to-all-start.1 = ((f32[4,16,8,512]{3,2,0,1:T(8,128)}), f32[4,16,8,512]{3,2,0,1:T(8,128)S(1)}, u32[]{:S(2)}, u32[]{:S(2)}) async-start(f32[4,16,8,512]{3,2,0,1:T(8,128)} %copy.44), calls=%async_computation.1 | async-start | bytes 2097152 | tf_op jit(solution)/shard_map/all_to_all | solution.py:84
  137.0 9.0 %collective-permute-start.12 = (f32[4,2,8,512]{3,2,1,0:T(8,128)}, f32[4,2,8,512]{3,2,1,0:T(8,128)S(1)}, u32[]{:S(2)}, u32[]{:S(2)}) collective-permute-start(f32[4,2,8,512]{3,2,1,0:T(8,128)} %get-tuple-element.22), channel_id=1, source_target_pairs={{0,128},{128,256},{256,384},{1,129},{129,257},{257,385},{2,130},{1... | collective-permute-start | bytes 393224 | tf_op jit(solution)/shard_map/ppermute | solution.py:20
  142.6 11.4 %collective-permute-start.13 = (f32[4,2,8,512]{3,2,1,0:T(8,128)}, f32[4,2,8,512]{3,2,1,0:T(8,128)}, u32[]{:S(2)}, u32[]{:S(2)}) collective-permute-start(f32[4,2,8,512]{3,2,1,0:T(8,128)} %get-tuple-element.23), channel_id=1, source_target_pairs={{128,0},{256,128},{384,256},{129,1},{257,129},{385,257},{130,2},{2... | collective-permute-start | bytes 393224 | tf_op jit(solution)/shard_map/ppermute | solution.py:21
  157.7 18.7 %all-to-all-start.2 = ((f32[4,16,8,512]{3,2,0,1:T(8,128)}), f32[4,16,8,512]{3,2,0,1:T(8,128)S(1)}, u32[]{:S(2)}, u32[]{:S(2)}) async-start(f32[4,16,8,512]{3,2,0,1:T(8,128)} %copy.46), calls=%async_computation.2 | async-start | bytes 2097152 | tf_op jit(solution)/shard_map/all_to_all | solution.py:85
  176.4 2.4 copy-start.2
  176.4 2.4 copy-start.3
  295.7 12.0 %all-to-all-start.6 = ((f32[16,1,2048]{2,1,0:T(1,128)}), f32[16,1,2048]{2,1,0:T(1,128)S(1)}, u32[]{:S(2)}, u32[]{:S(2)}) async-start(f32[16,1,2048]{2,1,0:T(1,128)} %reshape.1345), calls=%async_computation.6 | async-start | bytes 262144 | tf_op jit(solution)/shard_map/all_to_all | solution.py:40
  (7 other events, 13.8 us)

commit v8 on v6

--- a/solution.py
+++ b/solution.py
@@ -90,9 +90,9 @@
     sign_block = (2 * sign_bits - 1).astype(jnp.float32)
     flat = (stacked * sign_block[None]).reshape(2 * count, -1, 128)
     mixed = jnp.einsum("nac,cd->nad", flat, hadamard_table(128), precision=HIGHEST)
-    mixed = jnp.einsum("ba,nac->nbc", hadamard_table(cells // 128), mixed, precision=HIGHEST)
-    mixed = mixed.reshape(2 * count, cells)
-    picked = jnp.take(mixed, sampled_rows[0, 0, :M], axis=1)
+    mixed = jnp.einsum("ba,nac->bcn", hadamard_table(cells // 128), mixed, precision=HIGHEST)
+    mixed = mixed.reshape(cells, 2 * count)
+    picked = jnp.take(mixed, sampled_rows[0, 0, :M], axis=0).T
     devices = lax.axis_size("zh") * lax.axis_size("xl") * lax.axis_size("gy")
     term = (picked / jnp.sqrt(jnp.float32(M * devices))).reshape(2, count, M)
     summed = exchange_scatter(term.reshape(2 * count, M))

time: 318 us -> 314 us (0.987)
  local copies, waits for them, and re-layouts: 37.1 us -> 32.9 us
    gather x1, local copies, waits for them, and re-layouts: 16.4 us -> 13 us  [shards(): picked = jnp.take(mixed, sampled_rows[0, 0, :M], axis=0).T]
    unnamed x27 -> x19, local copies, waits for them, and re-layouts: 8.87 us -> 8.86 us
  transfers between devices with their start and end apart: 20 -> 20, of which waited for: 12 -> 12; matrix products, arithmetic and copies ran while one was open for 3% -> 2% of each run, Pallas kernels for 0% -> 0%
where the time goes in v8:
time: 314 us; the launch traced here: 312 us
  starting transfers between devices  88.7 us (28%)
  waiting for transfers between devices  79.7 us (25%)
  blocking collectives  72.6 us (23%)
  local copies, waits for them, and re-layouts  32.9 us (10%)
  other arithmetic  30.1 us (10%)
  matrix products  6.6 us (2%)
    ppermute x8, starting transfers between devices, halos(): before = lax.ppermute(last, axis, up)  55.1 us
    ppermute x8, waiting for transfers between devices, halos(): after = lax.ppermute(initial, axis, down)  37.6 us
    all_to_all x1, blocking collectives, exchange_scatter(): y = lax.all_to_all(y.transpose(0, 2, 1, 3), 'gy', 1, 1, tiled=True).sum(1)  27.8 us
    all_to_all x2, blocking collectives, exchange_sum(): x = lax.all_to_all(copies, axis, 0, 0, tiled=True).sum(0)  25.3 us
    all_to_all x1, blocking collectives, exchange_scatter(): y = lax.all_to_all(y, 'xl', 1, 1, tiled=True).sum(1)  19.6 us
    all_to_all x1, waiting for transfers between devices, shards(): both = lax.all_to_all(both, 'xl', 0, 1, tiled=True)  16.6 us
    all_to_all x1, waiting for transfers between devices, shards(): applied = lax.all_to_all(spread_applied, 'xl', 1, 0, tiled=True)  13.7 us
    gather x1, local copies, waits for them, and re-layouts, shards(): picked = jnp.take(mixed, sampled_rows[0, 0, :M], axis=0).T  13 us
  transfers between devices with their start and end apart: 20, of which 12 were waited for; matrix products, arithmetic and copies ran while one was open for 2% of the time, Pallas kernels for 0%

profile of v8, /device:TPU:6, one launch (start us, length us, event | category | flops | bytes accessed | tf_op | source)
XLA Modules:
  0.0 311.9 jit_solution(18220963440639836252)
XLA Ops:
  3.9 9.4 %all-to-all-start = ((f32[40,2,8,512]{3,2,1,0:T(8,128)}), f32[40,2,8,512]{3,2,1,0:T(8,128)S(1)}, u32[]{:S(2)}, u32[]{:S(2)}) async-start(f32[40,2,8,512]{3,2,1,0:T(8,128)} %bitcast.2), calls=%async_computation | async-start | bytes 2621440 | tf_op jit(solution)/shard_map/all_to_all | solution.py:77
  13.3 16.6 %all-to-all-done = f32[40,2,8,512]{3,2,1,0:T(8,128)S(1)} async-done(((f32[40,2,8,512]{3,2,1,0:T(8,128)}), f32[40,2,8,512]{3,2,1,0:T(8,128)S(1)}, u32[]{:S(2)}, u32[]{:S(2)}) %all-to-all-start) | async-done | bytes 1310752 | tf_op jit(solution)/shard_map/all_to_all | solution.py:77
  32.9 7.1 %collective-permute-start = (f32[4,2,8,512]{3,2,1,0:T(8,128)S(1)}, f32[4,2,8,512]{3,2,1,0:T(8,128)S(1)}, u32[]{:S(2)}, u32[]{:S(2)}) collective-permute-start(f32[4,2,8,512]{3,2,1,0:T(8,128)S(1)} %get-tuple-element.32), channel_id=1, source_target_pairs={{0,128},{128,256},{256,384},{1,129},{129,257},{257,385},{2,130},{1... | collective-permute-start | bytes 393224 | tf_op jit(solution)/shard_map/ppermute | solution.py:20
  42.5 11.5 %collective-permute-done.1 = f32[4,2,8,512]{3,2,1,0:T(8,128)S(1)} collective-permute-done((f32[4,2,8,512]{3,2,1,0:T(8,128)S(1)}, f32[4,2,8,512]{3,2,1,0:T(8,128)S(1)}, u32[]{:S(2)}, u32[]{:S(2)}) %collective-permute-start.1) | collective-permute-done | bytes 131104 | tf_op jit(solution)/shard_map/ppermute | solution.py:21
  56.6 10.4 %collective-permute-start.6 = (f32[4,16,2,512]{3,2,1,0:T(2,128)S(1)}, f32[4,16,2,512]{3,2,1,0:T(2,128)S(1)}, u32[]{:S(2)}, u32[]{:S(2)}) collective-permute-start(f32[4,16,2,512]{3,2,1,0:T(2,128)S(1)} %get-tuple-element.28), channel_id=1, source_target_pairs={{0,1},{1,2},{2,3},{3,4},{4,5},{5,6},{6,7},{7,8},{8,9},{9,10},{10,1... | collective-permute-start | bytes 786440 | tf_op jit(solution)/shard_map/ppermute | solution.py:20
  68.3 7.7 %collective-permute-start.4 = (f32[4,2,8,512]{3,2,1,0:T(8,128)S(1)}, f32[4,2,8,512]{3,2,1,0:T(8,128)S(1)}, u32[]{:S(2)}, u32[]{:S(2)}) collective-permute-start(f32[4,2,8,512]{3,2,1,0:T(8,128)S(1)} %get-tuple-element.30), channel_id=1, source_target_pairs={{0,128},{128,256},{256,384},{1,129},{129,257},{257,385},{2,130},{1... | collective-permute-start | bytes 393224 | tf_op jit(solution)/shard_map/ppermute | solution.py:20
  78.5 8.3 %collective-permute-done.5 = f32[4,2,8,512]{3,2,1,0:T(8,128)S(1)} collective-permute-done((f32[4,2,8,512]{3,2,1,0:T(8,128)S(1)}, f32[4,2,8,512]{3,2,1,0:T(8,128)S(1)}, u32[]{:S(2)}, u32[]{:S(2)}) %collective-permute-start.5) | collective-permute-done | bytes 131104 | tf_op jit(solution)/shard_map/ppermute | solution.py:21
  89.4 11.6 %collective-permute-start.10 = (f32[4,16,2,512]{3,2,1,0:T(2,128)S(1)}, f32[4,16,2,512]{3,2,1,0:T(2,128)S(1)}, u32[]{:S(2)}, u32[]{:S(2)}) collective-permute-start(f32[4,16,2,512]{3,2,1,0:T(2,128)S(1)} %get-tuple-element.24), channel_id=1, source_target_pairs={{0,1},{1,2},{2,3},{3,4},{4,5},{5,6},{6,7},{7,8},{8,9},{9,10},{10,1... | collective-permute-start | bytes 786440 | tf_op jit(solution)/shard_map/ppermute | solution.py:20
  107.5 8.5 %collective-permute-done.9 = f32[4,2,8,512]{3,2,1,0:T(8,128)S(1)} collective-permute-done((f32[4,2,8,512]{3,2,1,0:T(8,128)S(1)}, f32[4,2,8,512]{3,2,1,0:T(8,128)S(1)}, u32[]{:S(2)}, u32[]{:S(2)}) %collective-permute-start.9) | collective-permute-done | bytes 131104 | tf_op jit(solution)/shard_map/ppermute | solution.py:21
  120.5 8.1 %collective-permute-start.14 = (f32[4,16,2,512]{3,2,1,0:T(2,128)S(1)}, f32[4,16,2,512]{3,2,1,0:T(2,128)S(1)}, u32[]{:S(2)}, u32[]{:S(2)}) collective-permute-start(f32[4,16,2,512]{3,2,1,0:T(2,128)S(1)} %get-tuple-element.20), channel_id=1, source_target_pairs={{0,1},{1,2},{2,3},{3,4},{4,5},{5,6},{6,7},{7,8},{8,9},{9,10},{10,1... | collective-permute-start | bytes 786440 | tf_op jit(solution)/shard_map/ppermute | solution.py:20
  129.9 5.6 %all-to-all-start.1 = ((f32[4,16,8,512]{3,2,0,1:T(8,128)}), f32[4,16,8,512]{3,2,0,1:T(8,128)S(1)}, u32[]{:S(2)}, u32[]{:S(2)}) async-start(f32[4,16,8,512]{3,2,0,1:T(8,128)} %copy.43), calls=%async_computation.1 | async-start | bytes 2097152 | tf_op jit(solution)/shard_map/all_to_all | solution.py:85
  136.2 6.3 %collective-permute-start.12 = (f32[4,2,8,512]{3,2,1,0:T(8,128)}, f32[4,2,8,512]{3,2,1,0:T(8,128)}, u32[]{:S(2)}, u32[]{:S(2)}) collective-permute-start(f32[4,2,8,512]{3,2,1,0:T(8,128)} %get-tuple-element.22), channel_id=1, source_target_pairs={{0,128},{128,256},{256,384},{1,129},{129,257},{257,385},{2,130},{1... | collective-permute-start | bytes 393224 | tf_op jit(solution)/shard_map/ppermute | solution.py:20
  145.1 8.7 %collective-permute-done.13 = f32[4,2,8,512]{3,2,1,0:T(8,128)} collective-permute-done((f32[4,2,8,512]{3,2,1,0:T(8,128)}, f32[4,2,8,512]{3,2,1,0:T(8,128)}, u32[]{:S(2)}, u32[]{:S(2)}) %collective-permute-start.13) | collective-permute-done | bytes 131104 | tf_op jit(solution)/shard_map/ppermute | solution.py:21
  157.5 4.8 %all-to-all-start.2 = ((f32[4,16,8,512]{3,2,0,1:T(8,128)}), f32[4,16,8,512]{3,2,0,1:T(8,128)S(1)}, u32[]{:S(2)}, u32[]{:S(2)}) async-start(f32[4,16,8,512]{3,2,0,1:T(8,128)} %copy.45), calls=%async_computation.2 | async-start | bytes 2097152 | tf_op jit(solution)/shard_map/all_to_all | solution.py:86
  162.5 13.7 %all-to-all-done.2 = f32[4,16,8,512]{3,2,0,1:T(8,128)S(1)} async-done(((f32[4,16,8,512]{3,2,0,1:T(8,128)}), f32[4,16,8,512]{3,2,0,1:T(8,128)S(1)}, u32[]{:S(2)}, u32[]{:S(2)}) %all-to-all-start.2) | async-done | bytes 1048608 | tf_op jit(solution)/shard_map/all_to_all | solution.py:86
  185.4 13.0 %gather_fusion = f32[4096,64]{1,0:T(8,128)S(1)} fusion(f32[8192,64]{1,0:T(8,128)} %bitcast.101, s32[4096]{0:T(1024)S(1)} %broadcast_clamp_fusion), kind=kCustom, calls=%fused_computation | custom fusion | bytes 2113536 | tf_op jit(solution)/shard_map/jit(_take)/gather | solution.py:95
  202.9 19.6 %all_to_all.70 = f32[8,1,32768]{2,1,0:T(1,128)S(1)} all-to-all(f32[8,1,32768]{2,1,0:T(1,128)} %reshape.1326), channel_id=1, replica_groups=mesh['zh'=4,'xl'=8,'gy'=16] {'xl'}, dimensions={0} | all-to-all | bytes 2097152 | tf_op jit(solution)/shard_map/all_to_all | solution.py:32
  222.9 4.5 %reduce.6 = f32[8,32768]{1,0:T(8,128)} reduce(f32[8,1,32768]{2,1,0:T(1,128)S(1)} %all_to_all.70, f32[]{:T(128)} %broadcast.1727), dimensions={1}, to_apply=%all_to_all.57.reduce_sub_computation | reduce | bytes 2097156 | tf_op jit(solution)/shard_map/all_to_all | solution.py:32
  229.9 27.8 %all_to_all.71 = f32[16,1,2048]{2,1,0:T(1,128)S(1)} all-to-all(f32[16,1,2048]{2,1,0:T(1,128)S(1)} %reshape.1328), channel_id=1, replica_groups=mesh['zh'=4,'xl'=8,'gy'=16] {'gy'}, dimensions={0} | all-to-all | bytes 262144 | tf_op jit(solution)/shard_map/all_to_all | solution.py:33
  258.9 17.3 %all_to_all.72 = f32[4,1,2048]{2,1,0:T(1,128)S(1)} all-to-all(f32[4,1,2048]{2,1,0:T(1,128)S(1)} %reshape.1330), channel_id=1, replica_groups=mesh['zh'=4,'xl'=8,'gy'=16] {'zh'}, dimensions={0} | all-to-all | bytes 65536 | tf_op jit(solution)/shard_map/all_to_all | solution.py:41
  277.7 8.0 %all_to_all.73 = f32[8,1,2048]{2,1,0:T(1,128)S(1)} all-to-all(f32[8,1,2048]{2,1,0:T(1,128)S(1)} %reshape.1332), channel_id=1, replica_groups=mesh['zh'=4,'xl'=8,'gy'=16] {'xl'}, dimensions={0} | all-to-all | bytes 131072 | tf_op jit(solution)/shard_map/all_to_all | solution.py:41
  287.6 3.5 %all-to-all-start.7 = ((f32[16,1,2048]{2,1,0:T(1,128)}), f32[16,1,2048]{2,1,0:T(1,128)S(1)}, u32[]{:S(2)}, u32[]{:S(2)}) async-start(f32[16,1,2048]{2,1,0:T(1,128)} %reshape.1334), calls=%async_computation.7 | async-start | bytes 262144 | tf_op jit(solution)/shard_map/all_to_all | solution.py:41
  292.7 6.8 %all-to-all-done.7 = f32[16,1,2048]{2,1,0:T(1,128)S(1)} async-done(((f32[16,1,2048]{2,1,0:T(1,128)}), f32[16,1,2048]{2,1,0:T(1,128)S(1)}, u32[]{:S(2)}, u32[]{:S(2)}) %all-to-all-start.7) | async-done | bytes 131104 | tf_op jit(solution)/shard_map/all_to_all | solution.py:41
  300.9 2.9 cholesky.17
  (118 shorter events, 69.3 us)
Async XLA Ops:
  1.4 11.9 %slice-start = ((s32[1,1,8192]{2,1,0:T(1,128)}), s32[1,1,4096]{2,1,0:T(1,128)S(1)}, s32[]{:S(2)}) async-start(s32[1,1,8192]{2,1,0:T(1,128)} %param.7), calls=%async_computation.8 | async-start | bytes 32768 | tf_op jit(solution)/shard_map/slice | solution.py:95
  1.4 11.9 %copy-start.1 = (s32[2,8,512]{2,1,0:T(8,128)S(1)}, s32[2,8,512]{2,1,0:T(8,128)}, u32[]{:S(2)}) copy-start(s32[2,8,512]{2,1,0:T(8,128)} %param.6) | copy-start | bytes 98308
  3.9 26.0 %all-to-all-start = ((f32[40,2,8,512]{3,2,1,0:T(8,128)}), f32[40,2,8,512]{3,2,1,0:T(8,128)S(1)}, u32[]{:S(2)}, u32[]{:S(2)}) async-start(f32[40,2,8,512]{3,2,1,0:T(8,128)} %bitcast.2), calls=%async_computation | async-start | bytes 2621440 | tf_op jit(solution)/shard_map/all_to_all | solution.py:77
  30.3 23.7 %collective-permute-start.2 = (f32[4,16,2,512]{3,2,1,0:T(2,128)S(1)}, f32[4,16,2,512]{3,2,1,0:T(2,128)S(1)}, u32[]{:S(2)}, u32[]{:S(2)}) collective-permute-start(f32[4,16,2,512]{3,2,1,0:T(2,128)S(1)} %get-tuple-element.34), channel_id=1, source_target_pairs={{0,1},{1,2},{2,3},{3,4},{4,5},{5,6},{6,7},{7,8},{8,9},{9,10},{10,1... | collective-permute-start | bytes 786440 | tf_op jit(solution)/shard_map/ppermute | solution.py:20
  31.6 22.4 %collective-permute-start.3 = (f32[4,16,2,512]{3,2,1,0:T(2,128)S(1)}, f32[4,16,2,512]{3,2,1,0:T(2,128)S(1)}, u32[]{:S(2)}, u32[]{:S(2)}) collective-permute-start(f32[4,16,2,512]{3,2,1,0:T(2,128)S(1)} %get-tuple-element.35), channel_id=1, source_target_pairs={{1,0},{2,1},{3,2},{4,3},{5,4},{6,5},{7,6},{8,7},{9,8},{10,9},{11,1... | collective-permute-start | bytes 786440 | tf_op jit(solution)/shard_map/ppermute | solution.py:21
  32.9 9.6 %collective-permute-start = (f32[4,2,8,512]{3,2,1,0:T(8,128)S(1)}, f32[4,2,8,512]{3,2,1,0:T(8,128)S(1)}, u32[]{:S(2)}, u32[]{:S(2)}) collective-permute-start(f32[4,2,8,512]{3,2,1,0:T(8,128)S(1)} %get-tuple-element.32), channel_id=1, source_target_pairs={{0,128},{128,256},{256,384},{1,129},{129,257},{257,385},{2,130},{1... | collective-permute-start | bytes 393224 | tf_op jit(solution)/shard_map/ppermute | solution.py:20
  40.0 13.9 %collective-permute-start.1 = (f32[4,2,8,512]{3,2,1,0:T(8,128)S(1)}, f32[4,2,8,512]{3,2,1,0:T(8,128)S(1)}, u32[]{:S(2)}, u32[]{:S(2)}) collective-permute-start(f32[4,2,8,512]{3,2,1,0:T(8,128)S(1)} %get-tuple-element.33), channel_id=1, source_target_pairs={{128,0},{256,128},{384,256},{129,1},{257,129},{385,257},{130,2},{2... | collective-permute-start | bytes 393224 | tf_op jit(solution)/shard_map/ppermute | solution.py:21
  56.6 30.2 %collective-permute-start.6 = (f32[4,16,2,512]{3,2,1,0:T(2,128)S(1)}, f32[4,16,2,512]{3,2,1,0:T(2,128)S(1)}, u32[]{:S(2)}, u32[]{:S(2)}) collective-permute-start(f32[4,16,2,512]{3,2,1,0:T(2,128)S(1)} %get-tuple-element.28), channel_id=1, source_target_pairs={{0,1},{1,2},{2,3},{3,4},{4,5},{5,6},{6,7},{7,8},{8,9},{9,10},{10,1... | collective-permute-start | bytes 786440 | tf_op jit(solution)/shard_map/ppermute | solution.py:20
  67.0 19.8 %collective-permute-start.7 = (f32[4,16,2,512]{3,2,1,0:T(2,128)S(1)}, f32[4,16,2,512]{3,2,1,0:T(2,128)S(1)}, u32[]{:S(2)}, u32[]{:S(2)}) collective-permute-start(f32[4,16,2,512]{3,2,1,0:T(2,128)S(1)} %get-tuple-element.29), channel_id=1, source_target_pairs={{1,0},{2,1},{3,2},{4,3},{5,4},{6,5},{7,6},{8,7},{9,8},{10,9},{11,1... | collective-permute-start | bytes 786440 | tf_op jit(solution)/shard_map/ppermute | solution.py:21
  68.3 10.2 %collective-permute-start.4 = (f32[4,2,8,512]{3,2,1,0:T(8,128)S(1)}, f32[4,2,8,512]{3,2,1,0:T(8,128)S(1)}, u32[]{:S(2)}, u32[]{:S(2)}) collective-permute-start(f32[4,2,8,512]{3,2,1,0:T(8,128)S(1)} %get-tuple-element.30), channel_id=1, source_target_pairs={{0,128},{128,256},{256,384},{1,129},{129,257},{257,385},{2,130},{1... | collective-permute-start | bytes 393224 | tf_op jit(solution)/shard_map/ppermute | solution.py:20
  76.0 10.8 %collective-permute-start.5 = (f32[4,2,8,512]{3,2,1,0:T(8,128)S(1)}, f32[4,2,8,512]{3,2,1,0:T(8,128)S(1)}, u32[]{:S(2)}, u32[]{:S(2)}) collective-permute-start(f32[4,2,8,512]{3,2,1,0:T(8,128)S(1)} %get-tuple-element.31), channel_id=1, source_target_pairs={{128,0},{256,128},{384,256},{129,1},{257,129},{385,257},{130,2},{2... | collective-permute-start | bytes 393224 | tf_op jit(solution)/shard_map/ppermute | solution.py:21
  89.4 26.6 %collective-permute-start.10 = (f32[4,16,2,512]{3,2,1,0:T(2,128)S(1)}, f32[4,16,2,512]{3,2,1,0:T(2,128)S(1)}, u32[]{:S(2)}, u32[]{:S(2)}) collective-permute-start(f32[4,16,2,512]{3,2,1,0:T(2,128)S(1)} %get-tuple-element.24), channel_id=1, source_target_pairs={{0,1},{1,2},{2,3},{3,4},{4,5},{5,6},{6,7},{7,8},{8,9},{9,10},{10,1... | collective-permute-start | bytes 786440 | tf_op jit(solution)/shard_map/ppermute | solution.py:20
  101.0 15.8 %collective-permute-start.11 = (f32[4,16,2,512]{3,2,1,0:T(2,128)S(1)}, f32[4,16,2,512]{3,2,1,0:T(2,128)S(1)}, u32[]{:S(2)}, u32[]{:S(2)}) collective-permute-start(f32[4,16,2,512]{3,2,1,0:T(2,128)S(1)} %get-tuple-element.25), channel_id=1, source_target_pairs={{1,0},{2,1},{3,2},{4,3},{5,4},{6,5},{7,6},{8,7},{9,8},{10,9},{11,1... | collective-permute-start | bytes 786440 | tf_op jit(solution)/shard_map/ppermute | solution.py:21
  102.3 5.2 %collective-permute-start.8 = (f32[4,2,8,512]{3,2,1,0:T(8,128)S(1)}, f32[4,2,8,512]{3,2,1,0:T(8,128)S(1)}, u32[]{:S(2)}, u32[]{:S(2)}) collective-permute-start(f32[4,2,8,512]{3,2,1,0:T(8,128)S(1)} %get-tuple-element.26), channel_id=1, source_target_pairs={{0,128},{128,256},{256,384},{1,129},{129,257},{257,385},{2,130},{1... | collective-permute-start | bytes 393224 | tf_op jit(solution)/shard_map/ppermute | solution.py:20
  105.0 11.0 %collective-permute-start.9 = (f32[4,2,8,512]{3,2,1,0:T(8,128)S(1)}, f32[4,2,8,512]{3,2,1,0:T(8,128)S(1)}, u32[]{:S(2)}, u32[]{:S(2)}) collective-permute-start(f32[4,2,8,512]{3,2,1,0:T(8,128)S(1)} %get-tuple-element.27), channel_id=1, source_target_pairs={{128,0},{256,128},{384,256},{129,1},{257,129},{385,257},{130,2},{2... | collective-permute-start | bytes 393224 | tf_op jit(solution)/shard_map/ppermute | solution.py:21
  120.5 33.3 %collective-permute-start.14 = (f32[4,16,2,512]{3,2,1,0:T(2,128)S(1)}, f32[4,16,2,512]{3,2,1,0:T(2,128)S(1)}, u32[]{:S(2)}, u32[]{:S(2)}) collective-permute-start(f32[4,16,2,512]{3,2,1,0:T(2,128)S(1)} %get-tuple-element.20), channel_id=1, source_target_pairs={{0,1},{1,2},{2,3},{3,4},{4,5},{5,6},{6,7},{7,8},{8,9},{9,10},{10,1... | collective-permute-start | bytes 786440 | tf_op jit(solution)/shard_map/ppermute | solution.py:20
  128.6 25.3 %collective-permute-start.15 = (f32[4,16,2,512]{3,2,1,0:T(2,128)S(1)}, f32[4,16,2,512]{3,2,1,0:T(2,128)S(1)}, u32[]{:S(2)}, u32[]{:S(2)}) collective-permute-start(f32[4,16,2,512]{3,2,1,0:T(2,128)S(1)} %get-tuple-element.21), channel_id=1, source_target_pairs={{1,0},{2,1},{3,2},{4,3},{5,4},{6,5},{7,6},{8,7},{9,8},{10,9},{11,1... | collective-permute-start | bytes 786440 | tf_op jit(solution)/shard_map/ppermute | solution.py:21
  129.9 27.7 %all-to-all-start.1 = ((f32[4,16,8,512]{3,2,0,1:T(8,128)}), f32[4,16,8,512]{3,2,0,1:T(8,128)S(1)}, u32[]{:S(2)}, u32[]{:S(2)}) async-start(f32[4,16,8,512]{3,2,0,1:T(8,128)} %copy.43), calls=%async_computation.1 | async-start | bytes 2097152 | tf_op jit(solution)/shard_map/all_to_all | solution.py:85
  136.2 9.0 %collective-permute-start.12 = (f32[4,2,8,512]{3,2,1,0:T(8,128)}, f32[4,2,8,512]{3,2,1,0:T(8,128)}, u32[]{:S(2)}, u32[]{:S(2)}) collective-permute-start(f32[4,2,8,512]{3,2,1,0:T(8,128)} %get-tuple-element.22), channel_id=1, source_target_pairs={{0,128},{128,256},{256,384},{1,129},{129,257},{257,385},{2,130},{1... | collective-permute-start | bytes 393224 | tf_op jit(solution)/shard_map/ppermute | solution.py:20
  142.4 11.4 %collective-permute-start.13 = (f32[4,2,8,512]{3,2,1,0:T(8,128)}, f32[4,2,8,512]{3,2,1,0:T(8,128)}, u32[]{:S(2)}, u32[]{:S(2)}) collective-permute-start(f32[4,2,8,512]{3,2,1,0:T(8,128)} %get-tuple-element.23), channel_id=1, source_target_pairs={{128,0},{256,128},{384,256},{129,1},{257,129},{385,257},{130,2},{2... | collective-permute-start | bytes 393224 | tf_op jit(solution)/shard_map/ppermute | solution.py:21
  156.4 5.9 %copy-start = (s32[1,1,8192]{2,1,0:T(1,128)S(1)}, s32[1,1,8192]{2,1,0:T(1,128)}, u32[]{:S(2)}) copy-start(s32[1,1,8192]{2,1,0:T(1,128)} %param.7) | copy-start | bytes 98308
  157.5 18.7 %all-to-all-start.2 = ((f32[4,16,8,512]{3,2,0,1:T(8,128)}), f32[4,16,8,512]{3,2,0,1:T(8,128)S(1)}, u32[]{:S(2)}, u32[]{:S(2)}) async-start(f32[4,16,8,512]{3,2,0,1:T(8,128)} %copy.45), calls=%async_computation.2 | async-start | bytes 2097152 | tf_op jit(solution)/shard_map/all_to_all | solution.py:86
  287.6 11.9 %all-to-all-start.7 = ((f32[16,1,2048]{2,1,0:T(1,128)}), f32[16,1,2048]{2,1,0:T(1,128)S(1)}, u32[]{:S(2)}, u32[]{:S(2)}) async-start(f32[16,1,2048]{2,1,0:T(1,128)} %reshape.1334), calls=%async_computation.7 | async-start | bytes 262144 | tf_op jit(solution)/shard_map/all_to_all | solution.py:41

commit v9 on v8

--- a/solution.py
+++ b/solution.py
@@ -89,8 +89,8 @@
     stacked = jnp.concatenate([filtered, applied], axis=0)
     sign_block = (2 * sign_bits - 1).astype(jnp.float32)
     flat = (stacked * sign_block[None]).reshape(2 * count, -1, 128)
-    mixed = jnp.einsum("nac,cd->nad", flat, hadamard_table(128), precision=HIGHEST)
-    mixed = jnp.einsum("ba,nac->bcn", hadamard_table(cells // 128), mixed, precision=HIGHEST)
+    mixed = jnp.einsum("nac,cd->adn", flat, hadamard_table(128), precision=HIGHEST)
+    mixed = jnp.einsum("ba,adn->bdn", hadamard_table(cells // 128), mixed, precision=HIGHEST)
     mixed = mixed.reshape(cells, 2 * count)
     picked = jnp.take(mixed, sampled_rows[0, 0, :M], axis=0).T
     devices = lax.axis_size("zh") * lax.axis_size("xl") * lax.axis_size("gy")

time: 314 us -> 314 us (level)
  no operation moved by 1% of the time
where the time goes in v9:
time: 314 us; the launch traced here: 312 us
  starting transfers between devices  88.7 us (28%)
  waiting for transfers between devices  79.7 us (25%)
  blocking collectives  72.6 us (23%)
  local copies, waits for them, and re-layouts  32.9 us (10%)
  other arithmetic  30.1 us (10%)
  matrix products  6.56 us (2%)
    ppermute x8, starting transfers between devices, halos(): before = lax.ppermute(last, axis, up)  55.1 us
    ppermute x8, waiting for transfers between devices, halos(): after = lax.ppermute(initial, axis, down)  37.6 us
    all_to_all x1, blocking collectives, exchange_scatter(): y = lax.all_to_all(y.transpose(0, 2, 1, 3), 'gy', 1, 1, tiled=True).sum(1)  27.8 us
    all_to_all x2, blocking collectives, exchange_sum(): x = lax.all_to_all(copies, axis, 0, 0, tiled=True).sum(0)  25.3 us
    all_to_all x1, blocking collectives, exchange_scatter(): y = lax.all_to_all(y, 'xl', 1, 1, tiled=True).sum(1)  19.6 us
    all_to_all x1, waiting for transfers between devices, shards(): both = lax.all_to_all(both, 'xl', 0, 1, tiled=True)  16.6 us
    all_to_all x1, waiting for transfers between devices, shards(): applied = lax.all_to_all(spread_applied, 'xl', 1, 0, tiled=True)  13.7 us
    gather x1, local copies, waits for them, and re-layouts, shards(): picked = jnp.take(mixed, sampled_rows[0, 0, :M], axis=0).T  13 us
  transfers between devices with their start and end apart: 20, of which 12 were waited for; matrix products, arithmetic and copies ran while one was open for 2% of the time, Pallas kernels for 0%

profile of v9, /device:TPU:6, one launch (start us, length us, event | category | flops | bytes accessed | tf_op | source)
XLA Modules:
  0.0 311.9 jit_solution(13475877894528569851)
XLA Ops:
  3.9 9.4 %all-to-all-start = ((f32[40,2,8,512]{3,2,1,0:T(8,128)}), f32[40,2,8,512]{3,2,1,0:T(8,128)S(1)}, u32[]{:S(2)}, u32[]{:S(2)}) async-start(f32[40,2,8,512]{3,2,1,0:T(8,128)} %bitcast.4), calls=%async_computation | async-start | bytes 2621440 | tf_op jit(solution)/shard_map/all_to_all | solution.py:77
  13.3 16.6 %all-to-all-done = f32[40,2,8,512]{3,2,1,0:T(8,128)S(1)} async-done(((f32[40,2,8,512]{3,2,1,0:T(8,128)}), f32[40,2,8,512]{3,2,1,0:T(8,128)S(1)}, u32[]{:S(2)}, u32[]{:S(2)}) %all-to-all-start) | async-done | bytes 1310752 | tf_op jit(solution)/shard_map/all_to_all | solution.py:77
  32.9 7.1 %collective-permute-start = (f32[4,2,8,512]{3,2,1,0:T(8,128)S(1)}, f32[4,2,8,512]{3,2,1,0:T(8,128)S(1)}, u32[]{:S(2)}, u32[]{:S(2)}) collective-permute-start(f32[4,2,8,512]{3,2,1,0:T(8,128)S(1)} %get-tuple-element.32), channel_id=1, source_target_pairs={{0,128},{128,256},{256,384},{1,129},{129,257},{257,385},{2,130},{1... | collective-permute-start | bytes 393224 | tf_op jit(solution)/shard_map/ppermute | solution.py:20
  42.5 11.5 %collective-permute-done.1 = f32[4,2,8,512]{3,2,1,0:T(8,128)S(1)} collective-permute-done((f32[4,2,8,512]{3,2,1,0:T(8,128)S(1)}, f32[4,2,8,512]{3,2,1,0:T(8,128)S(1)}, u32[]{:S(2)}, u32[]{:S(2)}) %collective-permute-start.1) | collective-permute-done | bytes 131104 | tf_op jit(solution)/shard_map/ppermute | solution.py:21
  56.6 10.4 %collective-permute-start.6 = (f32[4,16,2,512]{3,2,1,0:T(2,128)S(1)}, f32[4,16,2,512]{3,2,1,0:T(2,128)S(1)}, u32[]{:S(2)}, u32[]{:S(2)}) collective-permute-start(f32[4,16,2,512]{3,2,1,0:T(2,128)S(1)} %get-tuple-element.28), channel_id=1, source_target_pairs={{0,1},{1,2},{2,3},{3,4},{4,5},{5,6},{6,7},{7,8},{8,9},{9,10},{10,1... | collective-permute-start | bytes 786440 | tf_op jit(solution)/shard_map/ppermute | solution.py:20
  68.3 7.7 %collective-permute-start.4 = (f32[4,2,8,512]{3,2,1,0:T(8,128)S(1)}, f32[4,2,8,512]{3,2,1,0:T(8,128)S(1)}, u32[]{:S(2)}, u32[]{:S(2)}) collective-permute-start(f32[4,2,8,512]{3,2,1,0:T(8,128)S(1)} %get-tuple-element.30), channel_id=1, source_target_pairs={{0,128},{128,256},{256,384},{1,129},{129,257},{257,385},{2,130},{1... | collective-permute-start | bytes 393224 | tf_op jit(solution)/shard_map/ppermute | solution.py:20
  78.5 8.3 %collective-permute-done.5 = f32[4,2,8,512]{3,2,1,0:T(8,128)S(1)} collective-permute-done((f32[4,2,8,512]{3,2,1,0:T(8,128)S(1)}, f32[4,2,8,512]{3,2,1,0:T(8,128)S(1)}, u32[]{:S(2)}, u32[]{:S(2)}) %collective-permute-start.5) | collective-permute-done | bytes 131104 | tf_op jit(solution)/shard_map/ppermute | solution.py:21
  89.4 11.6 %collective-permute-start.10 = (f32[4,16,2,512]{3,2,1,0:T(2,128)S(1)}, f32[4,16,2,512]{3,2,1,0:T(2,128)S(1)}, u32[]{:S(2)}, u32[]{:S(2)}) collective-permute-start(f32[4,16,2,512]{3,2,1,0:T(2,128)S(1)} %get-tuple-element.24), channel_id=1, source_target_pairs={{0,1},{1,2},{2,3},{3,4},{4,5},{5,6},{6,7},{7,8},{8,9},{9,10},{10,1... | collective-permute-start | bytes 786440 | tf_op jit(solution)/shard_map/ppermute | solution.py:20
  107.5 8.5 %collective-permute-done.9 = f32[4,2,8,512]{3,2,1,0:T(8,128)S(1)} collective-permute-done((f32[4,2,8,512]{3,2,1,0:T(8,128)S(1)}, f32[4,2,8,512]{3,2,1,0:T(8,128)S(1)}, u32[]{:S(2)}, u32[]{:S(2)}) %collective-permute-start.9) | collective-permute-done | bytes 131104 | tf_op jit(solution)/shard_map/ppermute | solution.py:21
  120.5 8.1 %collective-permute-start.14 = (f32[4,16,2,512]{3,2,1,0:T(2,128)S(1)}, f32[4,16,2,512]{3,2,1,0:T(2,128)S(1)}, u32[]{:S(2)}, u32[]{:S(2)}) collective-permute-start(f32[4,16,2,512]{3,2,1,0:T(2,128)S(1)} %get-tuple-element.20), channel_id=1, source_target_pairs={{0,1},{1,2},{2,3},{3,4},{4,5},{5,6},{6,7},{7,8},{8,9},{9,10},{10,1... | collective-permute-start | bytes 786440 | tf_op jit(solution)/shard_map/ppermute | solution.py:20
  129.9 5.6 %all-to-all-start.1 = ((f32[4,16,8,512]{3,2,0,1:T(8,128)}), f32[4,16,8,512]{3,2,0,1:T(8,128)S(1)}, u32[]{:S(2)}, u32[]{:S(2)}) async-start(f32[4,16,8,512]{3,2,0,1:T(8,128)} %copy.43), calls=%async_computation.1 | async-start | bytes 2097152 | tf_op jit(solution)/shard_map/all_to_all | solution.py:85
  136.2 6.3 %collective-permute-start.12 = (f32[4,2,8,512]{3,2,1,0:T(8,128)}, f32[4,2,8,512]{3,2,1,0:T(8,128)}, u32[]{:S(2)}, u32[]{:S(2)}) collective-permute-start(f32[4,2,8,512]{3,2,1,0:T(8,128)} %get-tuple-element.22), channel_id=1, source_target_pairs={{0,128},{128,256},{256,384},{1,129},{129,257},{257,385},{2,130},{1... | collective-permute-start | bytes 393224 | tf_op jit(solution)/shard_map/ppermute | solution.py:20
  145.1 8.7 %collective-permute-done.13 = f32[4,2,8,512]{3,2,1,0:T(8,128)} collective-permute-done((f32[4,2,8,512]{3,2,1,0:T(8,128)}, f32[4,2,8,512]{3,2,1,0:T(8,128)}, u32[]{:S(2)}, u32[]{:S(2)}) %collective-permute-start.13) | collective-permute-done | bytes 131104 | tf_op jit(solution)/shard_map/ppermute | solution.py:21
  157.5 4.8 %all-to-all-start.2 = ((f32[4,16,8,512]{3,2,0,1:T(8,128)}), f32[4,16,8,512]{3,2,0,1:T(8,128)S(1)}, u32[]{:S(2)}, u32[]{:S(2)}) async-start(f32[4,16,8,512]{3,2,0,1:T(8,128)} %copy.45), calls=%async_computation.2 | async-start | bytes 2097152 | tf_op jit(solution)/shard_map/all_to_all | solution.py:86
  162.5 13.7 %all-to-all-done.2 = f32[4,16,8,512]{3,2,0,1:T(8,128)S(1)} async-done(((f32[4,16,8,512]{3,2,0,1:T(8,128)}), f32[4,16,8,512]{3,2,0,1:T(8,128)S(1)}, u32[]{:S(2)}, u32[]{:S(2)}) %all-to-all-start.2) | async-done | bytes 1048608 | tf_op jit(solution)/shard_map/all_to_all | solution.py:86
  185.3 13.0 %gather_fusion = f32[4096,64]{1,0:T(8,128)S(1)} fusion(f32[8192,64]{1,0:T(8,128)} %bitcast.101, s32[4096]{0:T(1024)S(1)} %broadcast_clamp_fusion), kind=kCustom, calls=%fused_computation | custom fusion | bytes 2113536 | tf_op jit(solution)/shard_map/jit(_take)/gather | solution.py:95
  202.8 19.6 %all_to_all.70 = f32[8,1,32768]{2,1,0:T(1,128)S(1)} all-to-all(f32[8,1,32768]{2,1,0:T(1,128)} %reshape.1326), channel_id=1, replica_groups=mesh['zh'=4,'xl'=8,'gy'=16] {'xl'}, dimensions={0} | all-to-all | bytes 2097152 | tf_op jit(solution)/shard_map/all_to_all | solution.py:32
  222.9 4.5 %reduce.6 = f32[8,32768]{1,0:T(8,128)} reduce(f32[8,1,32768]{2,1,0:T(1,128)S(1)} %all_to_all.70, f32[]{:T(128)} %broadcast.1727), dimensions={1}, to_apply=%all_to_all.57.reduce_sub_computation | reduce | bytes 2097156 | tf_op jit(solution)/shard_map/all_to_all | solution.py:32
  229.9 27.8 %all_to_all.71 = f32[16,1,2048]{2,1,0:T(1,128)S(1)} all-to-all(f32[16,1,2048]{2,1,0:T(1,128)S(1)} %reshape.1328), channel_id=1, replica_groups=mesh['zh'=4,'xl'=8,'gy'=16] {'gy'}, dimensions={0} | all-to-all | bytes 262144 | tf_op jit(solution)/shard_map/all_to_all | solution.py:33
  258.9 17.3 %all_to_all.72 = f32[4,1,2048]{2,1,0:T(1,128)S(1)} all-to-all(f32[4,1,2048]{2,1,0:T(1,128)S(1)} %reshape.1330), channel_id=1, replica_groups=mesh['zh'=4,'xl'=8,'gy'=16] {'zh'}, dimensions={0} | all-to-all | bytes 65536 | tf_op jit(solution)/shard_map/all_to_all | solution.py:41
  277.7 8.0 %all_to_all.73 = f32[8,1,2048]{2,1,0:T(1,128)S(1)} all-to-all(f32[8,1,2048]{2,1,0:T(1,128)S(1)} %reshape.1332), channel_id=1, replica_groups=mesh['zh'=4,'xl'=8,'gy'=16] {'xl'}, dimensions={0} | all-to-all | bytes 131072 | tf_op jit(solution)/shard_map/all_to_all | solution.py:41
  287.6 3.5 %all-to-all-start.7 = ((f32[16,1,2048]{2,1,0:T(1,128)}), f32[16,1,2048]{2,1,0:T(1,128)S(1)}, u32[]{:S(2)}, u32[]{:S(2)}) async-start(f32[16,1,2048]{2,1,0:T(1,128)} %reshape.1334), calls=%async_computation.7 | async-start | bytes 262144 | tf_op jit(solution)/shard_map/all_to_all | solution.py:41
  292.6 6.8 %all-to-all-done.7 = f32[16,1,2048]{2,1,0:T(1,128)S(1)} async-done(((f32[16,1,2048]{2,1,0:T(1,128)}), f32[16,1,2048]{2,1,0:T(1,128)S(1)}, u32[]{:S(2)}, u32[]{:S(2)}) %all-to-all-start.7) | async-done | bytes 131104 | tf_op jit(solution)/shard_map/all_to_all | solution.py:41
  300.8 2.9 cholesky.17
  (118 shorter events, 69.3 us)
Async XLA Ops:
  1.4 11.9 %slice-start = ((s32[1,1,8192]{2,1,0:T(1,128)}), s32[1,1,4096]{2,1,0:T(1,128)S(1)}, s32[]{:S(2)}) async-start(s32[1,1,8192]{2,1,0:T(1,128)} %param.7), calls=%async_computation.8 | async-start | bytes 32768 | tf_op jit(solution)/shard_map/slice | solution.py:95
  1.4 11.9 %copy-start.1 = (s32[2,8,512]{2,1,0:T(8,128)S(1)}, s32[2,8,512]{2,1,0:T(8,128)}, u32[]{:S(2)}) copy-start(s32[2,8,512]{2,1,0:T(8,128)} %param.6) | copy-start | bytes 98308
  3.9 26.0 %all-to-all-start = ((f32[40,2,8,512]{3,2,1,0:T(8,128)}), f32[40,2,8,512]{3,2,1,0:T(8,128)S(1)}, u32[]{:S(2)}, u32[]{:S(2)}) async-start(f32[40,2,8,512]{3,2,1,0:T(8,128)} %bitcast.4), calls=%async_computation | async-start | bytes 2621440 | tf_op jit(solution)/shard_map/all_to_all | solution.py:77
  30.3 23.7 %collective-permute-start.2 = (f32[4,16,2,512]{3,2,1,0:T(2,128)S(1)}, f32[4,16,2,512]{3,2,1,0:T(2,128)S(1)}, u32[]{:S(2)}, u32[]{:S(2)}) collective-permute-start(f32[4,16,2,512]{3,2,1,0:T(2,128)S(1)} %get-tuple-element.34), channel_id=1, source_target_pairs={{0,1},{1,2},{2,3},{3,4},{4,5},{5,6},{6,7},{7,8},{8,9},{9,10},{10,1... | collective-permute-start | bytes 786440 | tf_op jit(solution)/shard_map/ppermute | solution.py:20
  31.6 22.4 %collective-permute-start.3 = (f32[4,16,2,512]{3,2,1,0:T(2,128)S(1)}, f32[4,16,2,512]{3,2,1,0:T(2,128)S(1)}, u32[]{:S(2)}, u32[]{:S(2)}) collective-permute-start(f32[4,16,2,512]{3,2,1,0:T(2,128)S(1)} %get-tuple-element.35), channel_id=1, source_target_pairs={{1,0},{2,1},{3,2},{4,3},{5,4},{6,5},{7,6},{8,7},{9,8},{10,9},{11,1... | collective-permute-start | bytes 786440 | tf_op jit(solution)/shard_map/ppermute | solution.py:21
  32.9 9.6 %collective-permute-start = (f32[4,2,8,512]{3,2,1,0:T(8,128)S(1)}, f32[4,2,8,512]{3,2,1,0:T(8,128)S(1)}, u32[]{:S(2)}, u32[]{:S(2)}) collective-permute-start(f32[4,2,8,512]{3,2,1,0:T(8,128)S(1)} %get-tuple-element.32), channel_id=1, source_target_pairs={{0,128},{128,256},{256,384},{1,129},{129,257},{257,385},{2,130},{1... | collective-permute-start | bytes 393224 | tf_op jit(solution)/shard_map/ppermute | solution.py:20
  40.0 13.9 %collective-permute-start.1 = (f32[4,2,8,512]{3,2,1,0:T(8,128)S(1)}, f32[4,2,8,512]{3,2,1,0:T(8,128)S(1)}, u32[]{:S(2)}, u32[]{:S(2)}) collective-permute-start(f32[4,2,8,512]{3,2,1,0:T(8,128)S(1)} %get-tuple-element.33), channel_id=1, source_target_pairs={{128,0},{256,128},{384,256},{129,1},{257,129},{385,257},{130,2},{2... | collective-permute-start | bytes 393224 | tf_op jit(solution)/shard_map/ppermute | solution.py:21
  56.6 30.2 %collective-permute-start.6 = (f32[4,16,2,512]{3,2,1,0:T(2,128)S(1)}, f32[4,16,2,512]{3,2,1,0:T(2,128)S(1)}, u32[]{:S(2)}, u32[]{:S(2)}) collective-permute-start(f32[4,16,2,512]{3,2,1,0:T(2,128)S(1)} %get-tuple-element.28), channel_id=1, source_target_pairs={{0,1},{1,2},{2,3},{3,4},{4,5},{5,6},{6,7},{7,8},{8,9},{9,10},{10,1... | collective-permute-start | bytes 786440 | tf_op jit(solution)/shard_map/ppermute | solution.py:20
  67.0 19.8 %collective-permute-start.7 = (f32[4,16,2,512]{3,2,1,0:T(2,128)S(1)}, f32[4,16,2,512]{3,2,1,0:T(2,128)S(1)}, u32[]{:S(2)}, u32[]{:S(2)}) collective-permute-start(f32[4,16,2,512]{3,2,1,0:T(2,128)S(1)} %get-tuple-element.29), channel_id=1, source_target_pairs={{1,0},{2,1},{3,2},{4,3},{5,4},{6,5},{7,6},{8,7},{9,8},{10,9},{11,1... | collective-permute-start | bytes 786440 | tf_op jit(solution)/shard_map/ppermute | solution.py:21
  68.3 10.2 %collective-permute-start.4 = (f32[4,2,8,512]{3,2,1,0:T(8,128)S(1)}, f32[4,2,8,512]{3,2,1,0:T(8,128)S(1)}, u32[]{:S(2)}, u32[]{:S(2)}) collective-permute-start(f32[4,2,8,512]{3,2,1,0:T(8,128)S(1)} %get-tuple-element.30), channel_id=1, source_target_pairs={{0,128},{128,256},{256,384},{1,129},{129,257},{257,385},{2,130},{1... | collective-permute-start | bytes 393224 | tf_op jit(solution)/shard_map/ppermute | solution.py:20
  76.0 10.8 %collective-permute-start.5 = (f32[4,2,8,512]{3,2,1,0:T(8,128)S(1)}, f32[4,2,8,512]{3,2,1,0:T(8,128)S(1)}, u32[]{:S(2)}, u32[]{:S(2)}) collective-permute-start(f32[4,2,8,512]{3,2,1,0:T(8,128)S(1)} %get-tuple-element.31), channel_id=1, source_target_pairs={{128,0},{256,128},{384,256},{129,1},{257,129},{385,257},{130,2},{2... | collective-permute-start | bytes 393224 | tf_op jit(solution)/shard_map/ppermute | solution.py:21
  89.4 26.6 %collective-permute-start.10 = (f32[4,16,2,512]{3,2,1,0:T(2,128)S(1)}, f32[4,16,2,512]{3,2,1,0:T(2,128)S(1)}, u32[]{:S(2)}, u32[]{:S(2)}) collective-permute-start(f32[4,16,2,512]{3,2,1,0:T(2,128)S(1)} %get-tuple-element.24), channel_id=1, source_target_pairs={{0,1},{1,2},{2,3},{3,4},{4,5},{5,6},{6,7},{7,8},{8,9},{9,10},{10,1... | collective-permute-start | bytes 786440 | tf_op jit(solution)/shard_map/ppermute | solution.py:20
  101.0 15.8 %collective-permute-start.11 = (f32[4,16,2,512]{3,2,1,0:T(2,128)S(1)}, f32[4,16,2,512]{3,2,1,0:T(2,128)S(1)}, u32[]{:S(2)}, u32[]{:S(2)}) collective-permute-start(f32[4,16,2,512]{3,2,1,0:T(2,128)S(1)} %get-tuple-element.25), channel_id=1, source_target_pairs={{1,0},{2,1},{3,2},{4,3},{5,4},{6,5},{7,6},{8,7},{9,8},{10,9},{11,1... | collective-permute-start | bytes 786440 | tf_op jit(solution)/shard_map/ppermute | solution.py:21
  102.3 5.2 %collective-permute-start.8 = (f32[4,2,8,512]{3,2,1,0:T(8,128)S(1)}, f32[4,2,8,512]{3,2,1,0:T(8,128)S(1)}, u32[]{:S(2)}, u32[]{:S(2)}) collective-permute-start(f32[4,2,8,512]{3,2,1,0:T(8,128)S(1)} %get-tuple-element.26), channel_id=1, source_target_pairs={{0,128},{128,256},{256,384},{1,129},{129,257},{257,385},{2,130},{1... | collective-permute-start | bytes 393224 | tf_op jit(solution)/shard_map/ppermute | solution.py:20
  105.0 11.0 %collective-permute-start.9 = (f32[4,2,8,512]{3,2,1,0:T(8,128)S(1)}, f32[4,2,8,512]{3,2,1,0:T(8,128)S(1)}, u32[]{:S(2)}, u32[]{:S(2)}) collective-permute-start(f32[4,2,8,512]{3,2,1,0:T(8,128)S(1)} %get-tuple-element.27), channel_id=1, source_target_pairs={{128,0},{256,128},{384,256},{129,1},{257,129},{385,257},{130,2},{2... | collective-permute-start | bytes 393224 | tf_op jit(solution)/shard_map/ppermute | solution.py:21
  120.5 33.3 %collective-permute-start.14 = (f32[4,16,2,512]{3,2,1,0:T(2,128)S(1)}, f32[4,16,2,512]{3,2,1,0:T(2,128)S(1)}, u32[]{:S(2)}, u32[]{:S(2)}) collective-permute-start(f32[4,16,2,512]{3,2,1,0:T(2,128)S(1)} %get-tuple-element.20), channel_id=1, source_target_pairs={{0,1},{1,2},{2,3},{3,4},{4,5},{5,6},{6,7},{7,8},{8,9},{9,10},{10,1... | collective-permute-start | bytes 786440 | tf_op jit(solution)/shard_map/ppermute | solution.py:20
  128.6 25.3 %collective-permute-start.15 = (f32[4,16,2,512]{3,2,1,0:T(2,128)S(1)}, f32[4,16,2,512]{3,2,1,0:T(2,128)S(1)}, u32[]{:S(2)}, u32[]{:S(2)}) collective-permute-start(f32[4,16,2,512]{3,2,1,0:T(2,128)S(1)} %get-tuple-element.21), channel_id=1, source_target_pairs={{1,0},{2,1},{3,2},{4,3},{5,4},{6,5},{7,6},{8,7},{9,8},{10,9},{11,1... | collective-permute-start | bytes 786440 | tf_op jit(solution)/shard_map/ppermute | solution.py:21
  129.9 27.7 %all-to-all-start.1 = ((f32[4,16,8,512]{3,2,0,1:T(8,128)}), f32[4,16,8,512]{3,2,0,1:T(8,128)S(1)}, u32[]{:S(2)}, u32[]{:S(2)}) async-start(f32[4,16,8,512]{3,2,0,1:T(8,128)} %copy.43), calls=%async_computation.1 | async-start | bytes 2097152 | tf_op jit(solution)/shard_map/all_to_all | solution.py:85
  136.2 9.0 %collective-permute-start.12 = (f32[4,2,8,512]{3,2,1,0:T(8,128)}, f32[4,2,8,512]{3,2,1,0:T(8,128)}, u32[]{:S(2)}, u32[]{:S(2)}) collective-permute-start(f32[4,2,8,512]{3,2,1,0:T(8,128)} %get-tuple-element.22), channel_id=1, source_target_pairs={{0,128},{128,256},{256,384},{1,129},{129,257},{257,385},{2,130},{1... | collective-permute-start | bytes 393224 | tf_op jit(solution)/shard_map/ppermute | solution.py:20
  142.4 11.4 %collective-permute-start.13 = (f32[4,2,8,512]{3,2,1,0:T(8,128)}, f32[4,2,8,512]{3,2,1,0:T(8,128)}, u32[]{:S(2)}, u32[]{:S(2)}) collective-permute-start(f32[4,2,8,512]{3,2,1,0:T(8,128)} %get-tuple-element.23), channel_id=1, source_target_pairs={{128,0},{256,128},{384,256},{129,1},{257,129},{385,257},{130,2},{2... | collective-permute-start | bytes 393224 | tf_op jit(solution)/shard_map/ppermute | solution.py:21
  156.4 5.9 %copy-start = (s32[1,1,8192]{2,1,0:T(1,128)S(1)}, s32[1,1,8192]{2,1,0:T(1,128)}, u32[]{:S(2)}) copy-start(s32[1,1,8192]{2,1,0:T(1,128)} %param.7) | copy-start | bytes 98308
  157.5 18.7 %all-to-all-start.2 = ((f32[4,16,8,512]{3,2,0,1:T(8,128)}), f32[4,16,8,512]{3,2,0,1:T(8,128)S(1)}, u32[]{:S(2)}, u32[]{:S(2)}) async-start(f32[4,16,8,512]{3,2,0,1:T(8,128)} %copy.45), calls=%async_computation.2 | async-start | bytes 2097152 | tf_op jit(solution)/shard_map/all_to_all | solution.py:86
  287.6 11.9 %all-to-all-start.7 = ((f32[16,1,2048]{2,1,0:T(1,128)}), f32[16,1,2048]{2,1,0:T(1,128)S(1)}, u32[]{:S(2)}, u32[]{:S(2)}) async-start(f32[16,1,2048]{2,1,0:T(1,128)} %reshape.1334), calls=%async_computation.7 | async-start | bytes 262144 | tf_op jit(solution)/shard_map/all_to_all | solution.py:41

commit v10 on v9

--- a/solution.py
+++ b/solution.py
@@ -23,15 +23,6 @@
 
 
 BLOCK_AXES = ("zh", "xl", "gy")
-
-
-def exchange_scatter(x):
-    n = x.shape[0]
-    zh, xl, gy = (lax.axis_size(axis) for axis in BLOCK_AXES)
-    y = x.reshape(n, zh, xl, gy, -1).transpose(0, 2, 1, 3, 4)
-    y = lax.all_to_all(y, "xl", 1, 1, tiled=True).sum(1)
-    y = lax.all_to_all(y.transpose(0, 2, 1, 3), "gy", 1, 1, tiled=True).sum(1)
-    return exchange_sum(y, ("zh",))
 
 
 def exchange_sum(x, axes):
@@ -92,10 +83,14 @@
     mixed = jnp.einsum("nac,cd->adn", flat, hadamard_table(128), precision=HIGHEST)
     mixed = jnp.einsum("ba,adn->bdn", hadamard_table(cells // 128), mixed, precision=HIGHEST)
     mixed = mixed.reshape(cells, 2 * count)
-    picked = jnp.take(mixed, sampled_rows[0, 0, :M], axis=0).T
-    devices = lax.axis_size("zh") * lax.axis_size("xl") * lax.axis_size("gy")
-    term = (picked / jnp.sqrt(jnp.float32(M * devices))).reshape(2, count, M)
-    summed = exchange_scatter(term.reshape(2 * count, M))
+    zh, xl, gy = (lax.axis_size(axis) for axis in BLOCK_AXES)
+    order = sampled_rows[0, 0, :M].reshape(zh, xl, gy, -1).transpose(1, 0, 2, 3).reshape(-1)
+    devices = zh * xl * gy
+    picked = jnp.take(mixed, order, axis=0) / jnp.sqrt(jnp.float32(M * devices))
+    y = lax.all_to_all(picked.reshape(xl, -1, 2 * count), "xl", 0, 0, tiled=True).sum(0)
+    y = y.reshape(zh, gy, -1, 2 * count).transpose(1, 0, 2, 3)
+    y = lax.all_to_all(y, "gy", 0, 0, tiled=True).sum(0)
+    summed = exchange_sum(y, ("zh",)).transpose(2, 0, 1)
     share = lax.dynamic_index_in_dim(summed, lax.axis_index("zh"), 1, keepdims=False)
     share = share.reshape(2, count, -1)
     both = summed.reshape(2, count, -1)

time: 314 us -> 306 us (0.975)
  waiting for transfers between devices: 79.7 us -> 73.7 us
    all_to_all x2 -> x1, other arithmetic: 5.45 us -> 0.95 us  [shards(): y = lax.all_to_all(y, 'gy', 0, 0, tiled=True).sum(0)]
    unnamed x19 -> x39, local copies, waits for them, and re-layouts: 8.86 us -> 4.69 us
    select_n x7, other arithmetic: 0.03 us -> 3.44 us  [hadamard_table(): index[:, None] // weight % 2 * (index[None, :] // weight % 2)]
    gather x1 -> x2, local copies, waits for them, and re-layouts: 13 us -> 14.5 us  [shards(): picked = jnp.take(mixed, order, axis=0) / jnp.sqrt(jnp.float32(M * devices))]
  transfers between devices with their start and end apart: 20 -> 20, of which waited for: 12 -> 11; matrix products, arithmetic and copies ran while one was open for 2% -> 4% of each run, Pallas kernels for 0% -> 0%
where the time goes in v10:
time: 306 us; the launch traced here: 304 us
  starting transfers between devices  88.4 us (29%)
  waiting for transfers between devices  73.7 us (24%)
  blocking collectives  72.2 us (24%)
  local copies, waits for them, and re-layouts  32.2 us (11%)
  other arithmetic  29.4 us (10%)
  matrix products  6.56 us (2%)
    ppermute x8, starting transfers between devices, halos(): before = lax.ppermute(last, axis, up)  54.5 us
    ppermute x8, waiting for transfers between devices, halos(): after = lax.ppermute(initial, axis, down)  37 us
    all_to_all x1, blocking collectives, shards(): y = lax.all_to_all(y, 'gy', 0, 0, tiled=True).sum(0)  27.8 us
    all_to_all x2, blocking collectives, exchange_sum(): x = lax.all_to_all(copies, axis, 0, 0, tiled=True).sum(0)  25.9 us
    all_to_all x1, blocking collectives, shards(): lax.all_to_all(picked.reshape(xl, -1, 2 * count), 'xl', 0, 0, tiled=True)  18.5 us
    gather x2, local copies, waits for them, and re-layouts, shards(): picked = jnp.take(mixed, order, axis=0) / jnp.sqrt(jnp.float32(M * devices))  14.5 us
    all_to_all x1, waiting for transfers between devices, shards(): both = lax.all_to_all(both, 'xl', 0, 1, tiled=True)  14.5 us
    all_to_all x1, waiting for transfers between devices, shards(): applied = lax.all_to_all(spread_applied, 'xl', 1, 0, tiled=True)  13.7 us
  transfers between devices with their start and end apart: 20, of which 11 were waited for; matrix products, arithmetic and copies ran while one was open for 4% of the time, Pallas kernels for 0%

profile of v10, /device:TPU:6, one launch (start us, length us, event | category | flops | bytes accessed | tf_op | source)
XLA Modules:
  0.0 303.8 jit_solution(5427824300683340624)
XLA Ops:
  3.9 9.5 %all-to-all-start = ((f32[40,2,8,512]{3,2,1,0:T(8,128)}), f32[40,2,8,512]{3,2,1,0:T(8,128)S(1)}, u32[]{:S(2)}, u32[]{:S(2)}) async-start(f32[40,2,8,512]{3,2,1,0:T(8,128)} %bitcast.4), calls=%async_computation | async-start | bytes 2621440 | tf_op jit(solution)/shard_map/all_to_all | solution.py:68
  15.6 14.5 %all-to-all-done = f32[40,2,8,512]{3,2,1,0:T(8,128)S(1)} async-done(((f32[40,2,8,512]{3,2,1,0:T(8,128)}), f32[40,2,8,512]{3,2,1,0:T(8,128)S(1)}, u32[]{:S(2)}, u32[]{:S(2)}) %all-to-all-start) | async-done | bytes 1310752 | tf_op jit(solution)/shard_map/all_to_all | solution.py:68
  33.1 7.1 %collective-permute-start = (f32[4,2,8,512]{3,2,1,0:T(8,128)S(1)}, f32[4,2,8,512]{3,2,1,0:T(8,128)S(1)}, u32[]{:S(2)}, u32[]{:S(2)}) collective-permute-start(f32[4,2,8,512]{3,2,1,0:T(8,128)S(1)} %get-tuple-element.38), channel_id=1, source_target_pairs={{0,128},{128,256},{256,384},{1,129},{129,257},{257,385},{2,130},{1... | collective-permute-start | bytes 393224 | tf_op jit(solution)/shard_map/ppermute | solution.py:20
  42.6 11.4 %collective-permute-done.1 = f32[4,2,8,512]{3,2,1,0:T(8,128)S(1)} collective-permute-done((f32[4,2,8,512]{3,2,1,0:T(8,128)S(1)}, f32[4,2,8,512]{3,2,1,0:T(8,128)S(1)}, u32[]{:S(2)}, u32[]{:S(2)}) %collective-permute-start.1) | collective-permute-done | bytes 131104 | tf_op jit(solution)/shard_map/ppermute | solution.py:21
  56.7 10.4 %collective-permute-start.6 = (f32[4,16,2,512]{3,2,1,0:T(2,128)S(1)}, f32[4,16,2,512]{3,2,1,0:T(2,128)S(1)}, u32[]{:S(2)}, u32[]{:S(2)}) collective-permute-start(f32[4,16,2,512]{3,2,1,0:T(2,128)S(1)} %get-tuple-element.34), channel_id=1, source_target_pairs={{0,1},{1,2},{2,3},{3,4},{4,5},{5,6},{6,7},{7,8},{8,9},{9,10},{10,1... | collective-permute-start | bytes 786440 | tf_op jit(solution)/shard_map/ppermute | solution.py:20
  68.4 7.7 %collective-permute-start.4 = (f32[4,2,8,512]{3,2,1,0:T(8,128)S(1)}, f32[4,2,8,512]{3,2,1,0:T(8,128)S(1)}, u32[]{:S(2)}, u32[]{:S(2)}) collective-permute-start(f32[4,2,8,512]{3,2,1,0:T(8,128)S(1)} %get-tuple-element.36), channel_id=1, source_target_pairs={{0,128},{128,256},{256,384},{1,129},{129,257},{257,385},{2,130},{1... | collective-permute-start | bytes 393224 | tf_op jit(solution)/shard_map/ppermute | solution.py:20
  78.7 8.3 %collective-permute-done.5 = f32[4,2,8,512]{3,2,1,0:T(8,128)S(1)} collective-permute-done((f32[4,2,8,512]{3,2,1,0:T(8,128)S(1)}, f32[4,2,8,512]{3,2,1,0:T(8,128)S(1)}, u32[]{:S(2)}, u32[]{:S(2)}) %collective-permute-start.5) | collective-permute-done | bytes 131104 | tf_op jit(solution)/shard_map/ppermute | solution.py:21
  89.5 11.6 %collective-permute-start.10 = (f32[4,16,2,512]{3,2,1,0:T(2,128)S(1)}, f32[4,16,2,512]{3,2,1,0:T(2,128)S(1)}, u32[]{:S(2)}, u32[]{:S(2)}) collective-permute-start(f32[4,16,2,512]{3,2,1,0:T(2,128)S(1)} %get-tuple-element.30), channel_id=1, source_target_pairs={{0,1},{1,2},{2,3},{3,4},{4,5},{5,6},{6,7},{7,8},{8,9},{9,10},{10,1... | collective-permute-start | bytes 786440 | tf_op jit(solution)/shard_map/ppermute | solution.py:20
  107.7 8.5 %collective-permute-done.9 = f32[4,2,8,512]{3,2,1,0:T(8,128)S(1)} collective-permute-done((f32[4,2,8,512]{3,2,1,0:T(8,128)S(1)}, f32[4,2,8,512]{3,2,1,0:T(8,128)S(1)}, u32[]{:S(2)}, u32[]{:S(2)}) %collective-permute-start.9) | collective-permute-done | bytes 131104 | tf_op jit(solution)/shard_map/ppermute | solution.py:21
  121.3 8.1 %collective-permute-start.14 = (f32[4,16,2,512]{3,2,1,0:T(2,128)}, f32[4,16,2,512]{3,2,1,0:T(2,128)S(1)}, u32[]{:S(2)}, u32[]{:S(2)}) collective-permute-start(f32[4,16,2,512]{3,2,1,0:T(2,128)} %get-tuple-element.26), channel_id=1, source_target_pairs={{0,1},{1,2},{2,3},{3,4},{4,5},{5,6},{6,7},{7,8},{8,9},{9,10},{10,1... | collective-permute-start | bytes 786440 | tf_op jit(solution)/shard_map/ppermute | solution.py:20
  130.7 5.6 %all-to-all-start.1 = ((f32[4,16,8,512]{3,2,0,1:T(8,128)}), f32[4,16,8,512]{3,2,0,1:T(8,128)S(1)}, u32[]{:S(2)}, u32[]{:S(2)}) async-start(f32[4,16,8,512]{3,2,0,1:T(8,128)} %copy.80), calls=%async_computation.1 | async-start | bytes 2097152 | tf_op jit(solution)/shard_map/all_to_all | solution.py:76
  137.0 5.6 %collective-permute-start.12 = (f32[4,2,8,512]{3,2,1,0:T(8,128)}, f32[4,2,8,512]{3,2,1,0:T(8,128)S(1)}, u32[]{:S(2)}, u32[]{:S(2)}) collective-permute-start(f32[4,2,8,512]{3,2,1,0:T(8,128)} %get-tuple-element.28), channel_id=1, source_target_pairs={{0,128},{128,256},{256,384},{1,129},{129,257},{257,385},{2,130},{1... | collective-permute-start | bytes 393224 | tf_op jit(solution)/shard_map/ppermute | solution.py:20
  146.0 8.0 %collective-permute-done.13 = f32[4,2,8,512]{3,2,1,0:T(8,128)} collective-permute-done((f32[4,2,8,512]{3,2,1,0:T(8,128)}, f32[4,2,8,512]{3,2,1,0:T(8,128)}, u32[]{:S(2)}, u32[]{:S(2)}) %collective-permute-start.13) | collective-permute-done | bytes 131104 | tf_op jit(solution)/shard_map/ppermute | solution.py:21
  157.7 4.8 %all-to-all-start.2 = ((f32[4,16,8,512]{3,2,0,1:T(8,128)}), f32[4,16,8,512]{3,2,0,1:T(8,128)S(1)}, u32[]{:S(2)}, u32[]{:S(2)}) async-start(f32[4,16,8,512]{3,2,0,1:T(8,128)} %copy.82), calls=%async_computation.2 | async-start | bytes 2097152 | tf_op jit(solution)/shard_map/all_to_all | solution.py:77
  162.7 13.7 %all-to-all-done.2 = f32[4,16,8,512]{3,2,0,1:T(8,128)S(1)} async-done(((f32[4,16,8,512]{3,2,0,1:T(8,128)}), f32[4,16,8,512]{3,2,0,1:T(8,128)S(1)}, u32[]{:S(2)}, u32[]{:S(2)}) %all-to-all-start.2) | async-done | bytes 1048608 | tf_op jit(solution)/shard_map/all_to_all | solution.py:77
  183.0 2.8 copy.96
  185.7 13.0 %gather_fusion = f32[4096,64]{1,0:T(8,128)S(1)} fusion(f32[8192,64]{1,0:T(8,128)} %bitcast.86, s32[4096]{0:T(1024)S(1)} %broadcast_clamp_fusion), kind=kCustom, calls=%fused_computation | custom fusion | bytes 2113536 | tf_op jit(solution)/shard_map/jit(_take)/gather | solution.py:89
  201.7 18.5 %all_to_all.70 = f32[8,512,64]{1,2,0:T(8,128)S(1)} all-to-all(f32[8,512,64]{1,2,0:T(8,128)S(1)} %select_multiply_fusion), channel_id=1, replica_groups=mesh['zh'=4,'xl'=8,'gy'=16] {'xl'}, dimensions={0} | all-to-all | bytes 2097152 | tf_op jit(solution)/shard_map/all_to_all | solution.py:90
  220.6 27.8 %all_to_all.71 = f32[16,1,2048]{2,1,0:T(1,128)S(1)} all-to-all(f32[16,1,2048]{2,1,0:T(1,128)S(1)} %reshape.1351), channel_id=1, replica_groups=mesh['zh'=4,'xl'=8,'gy'=16] {'gy'}, dimensions={0} | all-to-all | bytes 262144 | tf_op jit(solution)/shard_map/all_to_all | solution.py:92
  250.2 17.9 %all_to_all.72 = f32[4,1,2048]{2,1,0:T(1,128)S(1)} all-to-all(f32[4,1,2048]{2,1,0:T(1,128)S(1)} %reshape.1353), channel_id=1, replica_groups=mesh['zh'=4,'xl'=8,'gy'=16] {'zh'}, dimensions={0} | all-to-all | bytes 65536 | tf_op jit(solution)/shard_map/all_to_all | solution.py:32
  269.6 8.0 %all_to_all.73 = f32[8,1,2048]{2,1,0:T(1,128)S(1)} all-to-all(f32[8,1,2048]{2,1,0:T(1,128)S(1)} %reshape.1355), channel_id=1, replica_groups=mesh['zh'=4,'xl'=8,'gy'=16] {'xl'}, dimensions={0} | all-to-all | bytes 131072 | tf_op jit(solution)/shard_map/all_to_all | solution.py:32
  279.5 3.7 %all-to-all-start.7 = ((f32[16,1,2048]{2,1,0:T(1,128)}), f32[16,1,2048]{2,1,0:T(1,128)S(1)}, u32[]{:S(2)}, u32[]{:S(2)}) async-start(f32[16,1,2048]{2,1,0:T(1,128)} %reshape.1357), calls=%async_computation.7 | async-start | bytes 262144 | tf_op jit(solution)/shard_map/all_to_all | solution.py:32
  284.8 6.6 %all-to-all-done.7 = f32[16,1,2048]{2,1,0:T(1,128)S(1)} async-done(((f32[16,1,2048]{2,1,0:T(1,128)}), f32[16,1,2048]{2,1,0:T(1,128)S(1)}, u32[]{:S(2)}, u32[]{:S(2)}) %all-to-all-start.7) | async-done | bytes 131104 | tf_op jit(solution)/shard_map/all_to_all | solution.py:32
  292.7 2.9 cholesky.17
  (143 shorter events, 66.6 us)
Async XLA Ops:
  1.4 12.0 %copy-start.2 = (s32[1,1,8192]{2,1,0:T(1,128)S(1)}, s32[1,1,8192]{2,1,0:T(1,128)}, u32[]{:S(2)}) copy-start(s32[1,1,8192]{2,1,0:T(1,128)} %param.7) | copy-start | bytes 98308
  3.9 11.1 %copy-start = (s32[2,8,512]{2,1,0:T(8,128)S(1)}, s32[2,8,512]{2,1,0:T(8,128)}, u32[]{:S(2)}) copy-start(s32[2,8,512]{2,1,0:T(8,128)} %param.6) | copy-start | bytes 98308
  3.9 26.2 %all-to-all-start = ((f32[40,2,8,512]{3,2,1,0:T(8,128)}), f32[40,2,8,512]{3,2,1,0:T(8,128)S(1)}, u32[]{:S(2)}, u32[]{:S(2)}) async-start(f32[40,2,8,512]{3,2,1,0:T(8,128)} %bitcast.4), calls=%async_computation | async-start | bytes 2621440 | tf_op jit(solution)/shard_map/all_to_all | solution.py:68
  30.4 23.7 %collective-permute-start.2 = (f32[4,16,2,512]{3,2,1,0:T(2,128)S(1)}, f32[4,16,2,512]{3,2,1,0:T(2,128)S(1)}, u32[]{:S(2)}, u32[]{:S(2)}) collective-permute-start(f32[4,16,2,512]{3,2,1,0:T(2,128)S(1)} %get-tuple-element.40), channel_id=1, source_target_pairs={{0,1},{1,2},{2,3},{3,4},{4,5},{5,6},{6,7},{7,8},{8,9},{9,10},{10,1... | collective-permute-start | bytes 786440 | tf_op jit(solution)/shard_map/ppermute | solution.py:20
  31.7 22.4 %collective-permute-start.3 = (f32[4,16,2,512]{3,2,1,0:T(2,128)S(1)}, f32[4,16,2,512]{3,2,1,0:T(2,128)S(1)}, u32[]{:S(2)}, u32[]{:S(2)}) collective-permute-start(f32[4,16,2,512]{3,2,1,0:T(2,128)S(1)} %get-tuple-element.41), channel_id=1, source_target_pairs={{1,0},{2,1},{3,2},{4,3},{5,4},{6,5},{7,6},{8,7},{9,8},{10,9},{11,1... | collective-permute-start | bytes 786440 | tf_op jit(solution)/shard_map/ppermute | solution.py:21
  33.1 9.6 %collective-permute-start = (f32[4,2,8,512]{3,2,1,0:T(8,128)S(1)}, f32[4,2,8,512]{3,2,1,0:T(8,128)S(1)}, u32[]{:S(2)}, u32[]{:S(2)}) collective-permute-start(f32[4,2,8,512]{3,2,1,0:T(8,128)S(1)} %get-tuple-element.38), channel_id=1, source_target_pairs={{0,128},{128,256},{256,384},{1,129},{129,257},{257,385},{2,130},{1... | collective-permute-start | bytes 393224 | tf_op jit(solution)/shard_map/ppermute | solution.py:20
  40.1 13.9 %collective-permute-start.1 = (f32[4,2,8,512]{3,2,1,0:T(8,128)S(1)}, f32[4,2,8,512]{3,2,1,0:T(8,128)S(1)}, u32[]{:S(2)}, u32[]{:S(2)}) collective-permute-start(f32[4,2,8,512]{3,2,1,0:T(8,128)S(1)} %get-tuple-element.39), channel_id=1, source_target_pairs={{128,0},{256,128},{384,256},{129,1},{257,129},{385,257},{130,2},{2... | collective-permute-start | bytes 393224 | tf_op jit(solution)/shard_map/ppermute | solution.py:21
  56.7 30.2 %collective-permute-start.6 = (f32[4,16,2,512]{3,2,1,0:T(2,128)S(1)}, f32[4,16,2,512]{3,2,1,0:T(2,128)S(1)}, u32[]{:S(2)}, u32[]{:S(2)}) collective-permute-start(f32[4,16,2,512]{3,2,1,0:T(2,128)S(1)} %get-tuple-element.34), channel_id=1, source_target_pairs={{0,1},{1,2},{2,3},{3,4},{4,5},{5,6},{6,7},{7,8},{8,9},{9,10},{10,1... | collective-permute-start | bytes 786440 | tf_op jit(solution)/shard_map/ppermute | solution.py:20
  67.1 19.8 %collective-permute-start.7 = (f32[4,16,2,512]{3,2,1,0:T(2,128)S(1)}, f32[4,16,2,512]{3,2,1,0:T(2,128)S(1)}, u32[]{:S(2)}, u32[]{:S(2)}) collective-permute-start(f32[4,16,2,512]{3,2,1,0:T(2,128)S(1)} %get-tuple-element.35), channel_id=1, source_target_pairs={{1,0},{2,1},{3,2},{4,3},{5,4},{6,5},{7,6},{8,7},{9,8},{10,9},{11,1... | collective-permute-start | bytes 786440 | tf_op jit(solution)/shard_map/ppermute | solution.py:21
  68.4 10.2 %collective-permute-start.4 = (f32[4,2,8,512]{3,2,1,0:T(8,128)S(1)}, f32[4,2,8,512]{3,2,1,0:T(8,128)S(1)}, u32[]{:S(2)}, u32[]{:S(2)}) collective-permute-start(f32[4,2,8,512]{3,2,1,0:T(8,128)S(1)} %get-tuple-element.36), channel_id=1, source_target_pairs={{0,128},{128,256},{256,384},{1,129},{129,257},{257,385},{2,130},{1... | collective-permute-start | bytes 393224 | tf_op jit(solution)/shard_map/ppermute | solution.py:20
  76.1 10.8 %collective-permute-start.5 = (f32[4,2,8,512]{3,2,1,0:T(8,128)S(1)}, f32[4,2,8,512]{3,2,1,0:T(8,128)S(1)}, u32[]{:S(2)}, u32[]{:S(2)}) collective-permute-start(f32[4,2,8,512]{3,2,1,0:T(8,128)S(1)} %get-tuple-element.37), channel_id=1, source_target_pairs={{128,0},{256,128},{384,256},{129,1},{257,129},{385,257},{130,2},{2... | collective-permute-start | bytes 393224 | tf_op jit(solution)/shard_map/ppermute | solution.py:21
  89.5 26.6 %collective-permute-start.10 = (f32[4,16,2,512]{3,2,1,0:T(2,128)S(1)}, f32[4,16,2,512]{3,2,1,0:T(2,128)S(1)}, u32[]{:S(2)}, u32[]{:S(2)}) collective-permute-start(f32[4,16,2,512]{3,2,1,0:T(2,128)S(1)} %get-tuple-element.30), channel_id=1, source_target_pairs={{0,1},{1,2},{2,3},{3,4},{4,5},{5,6},{6,7},{7,8},{8,9},{9,10},{10,1... | collective-permute-start | bytes 786440 | tf_op jit(solution)/shard_map/ppermute | solution.py:20
  101.1 15.8 %collective-permute-start.11 = (f32[4,16,2,512]{3,2,1,0:T(2,128)S(1)}, f32[4,16,2,512]{3,2,1,0:T(2,128)S(1)}, u32[]{:S(2)}, u32[]{:S(2)}) collective-permute-start(f32[4,16,2,512]{3,2,1,0:T(2,128)S(1)} %get-tuple-element.31), channel_id=1, source_target_pairs={{1,0},{2,1},{3,2},{4,3},{5,4},{6,5},{7,6},{8,7},{9,8},{10,9},{11,1... | collective-permute-start | bytes 786440 | tf_op jit(solution)/shard_map/ppermute | solution.py:21
  102.4 5.2 %collective-permute-start.8 = (f32[4,2,8,512]{3,2,1,0:T(8,128)S(1)}, f32[4,2,8,512]{3,2,1,0:T(8,128)S(1)}, u32[]{:S(2)}, u32[]{:S(2)}) collective-permute-start(f32[4,2,8,512]{3,2,1,0:T(8,128)S(1)} %get-tuple-element.32), channel_id=1, source_target_pairs={{0,128},{128,256},{256,384},{1,129},{129,257},{257,385},{2,130},{1... | collective-permute-start | bytes 393224 | tf_op jit(solution)/shard_map/ppermute | solution.py:20
  105.1 11.0 %collective-permute-start.9 = (f32[4,2,8,512]{3,2,1,0:T(8,128)S(1)}, f32[4,2,8,512]{3,2,1,0:T(8,128)S(1)}, u32[]{:S(2)}, u32[]{:S(2)}) collective-permute-start(f32[4,2,8,512]{3,2,1,0:T(8,128)S(1)} %get-tuple-element.33), channel_id=1, source_target_pairs={{128,0},{256,128},{384,256},{129,1},{257,129},{385,257},{130,2},{2... | collective-permute-start | bytes 393224 | tf_op jit(solution)/shard_map/ppermute | solution.py:21
  121.3 32.7 %collective-permute-start.14 = (f32[4,16,2,512]{3,2,1,0:T(2,128)}, f32[4,16,2,512]{3,2,1,0:T(2,128)S(1)}, u32[]{:S(2)}, u32[]{:S(2)}) collective-permute-start(f32[4,16,2,512]{3,2,1,0:T(2,128)} %get-tuple-element.26), channel_id=1, source_target_pairs={{0,1},{1,2},{2,3},{3,4},{4,5},{5,6},{6,7},{7,8},{8,9},{9,10},{10,1... | collective-permute-start | bytes 786440 | tf_op jit(solution)/shard_map/ppermute | solution.py:20
  129.4 24.6 %collective-permute-start.15 = (f32[4,16,2,512]{3,2,1,0:T(2,128)S(1)}, f32[4,16,2,512]{3,2,1,0:T(2,128)S(1)}, u32[]{:S(2)}, u32[]{:S(2)}) collective-permute-start(f32[4,16,2,512]{3,2,1,0:T(2,128)S(1)} %get-tuple-element.27), channel_id=1, source_target_pairs={{1,0},{2,1},{3,2},{4,3},{5,4},{6,5},{7,6},{8,7},{9,8},{10,9},{11,1... | collective-permute-start | bytes 786440 | tf_op jit(solution)/shard_map/ppermute | solution.py:21
  130.7 27.0 %all-to-all-start.1 = ((f32[4,16,8,512]{3,2,0,1:T(8,128)}), f32[4,16,8,512]{3,2,0,1:T(8,128)S(1)}, u32[]{:S(2)}, u32[]{:S(2)}) async-start(f32[4,16,8,512]{3,2,0,1:T(8,128)} %copy.80), calls=%async_computation.1 | async-start | bytes 2097152 | tf_op jit(solution)/shard_map/all_to_all | solution.py:76
  137.0 9.0 %collective-permute-start.12 = (f32[4,2,8,512]{3,2,1,0:T(8,128)}, f32[4,2,8,512]{3,2,1,0:T(8,128)S(1)}, u32[]{:S(2)}, u32[]{:S(2)}) collective-permute-start(f32[4,2,8,512]{3,2,1,0:T(8,128)} %get-tuple-element.28), channel_id=1, source_target_pairs={{0,128},{128,256},{256,384},{1,129},{129,257},{257,385},{2,130},{1... | collective-permute-start | bytes 393224 | tf_op jit(solution)/shard_map/ppermute | solution.py:20
  142.6 11.4 %collective-permute-start.13 = (f32[4,2,8,512]{3,2,1,0:T(8,128)}, f32[4,2,8,512]{3,2,1,0:T(8,128)}, u32[]{:S(2)}, u32[]{:S(2)}) collective-permute-start(f32[4,2,8,512]{3,2,1,0:T(8,128)} %get-tuple-element.29), channel_id=1, source_target_pairs={{128,0},{256,128},{384,256},{129,1},{257,129},{385,257},{130,2},{2... | collective-permute-start | bytes 393224 | tf_op jit(solution)/shard_map/ppermute | solution.py:21
  157.7 18.7 %all-to-all-start.2 = ((f32[4,16,8,512]{3,2,0,1:T(8,128)}), f32[4,16,8,512]{3,2,0,1:T(8,128)S(1)}, u32[]{:S(2)}, u32[]{:S(2)}) async-start(f32[4,16,8,512]{3,2,0,1:T(8,128)} %copy.82), calls=%async_computation.2 | async-start | bytes 2097152 | tf_op jit(solution)/shard_map/all_to_all | solution.py:77
  176.4 2.4 copy-start.12
  176.4 2.4 copy-start.13
  279.5 11.9 %all-to-all-start.7 = ((f32[16,1,2048]{2,1,0:T(1,128)}), f32[16,1,2048]{2,1,0:T(1,128)S(1)}, u32[]{:S(2)}, u32[]{:S(2)}) async-start(f32[16,1,2048]{2,1,0:T(1,128)} %reshape.1357), calls=%async_computation.7 | async-start | bytes 262144 | tf_op jit(solution)/shard_map/all_to_all | solution.py:32
  (10 other events, 21.0 us)

commit v11 on v10

--- a/solution.py
+++ b/solution.py
@@ -77,12 +77,15 @@
     applied = lax.all_to_all(spread_applied, "xl", 1, 0, tiled=True)
     count = orbitals.shape[0]
     cells = orbitals.shape[1] * orbitals.shape[2] * orbitals.shape[3]
-    stacked = jnp.concatenate([filtered, applied], axis=0)
     sign_block = (2 * sign_bits - 1).astype(jnp.float32)
-    flat = (stacked * sign_block[None]).reshape(2 * count, -1, 128)
-    mixed = jnp.einsum("nac,cd->adn", flat, hadamard_table(128), precision=HIGHEST)
-    mixed = jnp.einsum("ba,adn->bdn", hadamard_table(cells // 128), mixed, precision=HIGHEST)
-    mixed = mixed.reshape(cells, 2 * count)
+
+    def transform(field):
+        flat = (field * sign_block[None]).reshape(count, -1, 128)
+        mixed = jnp.einsum("nac,cd->adn", flat, hadamard_table(128), precision=HIGHEST)
+        mixed = jnp.einsum("ba,adn->bdn", hadamard_table(cells // 128), mixed, precision=HIGHEST)
+        return mixed.reshape(cells, count)
+
+    mixed = jnp.concatenate([transform(filtered), transform(applied)], axis=1)
     zh, xl, gy = (lax.axis_size(axis) for axis in BLOCK_AXES)
     order = sampled_rows[0, 0, :M].reshape(zh, xl, gy, -1).transpose(1, 0, 2, 3).reshape(-1)
     devices = zh * xl * gy

time: 306 us -> 309 us (level)
    concatenate x0 -> x1, other arithmetic: none -> 6.57 us  [shards(): mixed = jnp.concatenate([transform(filtered), transform(applied)], axis=1)]
    all_to_all x1, waiting for transfers between devices: 13.7 us -> 8.75 us  [shards(): applied = lax.all_to_all(spread_applied, 'xl', 1, 0, tiled=True)]
    select_n x7, other arithmetic: 3.44 us -> 0.03 us  [hadamard_table(): index[:, None] // weight % 2 * (index[None, :] // weight % 2)]
    ppermute x8, waiting for transfers between devices: 1.9 us -> 5.29 us  [halos(): before = lax.ppermute(last, axis, up)]
  transfers between devices with their start and end apart: 20 -> 20, of which waited for: 11 -> 12; matrix products, arithmetic and copies ran while one was open for 4% -> 3% of each run, Pallas kernels for 0% -> 0%
where the time goes in v11:
time: 309 us; the launch traced here: 306 us
  starting transfers between devices  88.5 us (29%)
  waiting for transfers between devices  73.7 us (24%)
  blocking collectives  72.2 us (23%)
  local copies, waits for them, and re-layouts  32.6 us (11%)
  other arithmetic  31 us (10%)
  matrix products  7.09 us (2%)
    ppermute x8, starting transfers between devices, halos(): before = lax.ppermute(last, axis, up)  54.5 us
    ppermute x8, waiting for transfers between devices, halos(): after = lax.ppermute(initial, axis, down)  37 us
    all_to_all x1, blocking collectives, shards(): y = lax.all_to_all(y, 'gy', 0, 0, tiled=True).sum(0)  27.8 us
    all_to_all x2, blocking collectives, exchange_sum(): x = lax.all_to_all(copies, axis, 0, 0, tiled=True).sum(0)  25.9 us
    all_to_all x1, blocking collectives, shards(): lax.all_to_all(picked.reshape(xl, -1, 2 * count), 'xl', 0, 0, tiled=True)  18.5 us
    all_to_all x1, waiting for transfers between devices, shards(): both = lax.all_to_all(both, 'xl', 0, 1, tiled=True)  16.1 us
    gather x2, local copies, waits for them, and re-layouts, shards(): picked = jnp.take(mixed, order, axis=0) / jnp.sqrt(jnp.float32(M * devices))  14.5 us
    ppermute x8, starting transfers between devices, halos(): after = lax.ppermute(initial, axis, down)  10.3 us
  transfers between devices with their start and end apart: 20, of which 12 were waited for; matrix products, arithmetic and copies ran while one was open for 3% of the time, Pallas kernels for 0%

profile of v11, /device:TPU:6, one launch (start us, length us, event | category | flops | bytes accessed | tf_op | source)
XLA Modules:
  0.0 306.3 jit_solution(13314530203494539142)
XLA Ops:
  3.9 9.5 %all-to-all-start = ((f32[40,2,8,512]{3,2,1,0:T(8,128)}), f32[40,2,8,512]{3,2,1,0:T(8,128)S(1)}, u32[]{:S(2)}, u32[]{:S(2)}) async-start(f32[40,2,8,512]{3,2,1,0:T(8,128)} %bitcast.4), calls=%async_computation | async-start | bytes 2621440 | tf_op jit(solution)/shard_map/all_to_all | solution.py:68
  14.0 16.1 %all-to-all-done = f32[40,2,8,512]{3,2,1,0:T(8,128)S(1)} async-done(((f32[40,2,8,512]{3,2,1,0:T(8,128)}), f32[40,2,8,512]{3,2,1,0:T(8,128)S(1)}, u32[]{:S(2)}, u32[]{:S(2)}) %all-to-all-start) | async-done | bytes 1310752 | tf_op jit(solution)/shard_map/all_to_all | solution.py:68
  33.1 7.1 %collective-permute-start = (f32[4,2,8,512]{3,2,1,0:T(8,128)S(1)}, f32[4,2,8,512]{3,2,1,0:T(8,128)S(1)}, u32[]{:S(2)}, u32[]{:S(2)}) collective-permute-start(f32[4,2,8,512]{3,2,1,0:T(8,128)S(1)} %get-tuple-element.38), channel_id=1, source_target_pairs={{0,128},{128,256},{256,384},{1,129},{129,257},{257,385},{2,130},{1... | collective-permute-start | bytes 393224 | tf_op jit(solution)/shard_map/ppermute | solution.py:20
  42.6 11.4 %collective-permute-done.1 = f32[4,2,8,512]{3,2,1,0:T(8,128)S(1)} collective-permute-done((f32[4,2,8,512]{3,2,1,0:T(8,128)S(1)}, f32[4,2,8,512]{3,2,1,0:T(8,128)S(1)}, u32[]{:S(2)}, u32[]{:S(2)}) %collective-permute-start.1) | collective-permute-done | bytes 131104 | tf_op jit(solution)/shard_map/ppermute | solution.py:21
  56.6 10.5 %collective-permute-start.6 = (f32[4,16,2,512]{3,2,1,0:T(2,128)S(1)}, f32[4,16,2,512]{3,2,1,0:T(2,128)S(1)}, u32[]{:S(2)}, u32[]{:S(2)}) collective-permute-start(f32[4,16,2,512]{3,2,1,0:T(2,128)S(1)} %get-tuple-element.34), channel_id=1, source_target_pairs={{0,1},{1,2},{2,3},{3,4},{4,5},{5,6},{6,7},{7,8},{8,9},{9,10},{10,1... | collective-permute-start | bytes 786440 | tf_op jit(solution)/shard_map/ppermute | solution.py:20
  68.4 7.7 %collective-permute-start.4 = (f32[4,2,8,512]{3,2,1,0:T(8,128)S(1)}, f32[4,2,8,512]{3,2,1,0:T(8,128)S(1)}, u32[]{:S(2)}, u32[]{:S(2)}) collective-permute-start(f32[4,2,8,512]{3,2,1,0:T(8,128)S(1)} %get-tuple-element.36), channel_id=1, source_target_pairs={{0,128},{128,256},{256,384},{1,129},{129,257},{257,385},{2,130},{1... | collective-permute-start | bytes 393224 | tf_op jit(solution)/shard_map/ppermute | solution.py:20
  78.7 8.3 %collective-permute-done.5 = f32[4,2,8,512]{3,2,1,0:T(8,128)S(1)} collective-permute-done((f32[4,2,8,512]{3,2,1,0:T(8,128)S(1)}, f32[4,2,8,512]{3,2,1,0:T(8,128)S(1)}, u32[]{:S(2)}, u32[]{:S(2)}) %collective-permute-start.5) | collective-permute-done | bytes 131104 | tf_op jit(solution)/shard_map/ppermute | solution.py:21
  89.5 11.6 %collective-permute-start.10 = (f32[4,16,2,512]{3,2,1,0:T(2,128)S(1)}, f32[4,16,2,512]{3,2,1,0:T(2,128)S(1)}, u32[]{:S(2)}, u32[]{:S(2)}) collective-permute-start(f32[4,16,2,512]{3,2,1,0:T(2,128)S(1)} %get-tuple-element.30), channel_id=1, source_target_pairs={{0,1},{1,2},{2,3},{3,4},{4,5},{5,6},{6,7},{7,8},{8,9},{9,10},{10,1... | collective-permute-start | bytes 786440 | tf_op jit(solution)/shard_map/ppermute | solution.py:20
  107.7 8.5 %collective-permute-done.9 = f32[4,2,8,512]{3,2,1,0:T(8,128)S(1)} collective-permute-done((f32[4,2,8,512]{3,2,1,0:T(8,128)S(1)}, f32[4,2,8,512]{3,2,1,0:T(8,128)S(1)}, u32[]{:S(2)}, u32[]{:S(2)}) %collective-permute-start.9) | collective-permute-done | bytes 131104 | tf_op jit(solution)/shard_map/ppermute | solution.py:21
  120.6 8.1 %collective-permute-start.14 = (f32[4,16,2,512]{3,2,1,0:T(2,128)S(1)}, f32[4,16,2,512]{3,2,1,0:T(2,128)S(1)}, u32[]{:S(2)}, u32[]{:S(2)}) collective-permute-start(f32[4,16,2,512]{3,2,1,0:T(2,128)S(1)} %get-tuple-element.26), channel_id=1, source_target_pairs={{0,1},{1,2},{2,3},{3,4},{4,5},{5,6},{6,7},{7,8},{8,9},{9,10},{10,1... | collective-permute-start | bytes 786440 | tf_op jit(solution)/shard_map/ppermute | solution.py:20
  130.0 5.6 %all-to-all-start.1 = ((f32[4,16,8,512]{3,2,0,1:T(8,128)}), f32[4,16,8,512]{3,2,0,1:T(8,128)S(1)}, u32[]{:S(2)}, u32[]{:S(2)}) async-start(f32[4,16,8,512]{3,2,0,1:T(8,128)} %copy.86), calls=%async_computation.1 | async-start | bytes 2097152 | tf_op jit(solution)/shard_map/all_to_all | solution.py:76
  135.6 5.6 %collective-permute-start.12 = (f32[4,2,8,512]{3,2,1,0:T(8,128)S(1)}, f32[4,2,8,512]{3,2,1,0:T(8,128)S(1)}, u32[]{:S(2)}, u32[]{:S(2)}) collective-permute-start(f32[4,2,8,512]{3,2,1,0:T(8,128)S(1)} %get-tuple-element.28), channel_id=1, source_target_pairs={{0,128},{128,256},{256,384},{1,129},{129,257},{257,385},{2,130},{1... | collective-permute-start | bytes 393224 | tf_op jit(solution)/shard_map/ppermute | solution.py:20
  144.3 8.0 %collective-permute-done.13 = f32[4,2,8,512]{3,2,1,0:T(8,128)S(1)} collective-permute-done((f32[4,2,8,512]{3,2,1,0:T(8,128)S(1)}, f32[4,2,8,512]{3,2,1,0:T(8,128)S(1)}, u32[]{:S(2)}, u32[]{:S(2)}) %collective-permute-start.13) | collective-permute-done | bytes 131104 | tf_op jit(solution)/shard_map/ppermute | solution.py:21
  155.7 4.8 %all-to-all-start.2 = ((f32[4,16,8,512]{3,2,0,1:T(8,128)}), f32[4,16,8,512]{3,2,0,1:T(8,128)S(1)}, u32[]{:S(2)}, u32[]{:S(2)}) async-start(f32[4,16,8,512]{3,2,0,1:T(8,128)} %copy.88), calls=%async_computation.2 | async-start | bytes 2097152 | tf_op jit(solution)/shard_map/all_to_all | solution.py:77
  165.6 8.8 %all-to-all-done.2 = f32[4,16,8,512]{3,2,0,1:T(8,128)S(1)} async-done(((f32[4,16,8,512]{3,2,0,1:T(8,128)}), f32[4,16,8,512]{3,2,0,1:T(8,128)S(1)}, u32[]{:S(2)}, u32[]{:S(2)}) %all-to-all-start.2) | async-done | bytes 1048608 | tf_op jit(solution)/shard_map/all_to_all | solution.py:77
  181.7 6.6 %pad_maximum_fusion = f32[8192,64]{1,0:T(8,128)} fusion(f32[8192,32]{1,0:T(8,128)} %bitcast.93, f32[8192,32]{1,0:T(8,128)} %bitcast.92), kind=kLoop, calls=%fused_computation.1 | loop fusion | flops 524288 | bytes 4194304 | tf_op jit(solution)/shard_map/concatenate | solution.py:88
  188.3 13.0 %gather_fusion = f32[4096,64]{1,0:T(8,128)S(1)} fusion(f32[8192,64]{1,0:T(8,128)} %pad_maximum_fusion, s32[4096]{0:T(1024)S(1)} %broadcast_clamp_fusion), kind=kCustom, calls=%fused_computation | custom fusion | bytes 2113536 | tf_op jit(solution)/shard_map/jit(_take)/gather | solution.py:92
  204.2 18.5 %all_to_all.76 = f32[8,512,64]{1,2,0:T(8,128)S(1)} all-to-all(f32[8,512,64]{1,2,0:T(8,128)S(1)} %select_multiply_fusion), channel_id=1, replica_groups=mesh['zh'=4,'xl'=8,'gy'=16] {'xl'}, dimensions={0} | all-to-all | bytes 2097152 | tf_op jit(solution)/shard_map/all_to_all | solution.py:93
  223.1 27.8 %all_to_all.77 = f32[16,1,2048]{2,1,0:T(1,128)S(1)} all-to-all(f32[16,1,2048]{2,1,0:T(1,128)S(1)} %reshape.1355), channel_id=1, replica_groups=mesh['zh'=4,'xl'=8,'gy'=16] {'gy'}, dimensions={0} | all-to-all | bytes 262144 | tf_op jit(solution)/shard_map/all_to_all | solution.py:95
  252.7 17.9 %all_to_all.78 = f32[4,1,2048]{2,1,0:T(1,128)S(1)} all-to-all(f32[4,1,2048]{2,1,0:T(1,128)S(1)} %reshape.1357), channel_id=1, replica_groups=mesh['zh'=4,'xl'=8,'gy'=16] {'zh'}, dimensions={0} | all-to-all | bytes 65536 | tf_op jit(solution)/shard_map/all_to_all | solution.py:32
  272.1 8.0 %all_to_all.79 = f32[8,1,2048]{2,1,0:T(1,128)S(1)} all-to-all(f32[8,1,2048]{2,1,0:T(1,128)S(1)} %reshape.1359), channel_id=1, replica_groups=mesh['zh'=4,'xl'=8,'gy'=16] {'xl'}, dimensions={0} | all-to-all | bytes 131072 | tf_op jit(solution)/shard_map/all_to_all | solution.py:32
  282.0 3.7 %all-to-all-start.7 = ((f32[16,1,2048]{2,1,0:T(1,128)}), f32[16,1,2048]{2,1,0:T(1,128)S(1)}, u32[]{:S(2)}, u32[]{:S(2)}) async-start(f32[16,1,2048]{2,1,0:T(1,128)} %reshape.1361), calls=%async_computation.7 | async-start | bytes 262144 | tf_op jit(solution)/shard_map/all_to_all | solution.py:32
  287.3 6.6 %all-to-all-done.7 = f32[16,1,2048]{2,1,0:T(1,128)S(1)} async-done(((f32[16,1,2048]{2,1,0:T(1,128)}), f32[16,1,2048]{2,1,0:T(1,128)S(1)}, u32[]{:S(2)}, u32[]{:S(2)}) %all-to-all-start.7) | async-done | bytes 131104 | tf_op jit(solution)/shard_map/all_to_all | solution.py:32
  295.2 2.9 cholesky.17
  (123 shorter events, 68.6 us)
Async XLA Ops:
  1.4 12.0 %copy-start.1 = (s32[1,1,8192]{2,1,0:T(1,128)S(1)}, s32[1,1,8192]{2,1,0:T(1,128)}, u32[]{:S(2)}) copy-start(s32[1,1,8192]{2,1,0:T(1,128)} %param.7) | copy-start | bytes 98308
  3.9 10.1 %copy-start = (s32[2,8,512]{2,1,0:T(8,128)S(1)}, s32[2,8,512]{2,1,0:T(8,128)}, u32[]{:S(2)}) copy-start(s32[2,8,512]{2,1,0:T(8,128)} %param.6) | copy-start | bytes 98308
  3.9 26.2 %all-to-all-start = ((f32[40,2,8,512]{3,2,1,0:T(8,128)}), f32[40,2,8,512]{3,2,1,0:T(8,128)S(1)}, u32[]{:S(2)}, u32[]{:S(2)}) async-start(f32[40,2,8,512]{3,2,1,0:T(8,128)} %bitcast.4), calls=%async_computation | async-start | bytes 2621440 | tf_op jit(solution)/shard_map/all_to_all | solution.py:68
  30.4 23.6 %collective-permute-start.2 = (f32[4,16,2,512]{3,2,1,0:T(2,128)S(1)}, f32[4,16,2,512]{3,2,1,0:T(2,128)S(1)}, u32[]{:S(2)}, u32[]{:S(2)}) collective-permute-start(f32[4,16,2,512]{3,2,1,0:T(2,128)S(1)} %get-tuple-element.40), channel_id=1, source_target_pairs={{0,1},{1,2},{2,3},{3,4},{4,5},{5,6},{6,7},{7,8},{8,9},{9,10},{10,1... | collective-permute-start | bytes 786440 | tf_op jit(solution)/shard_map/ppermute | solution.py:20
  31.8 22.3 %collective-permute-start.3 = (f32[4,16,2,512]{3,2,1,0:T(2,128)S(1)}, f32[4,16,2,512]{3,2,1,0:T(2,128)S(1)}, u32[]{:S(2)}, u32[]{:S(2)}) collective-permute-start(f32[4,16,2,512]{3,2,1,0:T(2,128)S(1)} %get-tuple-element.41), channel_id=1, source_target_pairs={{1,0},{2,1},{3,2},{4,3},{5,4},{6,5},{7,6},{8,7},{9,8},{10,9},{11,1... | collective-permute-start | bytes 786440 | tf_op jit(solution)/shard_map/ppermute | solution.py:21
  33.1 9.6 %collective-permute-start = (f32[4,2,8,512]{3,2,1,0:T(8,128)S(1)}, f32[4,2,8,512]{3,2,1,0:T(8,128)S(1)}, u32[]{:S(2)}, u32[]{:S(2)}) collective-permute-start(f32[4,2,8,512]{3,2,1,0:T(8,128)S(1)} %get-tuple-element.38), channel_id=1, source_target_pairs={{0,128},{128,256},{256,384},{1,129},{129,257},{257,385},{2,130},{1... | collective-permute-start | bytes 393224 | tf_op jit(solution)/shard_map/ppermute | solution.py:20
  40.1 13.9 %collective-permute-start.1 = (f32[4,2,8,512]{3,2,1,0:T(8,128)S(1)}, f32[4,2,8,512]{3,2,1,0:T(8,128)S(1)}, u32[]{:S(2)}, u32[]{:S(2)}) collective-permute-start(f32[4,2,8,512]{3,2,1,0:T(8,128)S(1)} %get-tuple-element.39), channel_id=1, source_target_pairs={{128,0},{256,128},{384,256},{129,1},{257,129},{385,257},{130,2},{2... | collective-permute-start | bytes 393224 | tf_op jit(solution)/shard_map/ppermute | solution.py:21
  56.6 30.3 %collective-permute-start.6 = (f32[4,16,2,512]{3,2,1,0:T(2,128)S(1)}, f32[4,16,2,512]{3,2,1,0:T(2,128)S(1)}, u32[]{:S(2)}, u32[]{:S(2)}) collective-permute-start(f32[4,16,2,512]{3,2,1,0:T(2,128)S(1)} %get-tuple-element.34), channel_id=1, source_target_pairs={{0,1},{1,2},{2,3},{3,4},{4,5},{5,6},{6,7},{7,8},{8,9},{9,10},{10,1... | collective-permute-start | bytes 786440 | tf_op jit(solution)/shard_map/ppermute | solution.py:20
  67.1 19.8 %collective-permute-start.7 = (f32[4,16,2,512]{3,2,1,0:T(2,128)S(1)}, f32[4,16,2,512]{3,2,1,0:T(2,128)S(1)}, u32[]{:S(2)}, u32[]{:S(2)}) collective-permute-start(f32[4,16,2,512]{3,2,1,0:T(2,128)S(1)} %get-tuple-element.35), channel_id=1, source_target_pairs={{1,0},{2,1},{3,2},{4,3},{5,4},{6,5},{7,6},{8,7},{9,8},{10,9},{11,1... | collective-permute-start | bytes 786440 | tf_op jit(solution)/shard_map/ppermute | solution.py:21
  68.4 10.2 %collective-permute-start.4 = (f32[4,2,8,512]{3,2,1,0:T(8,128)S(1)}, f32[4,2,8,512]{3,2,1,0:T(8,128)S(1)}, u32[]{:S(2)}, u32[]{:S(2)}) collective-permute-start(f32[4,2,8,512]{3,2,1,0:T(8,128)S(1)} %get-tuple-element.36), channel_id=1, source_target_pairs={{0,128},{128,256},{256,384},{1,129},{129,257},{257,385},{2,130},{1... | collective-permute-start | bytes 393224 | tf_op jit(solution)/shard_map/ppermute | solution.py:20
  76.2 10.8 %collective-permute-start.5 = (f32[4,2,8,512]{3,2,1,0:T(8,128)S(1)}, f32[4,2,8,512]{3,2,1,0:T(8,128)S(1)}, u32[]{:S(2)}, u32[]{:S(2)}) collective-permute-start(f32[4,2,8,512]{3,2,1,0:T(8,128)S(1)} %get-tuple-element.37), channel_id=1, source_target_pairs={{128,0},{256,128},{384,256},{129,1},{257,129},{385,257},{130,2},{2... | collective-permute-start | bytes 393224 | tf_op jit(solution)/shard_map/ppermute | solution.py:21
  89.5 26.6 %collective-permute-start.10 = (f32[4,16,2,512]{3,2,1,0:T(2,128)S(1)}, f32[4,16,2,512]{3,2,1,0:T(2,128)S(1)}, u32[]{:S(2)}, u32[]{:S(2)}) collective-permute-start(f32[4,16,2,512]{3,2,1,0:T(2,128)S(1)} %get-tuple-element.30), channel_id=1, source_target_pairs={{0,1},{1,2},{2,3},{3,4},{4,5},{5,6},{6,7},{7,8},{8,9},{9,10},{10,1... | collective-permute-start | bytes 786440 | tf_op jit(solution)/shard_map/ppermute | solution.py:20
  101.1 15.8 %collective-permute-start.11 = (f32[4,16,2,512]{3,2,1,0:T(2,128)S(1)}, f32[4,16,2,512]{3,2,1,0:T(2,128)S(1)}, u32[]{:S(2)}, u32[]{:S(2)}) collective-permute-start(f32[4,16,2,512]{3,2,1,0:T(2,128)S(1)} %get-tuple-element.31), channel_id=1, source_target_pairs={{1,0},{2,1},{3,2},{4,3},{5,4},{6,5},{7,6},{8,7},{9,8},{10,9},{11,1... | collective-permute-start | bytes 786440 | tf_op jit(solution)/shard_map/ppermute | solution.py:21
  102.4 5.2 %collective-permute-start.8 = (f32[4,2,8,512]{3,2,1,0:T(8,128)S(1)}, f32[4,2,8,512]{3,2,1,0:T(8,128)S(1)}, u32[]{:S(2)}, u32[]{:S(2)}) collective-permute-start(f32[4,2,8,512]{3,2,1,0:T(8,128)S(1)} %get-tuple-element.32), channel_id=1, source_target_pairs={{0,128},{128,256},{256,384},{1,129},{129,257},{257,385},{2,130},{1... | collective-permute-start | bytes 393224 | tf_op jit(solution)/shard_map/ppermute | solution.py:20
  105.1 11.0 %collective-permute-start.9 = (f32[4,2,8,512]{3,2,1,0:T(8,128)S(1)}, f32[4,2,8,512]{3,2,1,0:T(8,128)S(1)}, u32[]{:S(2)}, u32[]{:S(2)}) collective-permute-start(f32[4,2,8,512]{3,2,1,0:T(8,128)S(1)} %get-tuple-element.33), channel_id=1, source_target_pairs={{128,0},{256,128},{384,256},{129,1},{257,129},{385,257},{130,2},{2... | collective-permute-start | bytes 393224 | tf_op jit(solution)/shard_map/ppermute | solution.py:21
  120.6 31.7 %collective-permute-start.14 = (f32[4,16,2,512]{3,2,1,0:T(2,128)S(1)}, f32[4,16,2,512]{3,2,1,0:T(2,128)S(1)}, u32[]{:S(2)}, u32[]{:S(2)}) collective-permute-start(f32[4,16,2,512]{3,2,1,0:T(2,128)S(1)} %get-tuple-element.26), channel_id=1, source_target_pairs={{0,1},{1,2},{2,3},{3,4},{4,5},{5,6},{6,7},{7,8},{8,9},{9,10},{10,1... | collective-permute-start | bytes 786440 | tf_op jit(solution)/shard_map/ppermute | solution.py:20
  128.7 23.6 %collective-permute-start.15 = (f32[4,16,2,512]{3,2,1,0:T(2,128)S(1)}, f32[4,16,2,512]{3,2,1,0:T(2,128)S(1)}, u32[]{:S(2)}, u32[]{:S(2)}) collective-permute-start(f32[4,16,2,512]{3,2,1,0:T(2,128)S(1)} %get-tuple-element.27), channel_id=1, source_target_pairs={{1,0},{2,1},{3,2},{4,3},{5,4},{6,5},{7,6},{8,7},{9,8},{10,9},{11,1... | collective-permute-start | bytes 786440 | tf_op jit(solution)/shard_map/ppermute | solution.py:21
  130.0 25.6 %all-to-all-start.1 = ((f32[4,16,8,512]{3,2,0,1:T(8,128)}), f32[4,16,8,512]{3,2,0,1:T(8,128)S(1)}, u32[]{:S(2)}, u32[]{:S(2)}) async-start(f32[4,16,8,512]{3,2,0,1:T(8,128)} %copy.86), calls=%async_computation.1 | async-start | bytes 2097152 | tf_op jit(solution)/shard_map/all_to_all | solution.py:76
  135.6 8.7 %collective-permute-start.12 = (f32[4,2,8,512]{3,2,1,0:T(8,128)S(1)}, f32[4,2,8,512]{3,2,1,0:T(8,128)S(1)}, u32[]{:S(2)}, u32[]{:S(2)}) collective-permute-start(f32[4,2,8,512]{3,2,1,0:T(8,128)S(1)} %get-tuple-element.28), channel_id=1, source_target_pairs={{0,128},{128,256},{256,384},{1,129},{129,257},{257,385},{2,130},{1... | collective-permute-start | bytes 393224 | tf_op jit(solution)/shard_map/ppermute | solution.py:20
  141.3 11.1 %collective-permute-start.13 = (f32[4,2,8,512]{3,2,1,0:T(8,128)S(1)}, f32[4,2,8,512]{3,2,1,0:T(8,128)S(1)}, u32[]{:S(2)}, u32[]{:S(2)}) collective-permute-start(f32[4,2,8,512]{3,2,1,0:T(8,128)S(1)} %get-tuple-element.29), channel_id=1, source_target_pairs={{128,0},{256,128},{384,256},{129,1},{257,129},{385,257},{130,2},{2... | collective-permute-start | bytes 393224 | tf_op jit(solution)/shard_map/ppermute | solution.py:21
  155.7 18.7 %all-to-all-start.2 = ((f32[4,16,8,512]{3,2,0,1:T(8,128)}), f32[4,16,8,512]{3,2,0,1:T(8,128)S(1)}, u32[]{:S(2)}, u32[]{:S(2)}) async-start(f32[4,16,8,512]{3,2,0,1:T(8,128)} %copy.88), calls=%async_computation.2 | async-start | bytes 2097152 | tf_op jit(solution)/shard_map/all_to_all | solution.py:77
  282.0 11.9 %all-to-all-start.7 = ((f32[16,1,2048]{2,1,0:T(1,128)}), f32[16,1,2048]{2,1,0:T(1,128)S(1)}, u32[]{:S(2)}, u32[]{:S(2)}) async-start(f32[16,1,2048]{2,1,0:T(1,128)} %reshape.1361), calls=%async_computation.7 | async-start | bytes 262144 | tf_op jit(solution)/shard_map/all_to_all | solution.py:32
